TPU v7x, 768 devices: a whole 4x8x12 slice. The times are simulated.
768 devices in a mesh: section: 64 (over z_lo, y, core), tp: 12 (over x, z_hi).
Axes of the slice: x: 4, y: 8, z: 12 (z_hi: 3, z_lo: 4; z = z_hi * 4 + z_lo), core: 2. Of those that a mesh axis runs over, the one named last changes fastest.
Arguments:
- saved_inputs: bfloat16 [2, 64, 1536, 4608], P(None, 'section', 'tp'), may hold values from -10.5 to 10.5
- incoming: bfloat16 [64, 1536, 4608], P('section', 'tp'), may hold values from -6 to 6
- qk_gain: float32 [64, 4608], P('section'), may hold values from -1 to 1
- value_gain: float32 [64, 4608], P('section'), may hold values from -1 to 1
Outputs:
- passed: bfloat16 [64, 1536, 4608], P('section', 'tp')
- qk_gain_grad: float32 [64, 4608], P('section', 'tp')
- value_gain_grad: float32 [64, 4608], P('section', 'tp')
All inputs are finite; a program needn't handle non-finite values.
Results may differ from a plain program's by a relative error of at most 0.0079.
Values may be sent and summed in bfloat16 or wider, within the bound.
No kernel may reach another device: no remote copies, remote signals or barrier semaphores. Data moves between devices by JAX's collectives and lax.ppermute only.
A program may use at most 64 MiB of HBM per device.

v0:
```python
import jax
import jax.numpy as jnp
from jax import lax
from jax.sharding import PartitionSpec as P

HEAD_DIM = 128
SEQ_LEN = 256


def from_behind(block, axis, distance):
    devices = range(lax.axis_size(axis))
    route = [((i - distance) % len(devices), i) for i in devices]
    return lax.ppermute(block, axis, route)


def attend_grads(queries, keys, values, upstream, allowed, scale):
    scores = (
        jnp.einsum("nqhe,nkhe->nhqk", queries, keys, preferred_element_type=jnp.float32) * scale
    )
    scores = jnp.where(allowed, scores, -jnp.inf)
    row_max = jnp.max(scores, axis=-1, keepdims=True)
    weights = jnp.exp(scores - row_max)
    probs = weights / jnp.sum(weights, axis=-1, keepdims=True)
    probs_low = probs.astype(jnp.bfloat16)
    prob_grad = jnp.einsum("nqhe,nkhe->nhqk", upstream, values, preferred_element_type=jnp.float32)
    score_grad = probs * (prob_grad - jnp.sum(probs * prob_grad, axis=-1, keepdims=True))
    score_low = score_grad.astype(jnp.bfloat16)
    query_grad = (
        jnp.einsum("nhqk,nkhe->nqhe", score_low, keys, preferred_element_type=jnp.float32) * scale
    )
    key_grad = (
        jnp.einsum("nhqk,nqhe->nkhe", score_low, queries, preferred_element_type=jnp.float32)
        * scale
    )
    value_grad = jnp.einsum(
        "nhqk,nqhe->nkhe", probs_low, upstream, preferred_element_type=jnp.float32
    )
    return (query_grad, key_grad, value_grad)


def pass_on(grad_in):
    return from_behind(grad_in, "section", -1)


def local_backward(inputs, upstream, gain_qk, gain_value):
    row_total = inputs.shape[0]
    local_width = inputs.shape[1]
    count = row_total // SEQ_LEN
    local_heads = local_width // HEAD_DIM
    wide = inputs.astype(jnp.float32)
    keys = (wide * gain_qk).astype(jnp.bfloat16)
    values = (wide * gain_value).astype(jnp.bfloat16)
    shape_four = (count, SEQ_LEN, local_heads, HEAD_DIM)
    allowed = jnp.tril(jnp.ones((SEQ_LEN, SEQ_LEN), dtype=bool))
    query_grad, key_grad, value_grad = attend_grads(
        keys.reshape(shape_four),
        keys.reshape(shape_four),
        values.reshape(shape_four),
        upstream.reshape(shape_four),
        allowed,
        HEAD_DIM ** (-0.5),
    )
    qk_total = (query_grad + key_grad).reshape(row_total, local_width)
    value_total = value_grad.reshape(row_total, local_width)
    grad_in = (upstream.astype(jnp.float32) + qk_total * gain_qk + value_total * gain_value).astype(
        jnp.bfloat16
    )
    return (grad_in, jnp.sum(wide * qk_total, axis=0), jnp.sum(wide * value_total, axis=0))


def heads_tick(inputs, upstream, gain_qk, gain_value):
    inputs_head, upstream_head = (
        lax.all_to_all(inputs, "tp", split_axis=1, concat_axis=0, tiled=True),
        lax.all_to_all(upstream, "tp", split_axis=1, concat_axis=0, tiled=True),
    )
    grad_in, qk_part, value_part = local_backward(inputs_head, upstream_head, gain_qk, gain_value)
    grad_tokens = lax.all_to_all(grad_in, "tp", split_axis=0, concat_axis=1, tiled=True)
    return (grad_tokens, qk_part, value_part)


def shards(saved_inputs, incoming, qk_gain, value_gain):
    upstream = incoming[0]
    tick_count = saved_inputs.shape[0]
    local_width = qk_gain.shape[1] // lax.axis_size("tp")
    offset = lax.axis_index("tp") * local_width
    gain_qk = lax.dynamic_slice_in_dim(qk_gain[0], offset, local_width)
    gain_value = lax.dynamic_slice_in_dim(value_gain[0], offset, local_width)
    qk_sum = jnp.zeros((local_width,), jnp.float32)
    value_sum = jnp.zeros((local_width,), jnp.float32)
    for tick_index in range(tick_count):
        grad_in, qk_part, value_part = heads_tick(
            saved_inputs[tick_index, 0], upstream, gain_qk, gain_value
        )
        qk_sum = qk_sum + qk_part
        value_sum = value_sum + value_part
        upstream = pass_on(grad_in)
    return (upstream[None], qk_sum[None], value_sum[None])


def solution(mesh):
    return jax.shard_map(
        shards,
        mesh=mesh,
        in_specs=(
            P(None, "section", "tp", None),
            P("section", "tp", None),
            P("section", None),
            P("section", None),
        ),
        out_specs=(P("section", "tp", None), P("section", "tp"), P("section", "tp")),
        check_vma=False,
    )
```

profile of v0, /device:TPU:57, one launch (start us, length us, event | category | flops | bytes accessed | tf_op | source)
XLA Modules:
  0.0 391.1 jit_solution(15409272666664470944)
XLA Ops:
  0.6 1.8 fusion.38
  3.8 16.1 %all-to-all-start.1 = ((bf16[128,12,384]{0,2,1:T(8,128)(2,1)}), bf16[128,12,384]{0,2,1:T(8,128)(2,1)S(1)}, u32[]{:S(2)}, u32[]{:S(2)}) async-start(bf16[128,12,384]{0,2,1:T(8,128)(2,1)} %bitcast.2), calls=%async_computation.1 | async-start | bytes 2359296 | tf_op jit(solution)/shard_map/all_to_all | solution.py:73
  21.4 37.5 %all-to-all-done.1 = bf16[128,12,384]{0,2,1:T(8,128)(2,1)S(1)} async-done(((bf16[128,12,384]{0,2,1:T(8,128)(2,1)}), bf16[128,12,384]{0,2,1:T(8,128)(2,1)S(1)}, u32[]{:S(2)}, u32[]{:S(2)}) %all-to-all-start.1) | async-done | bytes 1179680 | tf_op jit(solution)/shard_map/all_to_all | solution.py:73
  58.9 5.0 %all-to-all-start.4 = ((bf16[128,12,384]{0,2,1:T(8,128)(2,1)}), bf16[128,12,384]{0,2,1:T(8,128)(2,1)S(1)}, u32[]{:S(2)}, u32[]{:S(2)}) async-start(bf16[128,12,384]{0,2,1:T(8,128)(2,1)} %bitcast.11), calls=%async_computation.4 | async-start | bytes 2359296 | tf_op jit(solution)/shard_map/all_to_all | solution.py:73
  65.4 39.5 %all-to-all-done.4 = bf16[128,12,384]{0,2,1:T(8,128)(2,1)S(1)} async-done(((bf16[128,12,384]{0,2,1:T(8,128)(2,1)}), bf16[128,12,384]{0,2,1:T(8,128)(2,1)S(1)}, u32[]{:S(2)}, u32[]{:S(2)}) %all-to-all-start.4) | async-done | bytes 1179680 | tf_op jit(solution)/shard_map/all_to_all | solution.py:73
  104.9 7.0 %all-to-all-start = ((bf16[128,12,384]{0,2,1:T(8,128)(2,1)}), bf16[128,12,384]{0,2,1:T(8,128)(2,1)}, u32[]{:S(2)}, u32[]{:S(2)}) async-start(bf16[128,12,384]{0,2,1:T(8,128)(2,1)} %bitcast), calls=%async_computation | async-start | bytes 2359296 | tf_op jit(solution)/shard_map/all_to_all | solution.py:74
  113.5 2.0 copy.61
  115.5 4.6 %reshape.169 = f32[6,256,3,128]{3,2,1,0:T(4,128)} reshape(f32[12,128,384]{2,1,0:T(8,128)} %copy.61) | data formatting | bytes 4718592 | tf_op jit(solution)/shard_map/convert_element_type | solution.py:50
  120.4 2.0 copy.76
  122.3 3.5 reshape.170
  125.8 4.5 %copy.91 = f32[6,256,3,128]{1,3,2,0:T(8,128)} copy(f32[6,256,3,128]{3,2,1,0:T(4,128)} %reshape.169) | data formatting | bytes 4718592 | tf_op jit(solution)/shard_map/convert_element_type | solution.py:50
  130.3 4.1 %fusion.7 = (bf16[6,256,3,128]{3,1,2,0:T(8,128)(2,1)}, bf16[6,256,3,128]{3,1,2,0:T(8,128)(2,1)}) fusion(f32[6,256,3,128]{3,2,1,0:T(4,128)S(1)} %reshape.170, f32[3,128]{1,0:T(4,128)S(1)} %bitcast.75, f32[6,256,3,128]{3,2,1,0:T(4,128)} %reshape.169), kind=kLoop, calls=%fused_computation.18 | loop fusion | flops 2359296 | bytes 7079424 | tf_op jit(solution)/shard_map/convert_element_type | solution.py:51
  134.4 3.0 multiply_convert_fusion.1
  137.4 14.1 %all-to-all-done = bf16[128,12,384]{0,2,1:T(8,128)(2,1)} async-done(((bf16[128,12,384]{0,2,1:T(8,128)(2,1)}), bf16[128,12,384]{0,2,1:T(8,128)(2,1)}, u32[]{:S(2)}, u32[]{:S(2)}) %all-to-all-start) | async-done | bytes 1179680 | tf_op jit(solution)/shard_map/all_to_all | solution.py:74
  151.6 2.4 copy.63
  154.0 4.1 %reshape.163 = bf16[6,256,3,128]{3,2,1,0:T(4,128)(2,1)} reshape(bf16[12,128,384]{2,1,0:T(8,128)(2,1)} %copy.63) | data formatting | bytes 2359296 | tf_op jit(solution)/shard_map/reshape | solution.py:59
  158.1 5.3 %fusion.39 = (f32[6,3,256]{2,1,0:T(4,128)S(1)}, f32[6,3,256,256]{2,3,1,0:T(8,128)}) fusion(pred[256,256]{0,1:T(8,128)(4,1)S(1)} %copy-done.13, bf16[6,256,3,128]{3,1,2,0:T(8,128)(2,1)} %get-tuple-element.16), kind=kOutput, calls=%fused_computation.64 | convolution fusion | flops 306708736 | bytes 5982208 | tf_op jit(solution)/shard_map/sub | solution.py:22
  163.4 6.1 %multiply_reduce_fusion.2 = (f32[3,128]{1,0:T(4,128)S(1)}, f32[6,256,3,128]{3,1,2,0:T(8,128)}) fusion(f32[6,256,3,128]{3,2,1,0:T(4,128)} %reshape.169, bf16[6,256,3,128]{3,2,1,0:T(4,128)(2,1)} %reshape.163, f32[6,3,256,256]{2,3,1,0:T(8,128)} %get-tuple-element.18, f32[6,3,256]{2,1,0:T(4,128)S(1)} %get-tuple-element.17), kind=kOutput, calls=%fused_computation.24 | convolution fusion | flops 305528448 | bytes 10636800 | tf_op jit(solution)/shard_map/nhqk,nqhe->nkhe/dot_general | solution.py:35
  174.3 2.4 multiply_reduce_fusion.4
  176.7 4.5 %copy.70 = f32[6,256,3,128]{3,2,1,0:T(4,128)} copy(f32[6,256,3,128]{1,3,2,0:T(8,128)} %get-tuple-element.26) | data formatting | bytes 4718592 | tf_op jit(solution)/shard_map/add | solution.py:63
  181.2 4.9 %reshape.164 = f32[12,128,384]{2,1,0:T(8,128)} reshape(f32[6,256,3,128]{3,2,1,0:T(4,128)} %copy.70) | data formatting | bytes 4718592 | tf_op jit(solution)/shard_map/reshape | solution.py:63
  186.1 3.1 copy.71
  189.2 4.9 %copy.73 = f32[6,256,3,128]{3,2,1,0:T(4,128)} copy(f32[6,256,3,128]{3,1,2,0:T(8,128)} %get-tuple-element.29) | data formatting | bytes 4718592 | tf_op jit(solution)/shard_map/nhqk,nqhe->nkhe/transpose | solution.py:35
  194.1 4.9 %reshape.165 = f32[12,128,384]{2,1,0:T(8,128)} reshape(f32[6,256,3,128]{3,2,1,0:T(4,128)} %copy.73) | data formatting | bytes 4718592 | tf_op jit(solution)/shard_map/reshape | solution.py:64
  199.0 3.1 copy.74
  202.1 3.3 add_convert_fusion.1
  205.4 30.6 %all_to_all.90 = bf16[12,128,384]{1,2,0:T(8,128)(2,1)S(1)} all-to-all(bf16[12,128,384]{1,2,0:T(8,128)(2,1)S(1)} %add_convert_fusion.1), channel_id=1, replica_groups=mesh['section'=64,'tp'=12] {'tp'}, dimensions={0} | all-to-all | bytes 2359296 | tf_op jit(solution)/shard_map/all_to_all | solution.py:77
  236.0 2.4 collective-permute-start
  238.5 46.7 %collective-permute-done = bf16[128,4608]{0,1:T(8,128)(2,1)S(1)} collective-permute-done((bf16[128,4608]{0,1:T(8,128)(2,1)S(1)}, bf16[128,4608]{0,1:T(8,128)(2,1)S(1)}, u32[]{:S(2)}, u32[]{:S(2)}) %collective-permute-start) | collective-permute-done | bytes 1179680 | tf_op jit(solution)/shard_map/ppermute | solution.py:13
  286.2 4.4 %all-to-all-start.3 = ((bf16[128,12,384]{0,2,1:T(8,128)(2,1)}), bf16[128,12,384]{0,2,1:T(8,128)(2,1)}, u32[]{:S(2)}, u32[]{:S(2)}) async-start(bf16[128,12,384]{0,2,1:T(8,128)(2,1)} %bitcast.72), calls=%async_computation.3 | async-start | bytes 2359296 | tf_op jit(solution)/shard_map/all_to_all | solution.py:74
  290.6 2.5 copy.92
  293.0 5.3 %fusion.40 = (f32[6,3,256]{2,1,0:T(4,128)S(1)}, f32[6,3,256,256]{2,3,1,0:T(8,128)}) fusion(pred[256,256]{0,1:T(8,128)(4,1)S(1)} %copy-done.13, bf16[6,256,3,128]{3,1,2,0:T(8,128)(2,1)} %get-tuple-element.15), kind=kOutput, calls=%fused_computation.65 | convolution fusion | flops 306708736 | bytes 5982208 | tf_op jit(solution)/shard_map/sub | solution.py:22
  298.4 7.4 %all-to-all-done.3 = bf16[128,12,384]{0,2,1:T(8,128)(2,1)} async-done(((bf16[128,12,384]{0,2,1:T(8,128)(2,1)}), bf16[128,12,384]{0,2,1:T(8,128)(2,1)}, u32[]{:S(2)}, u32[]{:S(2)}) %all-to-all-start.3) | async-done | bytes 1179680 | tf_op jit(solution)/shard_map/all_to_all | solution.py:74
  305.8 1.7 copy.78
  307.9 2.0 copy.87
  309.9 3.7 multiply_reduce_fusion
  315.8 2.4 multiply_bitcast_fusion
  318.1 3.0 copy.85
  321.2 6.5 %multiply_reduce_fusion.1 = (f32[3,128]{1,0:T(4,128)S(1)}, f32[3,128]{1,0:T(4,128)S(1)}, f32[6,256,3,128]{1,3,2,0:T(8,128)}) fusion(f32[6,256,3,128]{1,3,2,0:T(8,128)} %copy.92, f32[6,256,3,128]{1,3,2,0:T(8,128)} %multiply_bitcast_fusion, bf16[6,256,3,128]{1,3,2,0:T(8,128)(2,1)} %copy.87, f32[6,3,256,256]{2,3,1,0:T(8,128)} %get-tuple-element.22, ...), kind=kOutput, calls=%fused_computation.23 | convolution fusion | flops 306707712 | bytes 12997632 | tf_op jit(solution)/shard_map/nhqk,nqhe->nkhe/dot_general | solution.py:35
  327.7 4.5 %copy.89 = f32[6,256,3,128]{3,2,1,0:T(4,128)} copy(f32[6,256,3,128]{1,3,2,0:T(8,128)} %get-tuple-element.27) | data formatting | bytes 4718592 | tf_op jit(solution)/shard_map/nhqk,nqhe->nkhe/transpose | solution.py:35
  332.2 4.9 %reshape.168 = f32[12,128,384]{2,1,0:T(8,128)} reshape(f32[6,256,3,128]{3,2,1,0:T(4,128)} %copy.89) | data formatting | bytes 4718592 | tf_op jit(solution)/shard_map/reshape | solution.py:64
  337.1 3.1 copy.90
  340.2 2.6 reshape.167
  342.8 3.2 copy.86
  346.0 2.6 add_convert_fusion
  348.6 21.5 %all_to_all.91 = bf16[12,128,384]{1,2,0:T(8,128)(2,1)S(1)} all-to-all(bf16[12,128,384]{1,2,0:T(8,128)(2,1)S(1)} %add_convert_fusion), channel_id=1, replica_groups=mesh['section'=64,'tp'=12] {'tp'}, dimensions={0} | all-to-all | bytes 2359296 | tf_op jit(solution)/shard_map/all_to_all | solution.py:77
  370.1 2.4 collective-permute-start.1
  373.7 16.0 %collective-permute-done.1 = bf16[128,4608]{0,1:T(8,128)(2,1)S(1)} collective-permute-done((bf16[128,4608]{0,1:T(8,128)(2,1)S(1)}, bf16[128,4608]{0,1:T(8,128)(2,1)S(1)}, u32[]{:S(2)}, u32[]{:S(2)}) %collective-permute-start.1) | collective-permute-done | bytes 1179680 | tf_op jit(solution)/shard_map/ppermute | solution.py:13
  (51 shorter events, 16.9 us)
Async XLA Ops:
  3.8 55.1 %all-to-all-start.1 = ((bf16[128,12,384]{0,2,1:T(8,128)(2,1)}), bf16[128,12,384]{0,2,1:T(8,128)(2,1)S(1)}, u32[]{:S(2)}, u32[]{:S(2)}) async-start(bf16[128,12,384]{0,2,1:T(8,128)(2,1)} %bitcast.2), calls=%async_computation.1 | async-start | bytes 2359296 | tf_op jit(solution)/shard_map/all_to_all | solution.py:73
  20.0 44.0 %copy-start.11 = (bf16[1,128,4608]{2,1,0:T(8,128)(2,1)S(1)}, bf16[1,128,4608]{2,1,0:T(8,128)(2,1)}, u32[]{:S(2)}) copy-start(bf16[1,128,4608]{2,1,0:T(8,128)(2,1)} %param.5) | copy-start | bytes 3538948
  58.9 46.0 %all-to-all-start.4 = ((bf16[128,12,384]{0,2,1:T(8,128)(2,1)}), bf16[128,12,384]{0,2,1:T(8,128)(2,1)S(1)}, u32[]{:S(2)}, u32[]{:S(2)}) async-start(bf16[128,12,384]{0,2,1:T(8,128)(2,1)} %bitcast.11), calls=%async_computation.4 | async-start | bytes 2359296 | tf_op jit(solution)/shard_map/all_to_all | solution.py:73
  104.9 7.8 %copy-start.5 = (bf16[128,12,384]{0,2,1:T(8,128)(2,1)}, bf16[128,12,384]{0,2,1:T(8,128)(2,1)S(1)}, u32[]{:S(2)}) copy-start(bf16[128,12,384]{0,2,1:T(8,128)(2,1)S(1)} %all-to-all-done.4) | copy-start | bytes 3538948
  104.9 46.7 %all-to-all-start = ((bf16[128,12,384]{0,2,1:T(8,128)(2,1)}), bf16[128,12,384]{0,2,1:T(8,128)(2,1)}, u32[]{:S(2)}, u32[]{:S(2)}) async-start(bf16[128,12,384]{0,2,1:T(8,128)(2,1)} %bitcast), calls=%async_computation | async-start | bytes 2359296 | tf_op jit(solution)/shard_map/all_to_all | solution.py:74
  115.5 4.6 %copy-start.6 = (bf16[128,12,384]{0,2,1:T(8,128)(2,1)S(1)}, bf16[128,12,384]{0,2,1:T(8,128)(2,1)}, u32[]{:S(2)}) copy-start(bf16[128,12,384]{0,2,1:T(8,128)(2,1)} %copy-done.5) | copy-start | bytes 3538948
  130.3 4.1 %copy-start = (f32[6,256,3,128]{3,2,1,0:T(4,128)S(1)}, f32[6,256,3,128]{3,2,1,0:T(4,128)}, u32[]{:S(2)}) copy-start(f32[6,256,3,128]{3,2,1,0:T(4,128)} %reshape.169) | copy-start | bytes 7077892
  151.6 6.5 %copy-start.13 = (pred[256,256]{0,1:T(8,128)(4,1)S(1)}, pred[256,256]{0,1:T(8,128)(4,1)}, u32[]{:S(2)}) copy-start(pred[256,256]{0,1:T(8,128)(4,1)} %iota_compare_fusion) | copy-start | bytes 196612
  163.4 6.1 %copy-start.7 = (f32[6,3,256,256]{2,3,1,0:T(8,128)S(1)}, f32[6,3,256,256]{2,3,1,0:T(8,128)}, u32[]{:S(2)}) copy-start(f32[6,3,256,256]{2,3,1,0:T(8,128)} %get-tuple-element.18) | copy-start | bytes 14155780
  163.4 6.1 %copy-start.9 = (bf16[6,256,3,128]{3,2,1,0:T(4,128)(2,1)S(1)}, bf16[6,256,3,128]{3,2,1,0:T(4,128)(2,1)}, u32[]{:S(2)}) copy-start(bf16[6,256,3,128]{3,2,1,0:T(4,128)(2,1)} %get-tuple-element.14) | copy-start | bytes 3538948
  163.4 6.9 %copy-start.10 = (bf16[6,256,3,128]{3,2,1,0:T(4,128)(2,1)S(1)}, bf16[6,256,3,128]{3,2,1,0:T(4,128)(2,1)}, u32[]{:S(2)}) copy-start(bf16[6,256,3,128]{3,2,1,0:T(4,128)(2,1)} %reshape.163) | copy-start | bytes 3538948
  171.3 1.3 copy-start.2
  172.6 1.7 copy-start.4
  236.0 49.1 %collective-permute-start = (bf16[128,4608]{0,1:T(8,128)(2,1)S(1)}, bf16[128,4608]{0,1:T(8,128)(2,1)S(1)}, u32[]{:S(2)}, u32[]{:S(2)}) collective-permute-start(bf16[128,4608]{0,1:T(8,128)(2,1)S(1)} %bitcast.73), channel_id=1, source_target_pairs={{12,0},{24,12},{36,24},{48,36},{60,48},{72,60},{84,72},{96,84},{10... | collective-permute-start | bytes 3538952 | tf_op jit(solution)/shard_map/ppermute | solution.py:13
  285.1 1.0 copy-start.12
  286.2 19.6 %all-to-all-start.3 = ((bf16[128,12,384]{0,2,1:T(8,128)(2,1)}), bf16[128,12,384]{0,2,1:T(8,128)(2,1)}, u32[]{:S(2)}, u32[]{:S(2)}) async-start(bf16[128,12,384]{0,2,1:T(8,128)(2,1)} %bitcast.72), calls=%async_computation.3 | async-start | bytes 2359296 | tf_op jit(solution)/shard_map/all_to_all | solution.py:74
  307.9 2.0 copy-start.8
  309.9 3.9 %slice-start = ((s8[4718592]{0:T(1024)(128)(4,1)}), s8[4194304]{0:T(1024)(128)(4,1)S(1)}, s32[]{:S(2)}) async-start(s8[4718592]{0:T(1024)(128)(4,1)} %bitcast.68), calls=%async_computation.6 | async-start | bytes 8388608
  309.9 4.0 %slice-start.1 = ((s8[4718592]{0:T(1024)(128)(4,1)}), s8[524288]{0:T(1024)(128)(4,1)S(1)}, s32[]{:S(2)}) async-start(s8[4718592]{0:T(1024)(128)(4,1)} %bitcast.68), calls=%async_computation.7 | async-start | bytes 1048576
  313.9 1.3 copy-start.1
  342.8 3.2 copy-start.3
  370.1 19.6 %collective-permute-start.1 = (bf16[128,4608]{0,1:T(8,128)(2,1)S(1)}, bf16[128,4608]{0,1:T(8,128)(2,1)S(1)}, u32[]{:S(2)}, u32[]{:S(2)}) collective-permute-start(bf16[128,4608]{0,1:T(8,128)(2,1)S(1)} %bitcast.70), channel_id=1, source_target_pairs={{12,0},{24,12},{36,24},{48,36},{60,48},{72,60},{84,72},{96,84},{10... | collective-permute-start | bytes 3538952 | tf_op jit(solution)/shard_map/ppermute | solution.py:13
where the time goes:
time: 395 us; the launch traced here: 391 us
  waiting for transfers between devices  161 us (41%)
  local copies, waits for them, and re-layouts  89.3 us (23%)
  blocking collectives  52.1 us (13%)
  starting transfers between devices  37.5 us (9%)
  matrix products  33.9 us (9%)
  other arithmetic  16.2 us (4%)
    all_to_all x2, waiting for transfers between devices, heads_tick(): lax.all_to_all(inputs, 'tp', split_axis=1, concat_axis=0, tiled=True)  77.1 us
    ppermute x2, waiting for transfers between devices, from_behind(): return lax.ppermute(block, axis, route)  62.7 us
    all_to_all x2, blocking collectives, heads_tick(): lax.all_to_all(grad_in, 'tp', split_axis=0, concat_axis=1, tiled=True)  52.1 us
    all_to_all x2, waiting for transfers between devices, heads_tick(): lax.all_to_all(upstream, 'tp', split_axis=1, concat_axis=0, tiled=True)  21.5 us
    all_to_all x2, starting transfers between devices, heads_tick(): lax.all_to_all(inputs, 'tp', split_axis=1, concat_axis=0, tiled=True)  21.2 us
    convert_element_type x6, local copies, waits for them, and re-layouts, local_backward(): wide = inputs.astype(jnp.float32)  19 us
    reshape x4, local copies, waits for them, and re-layouts, local_backward(): value_total = value_grad.reshape(row_total, local_width)  15.9 us
    reshape x4, local copies, waits for them, and re-layouts, local_backward(): qk_total = (query_grad + key_grad).reshape(row_total, local_width)  13.8 us
  transfers between devices with their start and end apart: 6, of which 6 were waited for; matrix products, arithmetic and copies ran while one was open for 10% of the time, Pallas kernels for 0%

commit v1 on v0

--- a/solution.py
+++ b/solution.py
@@ -68,33 +68,30 @@
     return (grad_in, jnp.sum(wide * qk_total, axis=0), jnp.sum(wide * value_total, axis=0))
 
 
-def heads_tick(inputs, upstream, gain_qk, gain_value):
-    inputs_head, upstream_head = (
-        lax.all_to_all(inputs, "tp", split_axis=1, concat_axis=0, tiled=True),
-        lax.all_to_all(upstream, "tp", split_axis=1, concat_axis=0, tiled=True),
-    )
-    grad_in, qk_part, value_part = local_backward(inputs_head, upstream_head, gain_qk, gain_value)
-    grad_tokens = lax.all_to_all(grad_in, "tp", split_axis=0, concat_axis=1, tiled=True)
-    return (grad_tokens, qk_part, value_part)
+def to_heads(block):
+    return lax.all_to_all(block, "tp", split_axis=block.ndim - 1, concat_axis=block.ndim - 2, tiled=True)
 
 
 def shards(saved_inputs, incoming, qk_gain, value_gain):
-    upstream = incoming[0]
     tick_count = saved_inputs.shape[0]
     local_width = qk_gain.shape[1] // lax.axis_size("tp")
     offset = lax.axis_index("tp") * local_width
     gain_qk = lax.dynamic_slice_in_dim(qk_gain[0], offset, local_width)
     gain_value = lax.dynamic_slice_in_dim(value_gain[0], offset, local_width)
+    first = to_heads(jnp.stack([saved_inputs[0, 0], incoming[0]]))
+    inputs_heads = [first[0]] + [to_heads(saved_inputs[t, 0]) for t in range(1, tick_count)]
+    upstream = first[1]
     qk_sum = jnp.zeros((local_width,), jnp.float32)
     value_sum = jnp.zeros((local_width,), jnp.float32)
     for tick_index in range(tick_count):
-        grad_in, qk_part, value_part = heads_tick(
-            saved_inputs[tick_index, 0], upstream, gain_qk, gain_value
+        grad_in, qk_part, value_part = local_backward(
+            inputs_heads[tick_index], upstream, gain_qk, gain_value
         )
         qk_sum = qk_sum + qk_part
         value_sum = value_sum + value_part
         upstream = pass_on(grad_in)
-    return (upstream[None], qk_sum[None], value_sum[None])
+    passed = lax.all_to_all(upstream, "tp", split_axis=0, concat_axis=1, tiled=True)
+    return (passed[None], qk_sum[None], value_sum[None])
 
 
 def solution(mesh):

time: 395 us -> 335 us (0.85)
  blocking collectives: 52.1 us -> 0 us
  local copies, waits for them, and re-layouts: 89.3 us -> 70.7 us
  other arithmetic: 16.2 us -> 23.1 us
    all_to_all x2 -> x0, blocking collectives: 52.1 us -> none  [heads_tick(): lax.all_to_all(grad_in, 'tp', split_axis=0, concat_axis=1, tiled=True)]
    all_to_all x4 -> x3, waiting for transfers between devices: 98.6 us -> 138 us  [the longest x2 101 us: to_heads(): lax.all_to_all(block, 'tp', split_axis=block.ndim - 1, concat_axis=block....]
    ppermute x2, waiting for transfers between devices: 62.7 us -> 26 us  [from_behind(): return lax.ppermute(block, axis, route)]
    another operation x0 -> x3, local copies, waits for them, and re-layouts: none -> 12.1 us  [the longest x2 7.62 us: local_backward(): upstream.reshape(shape_four)]
    transpose x2 -> x0, local copies, waits for them, and re-layouts: 9.41 us -> none  [attend_grads(): jnp.einsum('nhqk,nqhe->nkhe', probs_low, upstream, preferred_element_type...]
    add x2 -> x0, local copies, waits for them, and re-layouts: 7.52 us -> none  [local_backward(): qk_total = (query_grad + key_grad).reshape(row_total, local_width)]
    reshape x4 -> x2, local copies, waits for them, and re-layouts: 15.9 us -> 8.93 us  [local_backward(): value_total = value_grad.reshape(row_total, local_width)]
    reshape x4 -> x2, local copies, waits for them, and re-layouts: 13.8 us -> 7.49 us  [local_backward(): qk_total = (query_grad + key_grad).reshape(row_total, local_width)]
  transfers between devices with their start and end apart: 6 -> 5, of which waited for: 6 -> 5; matrix products, arithmetic and copies ran while one was open for 10% -> 7% of each run, Pallas kernels for 0% -> 0%
where the time goes in v1:
time: 335 us; the launch traced here: 331 us
  waiting for transfers between devices  164 us (49%)
  local copies, waits for them, and re-layouts  70.7 us (21%)
  matrix products  37.5 us (11%)
  starting transfers between devices  34.9 us (10%)
  other arithmetic  23.1 us (7%)
    all_to_all x2, waiting for transfers between devices, to_heads(): lax.all_to_all(block, 'tp', split_axis=block.ndim - 1, concat_axis=block....  101 us
    all_to_all x1, waiting for transfers between devices, shards(): lax.all_to_all(upstream, 'tp', split_axis=0, concat_axis=1, tiled=True)  37 us
    ppermute x2, waiting for transfers between devices, from_behind(): return lax.ppermute(block, axis, route)  26 us
    all_to_all x2, starting transfers between devices, to_heads(): lax.all_to_all(block, 'tp', split_axis=block.ndim - 1, concat_axis=block....  21.2 us
    convert_element_type x6, local copies, waits for them, and re-layouts, local_backward(): wide = inputs.astype(jnp.float32)  20 us
    dot_general x2, matrix products, attend_grads(): jnp.einsum('nhqk,nqhe->nkhe', probs_low, upstream, preferred_element_type...  13 us
    sub x2, matrix products, attend_grads(): weights = jnp.exp(scores - row_max)  10.9 us
    reshape x2, local copies, waits for them, and re-layouts, local_backward(): value_total = value_grad.reshape(row_total, local_width)  8.93 us
  transfers between devices with their start and end apart: 5, of which 5 were waited for; matrix products, arithmetic and copies ran while one was open for 7% of the time, Pallas kernels for 0%

profile of v1, /device:TPU:57, one launch (start us, length us, event | category | flops | bytes accessed | tf_op | source)
XLA Modules:
  0.0 331.0 jit_solution(3233210989299325705)
XLA Ops:
  0.6 2.8 fusion.40
  3.4 1.4 copy.206
  4.8 16.1 %all-to-all-start.1 = ((bf16[128,12,384]{0,2,1:T(8,128)(2,1)}), bf16[128,12,384]{0,2,1:T(8,128)(2,1)S(1)}, u32[]{:S(2)}, u32[]{:S(2)}) async-start(bf16[128,12,384]{0,2,1:T(8,128)(2,1)} %bitcast.7), calls=%async_computation.1 | async-start | bytes 2359296 | tf_op jit(solution)/shard_map/all_to_all | solution.py:72
  21.0 1.8 pad_maximum_fusion
  22.8 4.5 %copy.148 = bf16[2,128,4608]{1,0,2:T(2,128)(2,1)} copy(bf16[2,128,4608]{2,1,0:T(8,128)(2,1)S(1)} %pad_maximum_fusion) | data formatting | bytes 4718592 | tf_op jit(solution)/shard_map/stack | solution.py:81
  27.3 32.6 %all-to-all-done.1 = bf16[128,12,384]{0,2,1:T(8,128)(2,1)S(1)} async-done(((bf16[128,12,384]{0,2,1:T(8,128)(2,1)}), bf16[128,12,384]{0,2,1:T(8,128)(2,1)S(1)}, u32[]{:S(2)}, u32[]{:S(2)}) %all-to-all-start.1) | async-done | bytes 1179680 | tf_op jit(solution)/shard_map/all_to_all | solution.py:72
  59.9 5.0 %all-to-all-start = ((bf16[2,128,4608]{1,0,2:T(2,128)(2,1)}), bf16[2,128,4608]{1,0,2:T(2,128)(2,1)}, u32[]{:S(2)}, u32[]{:S(2)}) async-start(bf16[2,128,4608]{1,0,2:T(2,128)(2,1)} %copy.148), calls=%async_computation | async-start | bytes 4718592 | tf_op jit(solution)/shard_map/all_to_all | solution.py:72
  66.6 2.0 copy.167
  68.6 3.5 %reshape.135 = f32[6,256,3,128]{3,2,1,0:T(4,128)S(1)} reshape(f32[12,128,384]{2,1,0:T(8,128)} %copy.167) | data formatting | bytes 4718592 | tf_op jit(solution)/shard_map/convert_element_type | solution.py:50
  72.0 68.4 %all-to-all-done = bf16[2,128,4608]{1,0,2:T(2,128)(2,1)} async-done(((bf16[2,128,4608]{1,0,2:T(2,128)(2,1)}), bf16[2,128,4608]{1,0,2:T(2,128)(2,1)}, u32[]{:S(2)}, u32[]{:S(2)}) %all-to-all-start) | async-done | bytes 2359328 | tf_op jit(solution)/shard_map/all_to_all | solution.py:72
  140.4 2.0 copy.149
  142.4 3.0 slice_convert_fusion.1
  145.4 3.1 copy.151
  148.5 4.5 %reshape.134 = f32[6,256,3,128]{3,2,1,0:T(4,128)} reshape(f32[1,12,128,384]{3,2,1,0:T(8,128)} %copy.151) | data formatting | bytes 4718592 | tf_op jit(solution)/shard_map/convert_element_type | solution.py:50
  153.0 4.5 %copy.183 = f32[6,256,3,128]{1,3,2,0:T(8,128)} copy(f32[6,256,3,128]{3,2,1,0:T(4,128)} %reshape.134) | data formatting | bytes 4718592 | tf_op jit(solution)/shard_map/convert_element_type | solution.py:50
  157.5 4.1 %fusion.10 = (bf16[6,256,3,128]{3,1,2,0:T(8,128)(2,1)}, bf16[6,256,3,128]{3,1,2,0:T(8,128)(2,1)}) fusion(f32[6,256,3,128]{3,2,1,0:T(4,128)S(1)} %reshape.135, f32[3,128]{1,0:T(4,128)S(1)} %bitcast.103, f32[6,256,3,128]{3,2,1,0:T(4,128)} %reshape.134), kind=kLoop, calls=%fused_computation.26 | loop fusion | flops 2359296 | bytes 7079424 | tf_op jit(solution)/shard_map/convert_element_type | solution.py:51
  161.6 3.1 multiply_convert_fusion.2
  164.7 2.4 copy.153
  167.1 4.1 %reshape_squeeze.3 = bf16[6,256,3,128]{3,2,1,0:T(4,128)(2,1)} reshape(bf16[1,12,128,384]{3,2,1,0:T(8,128)(2,1)} %copy.153) | data formatting | bytes 2359296 | tf_op jit(solution)/shard_map/reshape;squeeze | solution.py:59
  171.2 3.5 %copy.162 = bf16[6,256,3,128]{1,3,2,0:T(8,128)(2,1)} copy(bf16[6,256,3,128]{3,2,1,0:T(4,128)(2,1)} %reshape_squeeze.3) | data formatting | bytes 2359296 | tf_op jit(solution)/shard_map/reshape;squeeze | solution.py:59
  174.7 5.4 %fusion.41 = (f32[6,3,256]{2,1,0:T(4,128)S(1)}, f32[6,3,256,256]{2,3,1,0:T(8,128)}) fusion(pred[256,256]{0,1:T(8,128)(4,1)S(1)} %copy-done.4, bf16[6,256,3,128]{3,1,2,0:T(8,128)(2,1)} %get-tuple-element.27), kind=kOutput, calls=%fused_computation.71 | convolution fusion | flops 306708736 | bytes 5982208 | tf_op jit(solution)/shard_map/sub | solution.py:22
  180.2 4.1 %multiply_reduce_fusion.1 = (f32[6,3,256]{2,1,0:T(4,128)S(1)}, f32[6,3,256,256]{2,3,1,0:T(8,128)S(1)}) fusion(f32[6,3,256,256]{2,3,1,0:T(8,128)} %get-tuple-element.29, f32[6,3,256]{2,1,0:T(4,128)S(1)} %get-tuple-element.28, bf16[6,256,3,128]{1,3,2,0:T(8,128)(2,1)} %copy.162, bf16[6,256,3,128]{3,2,1,0:T(4,128)(2,1)} %get-tuple-element.25), kind=kOutput, calls=%fused_computation.7 | convolution fusion | flops 305524224 | bytes 11833344 | tf_op jit(solution)/shard_map/nqhe,nkhe->nhqk/dot_general | solution.py:25
  184.6 1.0 multiply_convert_fusion.1
  186.5 2.4 multiply_bitcast_fusion.1
  188.8 4.4 %copy.198 = f32[6,256,3,128]{3,2,1,0:T(4,128)} copy(f32[6,256,3,128]{1,3,2,0:T(8,128)} %multiply_bitcast_fusion.1) | data formatting | bytes 4718592 | tf_op jit(solution)/shard_map/reshape | solution.py:63
  193.3 6.5 %multiply_reduce_fusion.3 = (f32[3,128]{1,0:T(4,128)S(1)}, f32[3,128]{1,0:T(4,128)S(1)}, f32[6,256,3,128]{1,3,2,0:T(8,128)}) fusion(f32[6,256,3,128]{1,3,2,0:T(8,128)} %copy.183, f32[6,256,3,128]{1,3,2,0:T(8,128)} %multiply_bitcast_fusion.1, bf16[6,256,3,128]{1,3,2,0:T(8,128)(2,1)} %copy.162, f32[6,3,256,256]{2,3,1,0:T(8,128)} %get-tuple-element.29, ...), kind=kOutput, calls=%fused_computation.33 | convolution fusion | flops 306707712 | bytes 12997632 | tf_op jit(solution)/shard_map/nhqk,nqhe->nkhe/dot_general | solution.py:35
  199.7 4.5 %copy.199 = f32[6,256,3,128]{3,2,1,0:T(4,128)} copy(f32[6,256,3,128]{1,3,2,0:T(8,128)} %get-tuple-element.36) | data formatting | bytes 4718592 | tf_op jit(solution)/shard_map/reshape | solution.py:64
  204.2 3.0 copy.150
  207.2 5.3 %fusion.8 = bf16[1536,384]{1,0:T(8,128)(2,1)} fusion(f32[192,8,3,128]{3,2,1,0:T(4,128)} %bitcast.93, f32[192,8,3,128]{3,2,1,0:T(4,128)} %bitcast.91, f32[1,12,128,384]{3,2,1,0:T(8,128)} %copy.150, f32[384]{0:T(512)S(1)} %get-tuple-element.38, f32[384]{0:T(512)S(1)} %get-tuple-element.39), kind=kLoop, calls=%fused_computation.21 | loop fusion | flops 2949120 | bytes 8260608 | tf_op jit(solution)/shard_map/convert_element_type | solution.py:65
  212.5 4.0 %collective-permute-start = (bf16[1536,384]{1,0:T(8,128)(2,1)}, bf16[1536,384]{1,0:T(8,128)(2,1)}, u32[]{:S(2)}, u32[]{:S(2)}) collective-permute-start(bf16[1536,384]{1,0:T(8,128)(2,1)} %fusion.8), channel_id=1, source_target_pairs={{12,0},{24,12},{36,24},{48,36},{60,48},{72,60},{84,72},{96,84},{10... | collective-permute-start | bytes 3538952 | tf_op jit(solution)/shard_map/ppermute | solution.py:13
  216.5 2.5 copy.184
  219.0 5.4 %fusion.42 = (f32[6,3,256]{2,1,0:T(4,128)S(1)}, f32[6,3,256,256]{2,3,1,0:T(8,128)}) fusion(pred[256,256]{0,1:T(8,128)(4,1)S(1)} %copy-done.4, bf16[6,256,3,128]{3,1,2,0:T(8,128)(2,1)} %get-tuple-element.26), kind=kOutput, calls=%fused_computation.72 | convolution fusion | flops 306708736 | bytes 5982208 | tf_op jit(solution)/shard_map/sub | solution.py:22
  224.5 8.2 %collective-permute-done = bf16[1536,384]{1,0:T(8,128)(2,1)} collective-permute-done((bf16[1536,384]{1,0:T(8,128)(2,1)}, bf16[1536,384]{1,0:T(8,128)(2,1)}, u32[]{:S(2)}, u32[]{:S(2)}) %collective-permute-start) | collective-permute-done | bytes 1179680 | tf_op jit(solution)/shard_map/ppermute | solution.py:13
  232.6 3.3 reshape.144
  235.9 2.0 copy.178
  237.9 3.6 %multiply_reduce_fusion = (f32[6,3,256]{2,1,0:T(4,128)S(1)}, f32[6,3,256,256]{2,3,1,0:T(8,128)S(1)}) fusion(f32[6,3,256,256]{2,3,1,0:T(8,128)} %get-tuple-element.33, f32[6,3,256]{2,1,0:T(4,128)S(1)} %get-tuple-element.32, bf16[6,256,3,128]{1,3,2,0:T(8,128)(2,1)} %copy.178, bf16[6,256,3,128]{3,2,1,0:T(4,128)(2,1)S(1)} %copy-done.3), kind=kOutput, calls=%fused_computation.3 | convolution fusion | flops 305524224 | bytes 11833344 | tf_op jit(solution)/shard_map/nqhe,nkhe->nhqk/dot_general | solution.py:25
  242.0 1.0 multiply_convert_fusion
  243.8 2.4 multiply_bitcast_fusion
  246.2 3.0 copy.200
  249.2 6.5 %multiply_reduce_fusion.2 = (f32[3,128]{1,0:T(4,128)S(1)}, f32[3,128]{1,0:T(4,128)S(1)}, f32[6,256,3,128]{1,3,2,0:T(8,128)}) fusion(f32[6,256,3,128]{1,3,2,0:T(8,128)} %copy.184, f32[6,256,3,128]{1,3,2,0:T(8,128)} %multiply_bitcast_fusion, bf16[6,256,3,128]{1,3,2,0:T(8,128)(2,1)} %copy.178, f32[6,3,256,256]{2,3,1,0:T(8,128)} %get-tuple-element.33, ...), kind=kOutput, calls=%fused_computation.32 | convolution fusion | flops 306707712 | bytes 12997632 | tf_op jit(solution)/shard_map/nhqk,nqhe->nkhe/dot_general | solution.py:35
  255.8 4.5 %copy.201 = f32[6,256,3,128]{3,2,1,0:T(4,128)} copy(f32[6,256,3,128]{1,3,2,0:T(8,128)} %get-tuple-element.37) | data formatting | bytes 4718592 | tf_op jit(solution)/shard_map/reshape | solution.py:64
  260.2 2.9 fusion.5
  263.1 1.9 collective-permute-start.1
  265.1 17.8 %collective-permute-done.1 = bf16[1536,384]{1,0:T(8,128)(2,1)} collective-permute-done((bf16[1536,384]{1,0:T(8,128)(2,1)S(1)}, bf16[1536,384]{1,0:T(8,128)(2,1)}, u32[]{:S(2)}, u32[]{:S(2)}) %collective-permute-start.1) | collective-permute-done | bytes 1179680 | tf_op jit(solution)/shard_map/ppermute | solution.py:13
  282.9 7.8 %all-to-all-start.2 = ((bf16[12,128,384]{2,1,0:T(8,128)(2,1)}), bf16[12,128,384]{2,1,0:T(8,128)(2,1)S(1)}, u32[]{:S(2)}, u32[]{:S(2)}) async-start(bf16[12,128,384]{2,1,0:T(8,128)(2,1)} %bitcast.11), calls=%async_computation.2 | async-start | bytes 2359296 | tf_op jit(solution)/shard_map/all_to_all | solution.py:93
  291.8 37.0 %all-to-all-done.2 = bf16[12,128,384]{2,1,0:T(8,128)(2,1)S(1)} async-done(((bf16[12,128,384]{2,1,0:T(8,128)(2,1)}), bf16[12,128,384]{2,1,0:T(8,128)(2,1)S(1)}, u32[]{:S(2)}, u32[]{:S(2)}) %all-to-all-start.2) | async-done | bytes 1179680 | tf_op jit(solution)/shard_map/all_to_all | solution.py:93
  328.8 0.8 copy.182
  329.6 1.4 copy.187
  (29 shorter events, 5.1 us)
Async XLA Ops:
  4.8 55.1 %all-to-all-start.1 = ((bf16[128,12,384]{0,2,1:T(8,128)(2,1)}), bf16[128,12,384]{0,2,1:T(8,128)(2,1)S(1)}, u32[]{:S(2)}, u32[]{:S(2)}) async-start(bf16[128,12,384]{0,2,1:T(8,128)(2,1)} %bitcast.7), calls=%async_computation.1 | async-start | bytes 2359296 | tf_op jit(solution)/shard_map/all_to_all | solution.py:72
  59.9 80.5 %all-to-all-start = ((bf16[2,128,4608]{1,0,2:T(2,128)(2,1)}), bf16[2,128,4608]{1,0,2:T(2,128)(2,1)}, u32[]{:S(2)}, u32[]{:S(2)}) async-start(bf16[2,128,4608]{1,0,2:T(2,128)(2,1)} %copy.148), calls=%async_computation | async-start | bytes 4718592 | tf_op jit(solution)/shard_map/all_to_all | solution.py:72
  157.5 4.1 %copy-start = (f32[6,256,3,128]{3,2,1,0:T(4,128)S(1)}, f32[6,256,3,128]{3,2,1,0:T(4,128)}, u32[]{:S(2)}) copy-start(f32[6,256,3,128]{3,2,1,0:T(4,128)} %reshape.134) | copy-start | bytes 7077892
  167.1 7.6 %copy-start.4 = (pred[256,256]{0,1:T(8,128)(4,1)S(1)}, pred[256,256]{0,1:T(8,128)(4,1)}, u32[]{:S(2)}) copy-start(pred[256,256]{0,1:T(8,128)(4,1)} %iota_compare_fusion) | copy-start | bytes 196612
  180.2 4.4 %slice-start.2 = ((s8[4718592]{0:T(1024)(128)(4,1)}), s8[4194304]{0:T(1024)(128)(4,1)S(1)}, s32[]{:S(2)}) async-start(s8[4718592]{0:T(1024)(128)(4,1)} %bitcast.98), calls=%async_computation.5 | async-start | bytes 8388608
  180.2 4.5 %slice-start.3 = ((s8[4718592]{0:T(1024)(128)(4,1)}), s8[524288]{0:T(1024)(128)(4,1)S(1)}, s32[]{:S(2)}) async-start(s8[4718592]{0:T(1024)(128)(4,1)} %bitcast.98), calls=%async_computation.6 | async-start | bytes 1048576
  184.6 1.3 copy-start.2
  212.5 20.1 %collective-permute-start = (bf16[1536,384]{1,0:T(8,128)(2,1)}, bf16[1536,384]{1,0:T(8,128)(2,1)}, u32[]{:S(2)}, u32[]{:S(2)}) collective-permute-start(bf16[1536,384]{1,0:T(8,128)(2,1)} %fusion.8), channel_id=1, source_target_pairs={{12,0},{24,12},{36,24},{48,36},{60,48},{72,60},{84,72},{96,84},{10... | collective-permute-start | bytes 3538952 | tf_op jit(solution)/shard_map/ppermute | solution.py:13
  224.5 13.5 %copy-start.3 = (bf16[6,256,3,128]{3,2,1,0:T(4,128)(2,1)S(1)}, bf16[6,256,3,128]{3,2,1,0:T(4,128)(2,1)}, u32[]{:S(2)}) copy-start(bf16[6,256,3,128]{3,2,1,0:T(4,128)(2,1)} %get-tuple-element.24) | copy-start | bytes 3538948
  237.9 3.9 %slice-start = ((s8[4718592]{0:T(1024)(128)(4,1)}), s8[4194304]{0:T(1024)(128)(4,1)S(1)}, s32[]{:S(2)}) async-start(s8[4718592]{0:T(1024)(128)(4,1)} %bitcast.96), calls=%async_computation.3 | async-start | bytes 8388608
  237.9 4.0 %slice-start.1 = ((s8[4718592]{0:T(1024)(128)(4,1)}), s8[524288]{0:T(1024)(128)(4,1)S(1)}, s32[]{:S(2)}) async-start(s8[4718592]{0:T(1024)(128)(4,1)} %bitcast.96), calls=%async_computation.4 | async-start | bytes 1048576
  241.9 1.3 copy-start.1
  263.1 19.7 %collective-permute-start.1 = (bf16[1536,384]{1,0:T(8,128)(2,1)S(1)}, bf16[1536,384]{1,0:T(8,128)(2,1)}, u32[]{:S(2)}, u32[]{:S(2)}) collective-permute-start(bf16[1536,384]{1,0:T(8,128)(2,1)S(1)} %fusion.5), channel_id=1, source_target_pairs={{12,0},{24,12},{36,24},{48,36},{60,48},{72,60},{84,72},{96,84},{10... | collective-permute-start | bytes 3538952 | tf_op jit(solution)/shard_map/ppermute | solution.py:13
  282.9 46.0 %all-to-all-start.2 = ((bf16[12,128,384]{2,1,0:T(8,128)(2,1)}), bf16[12,128,384]{2,1,0:T(8,128)(2,1)S(1)}, u32[]{:S(2)}, u32[]{:S(2)}) async-start(bf16[12,128,384]{2,1,0:T(8,128)(2,1)} %bitcast.11), calls=%async_computation.2 | async-start | bytes 2359296 | tf_op jit(solution)/shard_map/all_to_all | solution.py:93

commit v2 on v1

v2 whole, which is shorter than its diff:
```python
import jax
import jax.numpy as jnp
from jax import lax
from jax.sharding import PartitionSpec as P
from jax.experimental import pallas as pl

HEAD_DIM = 128
SEQ_LEN = 256


def from_behind(block, axis, distance):
    devices = range(lax.axis_size(axis))
    route = [((i - distance) % len(devices), i) for i in devices]
    return lax.ppermute(block, axis, route)


def pass_on(grad_in):
    return from_behind(grad_in, "section", -1)


def attention_kernel(x_ref, u_ref, gq_ref, gv_ref, g_ref, qs_ref, vs_ref):
    n = pl.program_id(1)
    scale = HEAD_DIM ** (-0.5)
    wide = x_ref[...].astype(jnp.float32)
    gq = gq_ref[...]
    gv = gv_ref[...]
    keys = (wide * gq).astype(jnp.bfloat16)
    values = (wide * gv).astype(jnp.bfloat16)
    up = u_ref[...]
    nt = (((1,), (1,)), ((), ()))
    tn = (((0,), (0,)), ((), ()))
    scores = lax.dot_general(keys, keys, nt, preferred_element_type=jnp.float32) * scale
    rows = lax.broadcasted_iota(jnp.int32, scores.shape, 0)
    cols = lax.broadcasted_iota(jnp.int32, scores.shape, 1)
    scores = jnp.where(cols <= rows, scores, -jnp.inf)
    row_max = jnp.max(scores, axis=1, keepdims=True)
    weights = jnp.exp(scores - row_max)
    probs = weights / jnp.sum(weights, axis=1, keepdims=True)
    prob_grad = lax.dot_general(up, values, nt, preferred_element_type=jnp.float32)
    score_grad = probs * (prob_grad - jnp.sum(probs * prob_grad, axis=1, keepdims=True))
    score_low = score_grad.astype(jnp.bfloat16)
    probs_low = probs.astype(jnp.bfloat16)
    query_grad = jnp.dot(score_low, keys, preferred_element_type=jnp.float32) * scale
    key_grad = lax.dot_general(score_low, keys, tn, preferred_element_type=jnp.float32) * scale
    value_grad = lax.dot_general(probs_low, up, tn, preferred_element_type=jnp.float32)
    qk_total = query_grad + key_grad
    g_ref[...] = (up.astype(jnp.float32) + qk_total * gq + value_grad * gv).astype(jnp.bfloat16)
    qk_part = jnp.sum(wide * qk_total, axis=0, keepdims=True)
    value_part = jnp.sum(wide * value_grad, axis=0, keepdims=True)

    @pl.when(n == 0)
    def _():
        qs_ref[...] = qk_part
        vs_ref[...] = value_part

    @pl.when(n > 0)
    def _():
        qs_ref[...] += qk_part
        vs_ref[...] += value_part


INTERPRET = False


def local_backward(inputs, upstream, gain_qk, gain_value):
    rows, width = inputs.shape
    heads = width // HEAD_DIM
    count = rows // SEQ_LEN
    tile = pl.BlockSpec((SEQ_LEN, HEAD_DIM), lambda h, n: (n, h))
    gain = pl.BlockSpec((1, HEAD_DIM), lambda h, n: (0, h))
    flops = heads * count * 5 * 2 * SEQ_LEN * SEQ_LEN * HEAD_DIM
    grad_in, qk_part, value_part = pl.pallas_call(
        attention_kernel,
        grid=(heads, count),
        in_specs=[tile, tile, gain, gain],
        out_specs=[tile, gain, gain],
        out_shape=[
            jax.ShapeDtypeStruct((rows, width), jnp.bfloat16),
            jax.ShapeDtypeStruct((1, width), jnp.float32),
            jax.ShapeDtypeStruct((1, width), jnp.float32),
        ],
        cost_estimate=pl.CostEstimate(
            flops=flops,
            transcendentals=heads * count * SEQ_LEN * SEQ_LEN,
            bytes_accessed=3 * rows * width * 2,
        ),
        interpret=INTERPRET,
    )(inputs, upstream, gain_qk[None], gain_value[None])
    return grad_in, qk_part[0], value_part[0]


def to_heads(block):
    return lax.all_to_all(block, "tp", split_axis=block.ndim - 1, concat_axis=block.ndim - 2, tiled=True)


def shards(saved_inputs, incoming, qk_gain, value_gain):
    tick_count = saved_inputs.shape[0]
    local_width = qk_gain.shape[1] // lax.axis_size("tp")
    offset = lax.axis_index("tp") * local_width
    gain_qk = lax.dynamic_slice_in_dim(qk_gain[0], offset, local_width)
    gain_value = lax.dynamic_slice_in_dim(value_gain[0], offset, local_width)
    first = to_heads(jnp.stack([saved_inputs[0, 0], incoming[0]]))
    inputs_heads = [first[0]]
    for t in range(1, tick_count):
        first, later = lax.optimization_barrier((first, saved_inputs[t, 0]))
        inputs_heads.append(to_heads(later))
    upstream = first[1]
    qk_sum = jnp.zeros((local_width,), jnp.float32)
    value_sum = jnp.zeros((local_width,), jnp.float32)
    for tick_index in range(tick_count):
        grad_in, qk_part, value_part = local_backward(
            inputs_heads[tick_index], upstream, gain_qk, gain_value
        )
        qk_sum = qk_sum + qk_part
        value_sum = value_sum + value_part
        upstream = pass_on(grad_in)
    passed = lax.all_to_all(upstream, "tp", split_axis=0, concat_axis=1, tiled=True)
    return (passed[None], qk_sum[None], value_sum[None])


def solution(mesh):
    return jax.shard_map(
        shards,
        mesh=mesh,
        in_specs=(
            P(None, "section", "tp", None),
            P("section", "tp", None),
            P("section", None),
            P("section", None),
        ),
        out_specs=(P("section", "tp", None), P("section", "tp"), P("section", "tp")),
        check_vma=False,
    )
```

time: 335 us -> 246 us (0.73)
  the two profiles are of different devices: /device:TPU:57 before, /device:TPU:64 now
where the time goes in v2:
time: 246 us; the launch traced here: 244 us
  waiting for transfers between devices  140 us (57%)
  starting transfers between devices  45.1 us (18%)
  Pallas kernels  32.8 us (13%)
  local copies, waits for them, and re-layouts  23.7 us (10%)
    all_to_all x2, waiting for transfers between devices, to_heads(): lax.all_to_all(block, 'tp', split_axis=block.ndim - 1, concat_axis=block....  67.2 us
    ppermute x2, waiting for transfers between devices, from_behind(): return lax.ppermute(block, axis, route)  41.1 us
    pallas_call x2, Pallas kernels, local_backward(): pl.pallas_call(attention_kernel, grid=(heads, count), in_specs=[tile, til...  32.8 us
    all_to_all x1, waiting for transfers between devices, shards(): lax.all_to_all(upstream, 'tp', split_axis=0, concat_axis=1, tiled=True)  32 us
    all_to_all x2, starting transfers between devices, to_heads(): lax.all_to_all(block, 'tp', split_axis=block.ndim - 1, concat_axis=block....  27.7 us
    ppermute x2, starting transfers between devices, from_behind(): return lax.ppermute(block, axis, route)  13.7 us
    all_to_all x3, local copies, waits for them, and re-layouts, to_heads(): lax.all_to_all(block, 'tp', split_axis=block.ndim - 1, concat_axis=block....  5.86 us
  transfers between devices with their start and end apart: 5, of which 4 were waited for; matrix products, arithmetic and copies ran while one was open for 4% of the time, Pallas kernels for 7%

profile of v2, /device:TPU:64, one launch (start us, length us, event | category | flops | bytes accessed | tf_op | source)
XLA Modules:
  0.0 244.0 jit_solution(8529476417974068167)
XLA Ops:
  0.6 0.0 copy-start.1
  0.6 1.9 fusion
  2.5 0.1 copy-done.1
  2.6 0.2 pad_maximum_fusion
  2.8 4.4 %copy.27 = bf16[2,128,4608]{1,0,2:T(2,128)(2,1)} copy(bf16[2,128,4608]{2,1,0:T(8,128)(2,1)S(1)} %pad_maximum_fusion) | data formatting | bytes 4718592 | tf_op jit(solution)/shard_map/stack | solution.py:102
  7.3 15.5 %all-to-all-start = ((bf16[2,128,4608]{1,0,2:T(2,128)(2,1)}), bf16[2,128,4608]{1,0,2:T(2,128)(2,1)}, u32[]{:S(2)}, u32[]{:S(2)}) async-start(bf16[2,128,4608]{1,0,2:T(2,128)(2,1)} %copy.27), calls=%async_computation | async-start | bytes 4718592 | tf_op jit(solution)/shard_map/all_to_all | solution.py:93
  22.8 1.4 copy.35
  24.2 67.2 %all-to-all-done = bf16[2,128,4608]{1,0,2:T(2,128)(2,1)} async-done(((bf16[2,128,4608]{1,0,2:T(2,128)(2,1)}), bf16[2,128,4608]{1,0,2:T(2,128)(2,1)}, u32[]{:S(2)}, u32[]{:S(2)}) %all-to-all-start) | async-done | bytes 2359328 | tf_op jit(solution)/shard_map/all_to_all | solution.py:93
  91.4 2.0 copy.28
  93.4 2.5 %copy.29 = bf16[2,12,128,384]{3,2,1,0:T(8,128)(2,1)} copy(bf16[2,12,128,384]{2,3,1,0:T(8,128)(2,1)S(1)} %bitcast.17) | data formatting | bytes 4718592 | tf_op jit(solution)/shard_map/all_to_all | solution.py:93
  95.9 12.2 %all-to-all-start.1 = ((bf16[128,12,384]{0,2,1:T(8,128)(2,1)}), bf16[128,12,384]{0,2,1:T(8,128)(2,1)S(1)}, u32[]{:S(2)}, u32[]{:S(2)}) async-start(bf16[128,12,384]{0,2,1:T(8,128)(2,1)} %bitcast.5), calls=%async_computation.1 | async-start | bytes 2359296 | tf_op jit(solution)/shard_map/all_to_all | solution.py:93
  108.1 1.3 constant_dynamic-slice_fusion
  109.4 1.1 slice.17
  110.5 0.0 copy-start
  110.5 2.5 %copy.32 = bf16[1,12,128,384]{3,2,1,0:T(8,128)(2,1)} copy(bf16[1,12,128,384]{2,3,1,0:T(8,128)(2,1)} %slice.17) | data formatting | bytes 2359296 | tf_op jit(solution)/shard_map/slice | solution.py:103
  113.0 0.0 copy-done
  113.0 1.2 slice_bitcast_fusion.u_ref
  114.2 16.4 %shard_map.67 = (bf16[1536,384]{1,0:T(8,128)(2,1)}, f32[1,384]{1,0:T(1,128)}, f32[1,384]{1,0:T(1,128)}) custom-call(bf16[1536,384]{1,0:T(8,128)(2,1)} %bitcast.23, bf16[1536,384]{1,0:T(8,128)(2,1)} %slice_bitcast_fusion.u_ref, f32[1,384]{1,0:T(1,128)} %get-tuple-element.31.gq_ref, f32[1,384]{1,0:T(1,128)} %get-tuple-element.30.gv_ref), custom_call_target="tpu_custom_call" | custom-call | flops 1509949440 | bytes 3538944 | tf_op jit(solution)/shard_map/pallas_call | solution.py:72
  130.6 7.9 %collective-permute-start = (bf16[1536,384]{1,0:T(8,128)(2,1)}, bf16[1536,384]{1,0:T(8,128)(2,1)S(1)}, u32[]{:S(2)}, u32[]{:S(2)}) collective-permute-start(bf16[1536,384]{1,0:T(8,128)(2,1)} %get-tuple-element.13), channel_id=1, source_target_pairs={{12,0},{24,12},{36,24},{48,36},{60,48},{72,60},{84,72},{96,84},{10... | collective-permute-start | bytes 3538952 | tf_op jit(solution)/shard_map/ppermute | solution.py:14
  138.5 0.0 all-to-all-done.1
  138.5 1.4 copy.31
  139.9 20.4 %collective-permute-done.u_ref = bf16[1536,384]{1,0:T(8,128)(2,1)S(1)} collective-permute-done((bf16[1536,384]{1,0:T(8,128)(2,1)}, bf16[1536,384]{1,0:T(8,128)(2,1)S(1)}, u32[]{:S(2)}, u32[]{:S(2)}) %collective-permute-start) | collective-permute-done | bytes 1179680 | tf_op jit(solution)/shard_map/ppermute | solution.py:14
  160.3 0.0 copy-start.6
  160.3 1.1 copy-done.6
  161.4 16.4 %shard_map.68 = (bf16[1536,384]{1,0:T(8,128)(2,1)}, f32[1,384]{1,0:T(1,128)}, f32[1,384]{1,0:T(1,128)}) custom-call(bf16[1536,384]{1,0:T(8,128)(2,1)} %bitcast.22, bf16[1536,384]{1,0:T(8,128)(2,1)} %copy-done.6, f32[1,384]{1,0:T(1,128)} %get-tuple-element.31.gq_ref, f32[1,384]{1,0:T(1,128)} %get-tuple-element.30.gv_ref), custom_call_target="tpu_custom_call" | custom-call | flops 1509949440 | bytes 3538944 | tf_op jit(solution)/shard_map/pallas_call | solution.py:72
  177.8 5.8 %collective-permute-start.1 = (bf16[1536,384]{1,0:T(8,128)(2,1)}, bf16[1536,384]{1,0:T(8,128)(2,1)S(1)}, u32[]{:S(2)}, u32[]{:S(2)}) collective-permute-start(bf16[1536,384]{1,0:T(8,128)(2,1)} %get-tuple-element.14), channel_id=1, source_target_pairs={{12,0},{24,12},{36,24},{48,36},{60,48},{72,60},{84,72},{96,84},{10... | collective-permute-start | bytes 3538952 | tf_op jit(solution)/shard_map/ppermute | solution.py:14
  183.6 20.7 %collective-permute-done.1 = bf16[1536,384]{1,0:T(8,128)(2,1)S(1)} collective-permute-done((bf16[1536,384]{1,0:T(8,128)(2,1)}, bf16[1536,384]{1,0:T(8,128)(2,1)S(1)}, u32[]{:S(2)}, u32[]{:S(2)}) %collective-permute-start.1) | collective-permute-done | bytes 1179680 | tf_op jit(solution)/shard_map/ppermute | solution.py:14
  204.3 1.4 copy.33
  205.7 0.0 copy-start.3
  205.7 0.0 copy-start.5
  205.7 0.0 copy-start.2
  205.7 0.0 copy-start.4
  205.8 3.7 %all-to-all-start.2 = ((bf16[12,128,384]{1,2,0:T(8,128)(2,1)}), bf16[12,128,384]{1,2,0:T(8,128)(2,1)S(1)}, u32[]{:S(2)}, u32[]{:S(2)}) async-start(bf16[12,128,384]{1,2,0:T(8,128)(2,1)} %copy.33), calls=%async_computation.2 | async-start | bytes 2359296 | tf_op jit(solution)/shard_map/all_to_all | solution.py:117
  209.5 0.0 copy-done.3
  209.5 0.0 copy-done.5
  209.5 0.6 add.14
  210.1 0.0 copy-done.2
  210.1 0.0 copy-done.4
  210.1 0.6 add.13
  210.6 32.0 %all-to-all-done.2 = bf16[12,128,384]{1,2,0:T(8,128)(2,1)S(1)} async-done(((bf16[12,128,384]{1,2,0:T(8,128)(2,1)}), bf16[12,128,384]{1,2,0:T(8,128)(2,1)S(1)}, u32[]{:S(2)}, u32[]{:S(2)}) %all-to-all-start.2) | async-done | bytes 1179680 | tf_op jit(solution)/shard_map/all_to_all | solution.py:117
  242.6 1.4 copy.34
Async XLA Ops:
  0.6 2.0 copy-start.1
  7.3 84.1 %all-to-all-start = ((bf16[2,128,4608]{1,0,2:T(2,128)(2,1)}), bf16[2,128,4608]{1,0,2:T(2,128)(2,1)}, u32[]{:S(2)}, u32[]{:S(2)}) async-start(bf16[2,128,4608]{1,0,2:T(2,128)(2,1)} %copy.27), calls=%async_computation | async-start | bytes 4718592 | tf_op jit(solution)/shard_map/all_to_all | solution.py:93
  95.9 42.6 %all-to-all-start.1 = ((bf16[128,12,384]{0,2,1:T(8,128)(2,1)}), bf16[128,12,384]{0,2,1:T(8,128)(2,1)S(1)}, u32[]{:S(2)}, u32[]{:S(2)}) async-start(bf16[128,12,384]{0,2,1:T(8,128)(2,1)} %bitcast.5), calls=%async_computation.1 | async-start | bytes 2359296 | tf_op jit(solution)/shard_map/all_to_all | solution.py:93
  110.5 2.5 %copy-start = (bf16[2,12,128,384]{3,2,1,0:T(8,128)(2,1)S(1)}, bf16[2,12,128,384]{3,2,1,0:T(8,128)(2,1)}, u32[]{:S(2)}) copy-start(bf16[2,12,128,384]{3,2,1,0:T(8,128)(2,1)} %copy.29) | copy-start | bytes 7077892
  130.6 29.7 %collective-permute-start = (bf16[1536,384]{1,0:T(8,128)(2,1)}, bf16[1536,384]{1,0:T(8,128)(2,1)S(1)}, u32[]{:S(2)}, u32[]{:S(2)}) collective-permute-start(bf16[1536,384]{1,0:T(8,128)(2,1)} %get-tuple-element.13), channel_id=1, source_target_pairs={{12,0},{24,12},{36,24},{48,36},{60,48},{72,60},{84,72},{96,84},{10... | collective-permute-start | bytes 3538952 | tf_op jit(solution)/shard_map/ppermute | solution.py:14
  160.3 1.1 copy-start.6
  177.8 26.5 %collective-permute-start.1 = (bf16[1536,384]{1,0:T(8,128)(2,1)}, bf16[1536,384]{1,0:T(8,128)(2,1)S(1)}, u32[]{:S(2)}, u32[]{:S(2)}) collective-permute-start(bf16[1536,384]{1,0:T(8,128)(2,1)} %get-tuple-element.14), channel_id=1, source_target_pairs={{12,0},{24,12},{36,24},{48,36},{60,48},{72,60},{84,72},{96,84},{10... | collective-permute-start | bytes 3538952 | tf_op jit(solution)/shard_map/ppermute | solution.py:14
  205.7 3.7 %copy-start.3 = (f32[1,384]{1,0:T(1,128)S(1)}, f32[1,384]{1,0:T(1,128)}, u32[]{:S(2)}) copy-start(f32[1,384]{1,0:T(1,128)} %get-tuple-element.17) | copy-start | bytes 4612
  205.7 3.7 %copy-start.5 = (f32[1,384]{1,0:T(1,128)S(1)}, f32[1,384]{1,0:T(1,128)}, u32[]{:S(2)}) copy-start(f32[1,384]{1,0:T(1,128)} %get-tuple-element.18) | copy-start | bytes 4612
  205.7 4.3 %copy-start.2 = (f32[1,384]{1,0:T(1,128)S(1)}, f32[1,384]{1,0:T(1,128)}, u32[]{:S(2)}) copy-start(f32[1,384]{1,0:T(1,128)} %get-tuple-element.15) | copy-start | bytes 4612
  205.7 4.3 %copy-start.4 = (f32[1,384]{1,0:T(1,128)S(1)}, f32[1,384]{1,0:T(1,128)}, u32[]{:S(2)}) copy-start(f32[1,384]{1,0:T(1,128)} %get-tuple-element.16) | copy-start | bytes 4612
  205.8 36.9 %all-to-all-start.2 = ((bf16[12,128,384]{1,2,0:T(8,128)(2,1)}), bf16[12,128,384]{1,2,0:T(8,128)(2,1)S(1)}, u32[]{:S(2)}, u32[]{:S(2)}) async-start(bf16[12,128,384]{1,2,0:T(8,128)(2,1)} %copy.33), calls=%async_computation.2 | async-start | bytes 2359296 | tf_op jit(solution)/shard_map/all_to_all | solution.py:117

commit v3 on v2

--- a/solution.py
+++ b/solution.py
@@ -94,28 +94,21 @@
 
 
 def shards(saved_inputs, incoming, qk_gain, value_gain):
-    tick_count = saved_inputs.shape[0]
     local_width = qk_gain.shape[1] // lax.axis_size("tp")
     offset = lax.axis_index("tp") * local_width
     gain_qk = lax.dynamic_slice_in_dim(qk_gain[0], offset, local_width)
     gain_value = lax.dynamic_slice_in_dim(value_gain[0], offset, local_width)
+    gains_next = pass_on(jnp.stack([gain_qk, gain_value]))
+    inputs_next = pass_on(saved_inputs[1, 0])
     first = to_heads(jnp.stack([saved_inputs[0, 0], incoming[0]]))
-    inputs_heads = [first[0]]
-    for t in range(1, tick_count):
-        first, later = lax.optimization_barrier((first, saved_inputs[t, 0]))
-        inputs_heads.append(to_heads(later))
-    upstream = first[1]
-    qk_sum = jnp.zeros((local_width,), jnp.float32)
-    value_sum = jnp.zeros((local_width,), jnp.float32)
-    for tick_index in range(tick_count):
-        grad_in, qk_part, value_part = local_backward(
-            inputs_heads[tick_index], upstream, gain_qk, gain_value
-        )
-        qk_sum = qk_sum + qk_part
-        value_sum = value_sum + value_part
-        upstream = pass_on(grad_in)
-    passed = lax.all_to_all(upstream, "tp", split_axis=0, concat_axis=1, tiled=True)
-    return (passed[None], qk_sum[None], value_sum[None])
+    grad_0, qk_0, value_0 = local_backward(first[0], first[1], gain_qk, gain_value)
+    upstream_next = from_behind(grad_0, "section", -2)
+    first, later = lax.optimization_barrier((first, inputs_next))
+    inputs_heads = to_heads(later)
+    grad_1, qk_1, value_1 = local_backward(inputs_heads, upstream_next, gains_next[0], gains_next[1])
+    sums_1 = from_behind(jnp.stack([qk_1, value_1]), "section", 1)
+    passed = lax.all_to_all(grad_1, "tp", split_axis=0, concat_axis=1, tiled=True)
+    return (passed[None], (qk_0 + sums_1[0])[None], (value_0 + sums_1[1])[None])
 
 
 def solution(mesh):

time: 246 us -> 255 us (1.037)
  the two profiles are of different devices: /device:TPU:64 before, /device:TPU:57 now
where the time goes in v3:
time: 255 us; the launch traced here: 253 us
  waiting for transfers between devices  149 us (58%)
  starting transfers between devices  49 us (19%)
  Pallas kernels  32.8 us (13%)
  local copies, waits for them, and re-layouts  20.3 us (8%)
    ppermute x4, waiting for transfers between devices, from_behind(): return lax.ppermute(block, axis, route)  137 us
    pallas_call x2, Pallas kernels, local_backward(): pl.pallas_call(attention_kernel, grid=(heads, count), in_specs=[tile, til...  32.8 us
    all_to_all x2, starting transfers between devices, to_heads(): lax.all_to_all(block, 'tp', split_axis=block.ndim - 1, concat_axis=block....  31.5 us
    all_to_all x1, waiting for transfers between devices, shards(): lax.all_to_all(grad_1, 'tp', split_axis=0, concat_axis=1, tiled=True)  12.2 us
    all_to_all x1, starting transfers between devices, shards(): lax.all_to_all(grad_1, 'tp', split_axis=0, concat_axis=1, tiled=True)  8.95 us
    ppermute x4, starting transfers between devices, from_behind(): return lax.ppermute(block, axis, route)  8.6 us
    another operation x2, local copies, waits for them, and re-layouts, shards(): first = to_heads(jnp.stack([saved_inputs[0, 0], incoming[0]]))  6.32 us
  transfers between devices with their start and end apart: 7, of which 4 were waited for; matrix products, arithmetic and copies ran while one was open for 3% of the time, Pallas kernels for 6%

profile of v3, /device:TPU:57, one launch (start us, length us, event | category | flops | bytes accessed | tf_op | source)
XLA Modules:
  0.0 253.0 jit_solution(12595476620329426561)
XLA Ops:
  0.6 0.0 copy-start.1
  0.6 1.9 slice_bitcast_fusion
  2.5 0.1 copy-done.1
  2.6 0.2 pad_maximum_fusion
  2.8 4.4 %copy.29 = bf16[2,128,4608]{1,0,2:T(2,128)(2,1)} copy(bf16[2,128,4608]{2,1,0:T(8,128)(2,1)S(1)} %pad_maximum_fusion) | data formatting | bytes 4718592 | tf_op jit(solution)/shard_map/stack | solution.py:103
  7.3 16.1 %all-to-all-start.1 = ((bf16[2,128,4608]{1,0,2:T(2,128)(2,1)}), bf16[2,128,4608]{1,0,2:T(2,128)(2,1)S(1)}, u32[]{:S(2)}, u32[]{:S(2)}) async-start(bf16[2,128,4608]{1,0,2:T(2,128)(2,1)} %copy.29), calls=%async_computation.1 | async-start | bytes 4718592 | tf_op jit(solution)/shard_map/all_to_all | solution.py:93
  23.4 1.4 copy.35
  24.8 2.9 %collective-permute-start = (bf16[128,4608]{0,1:T(8,128)(2,1)}, bf16[128,4608]{0,1:T(8,128)(2,1)S(1)}, u32[]{:S(2)}, u32[]{:S(2)}) collective-permute-start(bf16[128,4608]{0,1:T(8,128)(2,1)} %bitcast.23), channel_id=1, source_target_pairs={{12,0},{24,12},{36,24},{48,36},{60,48},{72,60},{84,72},{96,84},{10... | collective-permute-start | bytes 3538952 | tf_op jit(solution)/shard_map/ppermute | solution.py:14
  27.7 77.3 %collective-permute-done = bf16[128,4608]{0,1:T(8,128)(2,1)S(1)} collective-permute-done((bf16[128,4608]{0,1:T(8,128)(2,1)}, bf16[128,4608]{0,1:T(8,128)(2,1)S(1)}, u32[]{:S(2)}, u32[]{:S(2)}) %collective-permute-start) | collective-permute-done | bytes 1179680 | tf_op jit(solution)/shard_map/ppermute | solution.py:14
  105.0 0.0 copy-start
  105.0 0.0 all-to-all-done.1
  105.0 1.0 copy-done
  106.0 15.3 %all-to-all-start = ((bf16[128,12,384]{0,2,1:T(8,128)(2,1)}), bf16[128,12,384]{0,2,1:T(8,128)(2,1)S(1)}, u32[]{:S(2)}, u32[]{:S(2)}) async-start(bf16[128,12,384]{0,2,1:T(8,128)(2,1)} %bitcast.18), calls=%async_computation | async-start | bytes 2359296 | tf_op jit(solution)/shard_map/all_to_all | solution.py:93
  121.4 1.3 constant_dynamic-slice_fusion
  122.7 0.3 copy.30
  123.0 0.2 fusion
  123.2 1.4 copy.31
  124.6 1.4 copy.32
  126.0 0.0 copy-start.2
  126.0 0.0 copy-start.3
  126.0 16.4 %shard_map.67 = (bf16[1536,384]{1,0:T(8,128)(2,1)}, f32[1,384]{1,0:T(1,128)}, f32[1,384]{1,0:T(1,128)}) custom-call(bf16[1536,384]{1,0:T(8,128)(2,1)} %bitcast.20, bf16[1536,384]{1,0:T(8,128)(2,1)} %bitcast.22, f32[1,384]{1,0:T(1,128)} %get-tuple-element.33.gq_ref, f32[1,384]{1,0:T(1,128)} %get-tuple-element.32.gv_ref), custom_call_target="tpu_custom_call" | custom-call | flops 1509949440 | bytes 3538944 | tf_op jit(solution)/shard_map/pallas_call | solution.py:72
  142.5 1.9 collective-permute-start.1
  144.4 0.0 copy-done.2
  144.4 0.0 copy-done.3
  144.4 1.9 collective-permute-start.2
  146.4 33.7 %collective-permute-done.2 = f32[2,384]{1,0:T(2,128)S(1)} collective-permute-done((f32[2,384]{1,0:T(2,128)S(1)}, f32[2,384]{1,0:T(2,128)S(1)}, u32[]{:S(2)}, u32[]{:S(2)}) %collective-permute-start.2) | collective-permute-done | bytes 3104 | tf_op jit(solution)/shard_map/ppermute | solution.py:14
  180.0 0.6 fusion.1
  180.6 0.0 all-to-all-done
  180.6 1.4 copy.28
  182.0 0.0 collective-permute-done.1.u_ref
  182.0 0.0 copy-start.8
  182.0 1.0 copy-done.8
  183.1 16.4 %shard_map.68 = (bf16[1536,384]{1,0:T(8,128)(2,1)}, f32[1,384]{1,0:T(1,128)}, f32[1,384]{1,0:T(1,128)}) custom-call(bf16[1536,384]{1,0:T(8,128)(2,1)} %bitcast.19, bf16[1536,384]{1,0:T(8,128)(2,1)} %copy-done.8, f32[1,384]{1,0:T(1,128)} %get-tuple-element.31.gq_ref, f32[1,384]{1,0:T(1,128)} %get-tuple-element.30.gv_ref), custom_call_target="tpu_custom_call" | custom-call | flops 1509949440 | bytes 3538944 | tf_op jit(solution)/shard_map/pallas_call | solution.py:72
  199.5 2.4 copy.33
  201.8 0.0 copy-start.6
  201.8 0.0 copy-start.7
  201.8 0.0 copy-start.4
  201.8 0.0 copy-start.5
  201.8 8.9 %all-to-all-start.2 = ((bf16[12,128,384]{1,2,0:T(8,128)(2,1)}), bf16[12,128,384]{1,2,0:T(8,128)(2,1)S(1)}, u32[]{:S(2)}, u32[]{:S(2)}) async-start(bf16[12,128,384]{1,2,0:T(8,128)(2,1)} %copy.33), calls=%async_computation.2 | async-start | bytes 2359296 | tf_op jit(solution)/shard_map/all_to_all | solution.py:110
  210.8 0.0 copy-done.6
  210.8 0.0 copy-done.7
  210.8 1.9 collective-permute-start.3
  212.8 26.1 %collective-permute-done.3 = f32[2,384]{1,0:T(2,128)S(1)} collective-permute-done((f32[2,384]{1,0:T(2,128)S(1)}, f32[2,384]{1,0:T(2,128)S(1)}, u32[]{:S(2)}, u32[]{:S(2)}) %collective-permute-start.3) | collective-permute-done | bytes 3104 | tf_op jit(solution)/shard_map/ppermute | solution.py:14
  238.8 0.0 copy-done.4
  238.8 0.0 copy-done.5
  238.8 0.6 slice_add_fusion
  239.4 12.2 %all-to-all-done.2 = bf16[12,128,384]{1,2,0:T(8,128)(2,1)S(1)} async-done(((bf16[12,128,384]{1,2,0:T(8,128)(2,1)}), bf16[12,128,384]{1,2,0:T(8,128)(2,1)S(1)}, u32[]{:S(2)}, u32[]{:S(2)}) %all-to-all-start.2) | async-done | bytes 1179680 | tf_op jit(solution)/shard_map/all_to_all | solution.py:110
  251.6 1.4 copy.34
  (2 shorter events, 0.0 us)
Async XLA Ops:
  0.6 2.0 copy-start.1
  7.3 97.8 %all-to-all-start.1 = ((bf16[2,128,4608]{1,0,2:T(2,128)(2,1)}), bf16[2,128,4608]{1,0,2:T(2,128)(2,1)S(1)}, u32[]{:S(2)}, u32[]{:S(2)}) async-start(bf16[2,128,4608]{1,0,2:T(2,128)(2,1)} %copy.29), calls=%async_computation.1 | async-start | bytes 4718592 | tf_op jit(solution)/shard_map/all_to_all | solution.py:93
  24.8 80.2 %collective-permute-start = (bf16[128,4608]{0,1:T(8,128)(2,1)}, bf16[128,4608]{0,1:T(8,128)(2,1)S(1)}, u32[]{:S(2)}, u32[]{:S(2)}) collective-permute-start(bf16[128,4608]{0,1:T(8,128)(2,1)} %bitcast.23), channel_id=1, source_target_pairs={{12,0},{24,12},{36,24},{48,36},{60,48},{72,60},{84,72},{96,84},{10... | collective-permute-start | bytes 3538952 | tf_op jit(solution)/shard_map/ppermute | solution.py:14
  105.0 1.0 copy-start
  106.0 74.6 %all-to-all-start = ((bf16[128,12,384]{0,2,1:T(8,128)(2,1)}), bf16[128,12,384]{0,2,1:T(8,128)(2,1)S(1)}, u32[]{:S(2)}, u32[]{:S(2)}) async-start(bf16[128,12,384]{0,2,1:T(8,128)(2,1)} %bitcast.18), calls=%async_computation | async-start | bytes 2359296 | tf_op jit(solution)/shard_map/all_to_all | solution.py:93
  126.0 18.4 %copy-start.2 = (f32[1,384]{1,0:T(1,128)S(1)}, f32[1,384]{1,0:T(1,128)}, u32[]{:S(2)}) copy-start(f32[1,384]{1,0:T(1,128)} %get-tuple-element.32.gv_ref) | copy-start | bytes 4612
  126.0 18.4 %copy-start.3 = (f32[1,384]{1,0:T(1,128)S(1)}, f32[1,384]{1,0:T(1,128)}, u32[]{:S(2)}) copy-start(f32[1,384]{1,0:T(1,128)} %get-tuple-element.33.gq_ref) | copy-start | bytes 4612
  142.5 39.5 %collective-permute-start.1 = (bf16[1536,384]{1,0:T(8,128)(2,1)}, bf16[1536,384]{1,0:T(8,128)(2,1)S(1)}, u32[]{:S(2)}, u32[]{:S(2)}) collective-permute-start(bf16[1536,384]{1,0:T(8,128)(2,1)} %get-tuple-element.9), channel_id=1, source_target_pairs={{24,0},{36,12},{48,24},{60,36},{72,48},{84,60},{96,72},{108,84},{1... | collective-permute-start | bytes 3538952 | tf_op jit(solution)/shard_map/ppermute | solution.py:14
  144.4 35.6 %collective-permute-start.2 = (f32[2,384]{1,0:T(2,128)S(1)}, f32[2,384]{1,0:T(2,128)S(1)}, u32[]{:S(2)}, u32[]{:S(2)}) collective-permute-start(f32[2,384]{1,0:T(2,128)S(1)} %pad_maximum_fusion.1), channel_id=1, source_target_pairs={{12,0},{24,12},{36,24},{48,36},{60,48},{72,60},{84,72},{96,84},{10... | collective-permute-start | bytes 9224 | tf_op jit(solution)/shard_map/ppermute | solution.py:14
  182.0 1.0 copy-start.8
  201.8 9.0 %copy-start.6 = (f32[1,384]{1,0:T(1,128)S(1)}, f32[1,384]{1,0:T(1,128)}, u32[]{:S(2)}) copy-start(f32[1,384]{1,0:T(1,128)} %get-tuple-element.12) | copy-start | bytes 4612
  201.8 9.0 %copy-start.7 = (f32[1,384]{1,0:T(1,128)S(1)}, f32[1,384]{1,0:T(1,128)}, u32[]{:S(2)}) copy-start(f32[1,384]{1,0:T(1,128)} %get-tuple-element.13) | copy-start | bytes 4612
  201.8 37.0 %copy-start.4 = (f32[1,384]{1,0:T(1,128)S(1)}, f32[1,384]{1,0:T(1,128)}, u32[]{:S(2)}) copy-start(f32[1,384]{1,0:T(1,128)} %get-tuple-element.11) | copy-start | bytes 4612
  201.8 37.0 %copy-start.5 = (f32[1,384]{1,0:T(1,128)S(1)}, f32[1,384]{1,0:T(1,128)}, u32[]{:S(2)}) copy-start(f32[1,384]{1,0:T(1,128)} %get-tuple-element.14) | copy-start | bytes 4612
  201.8 49.7 %all-to-all-start.2 = ((bf16[12,128,384]{1,2,0:T(8,128)(2,1)}), bf16[12,128,384]{1,2,0:T(8,128)(2,1)S(1)}, u32[]{:S(2)}, u32[]{:S(2)}) async-start(bf16[12,128,384]{1,2,0:T(8,128)(2,1)} %copy.33), calls=%async_computation.2 | async-start | bytes 2359296 | tf_op jit(solution)/shard_map/all_to_all | solution.py:110
  210.8 28.0 %collective-permute-start.3 = (f32[2,384]{1,0:T(2,128)S(1)}, f32[2,384]{1,0:T(2,128)S(1)}, u32[]{:S(2)}, u32[]{:S(2)}) collective-permute-start(f32[2,384]{1,0:T(2,128)S(1)} %pad_maximum_fusion.2), channel_id=1, source_target_pairs={{756,0},{0,12},{12,24},{24,36},{36,48},{48,60},{60,72},{72,84},{84... | collective-permute-start | bytes 9224 | tf_op jit(solution)/shard_map/ppermute | solution.py:14

commit v4 on v3

--- a/solution.py
+++ b/solution.py
@@ -101,6 +101,7 @@
     gains_next = pass_on(jnp.stack([gain_qk, gain_value]))
     inputs_next = pass_on(saved_inputs[1, 0])
     first = to_heads(jnp.stack([saved_inputs[0, 0], incoming[0]]))
+    first, gains_next = lax.optimization_barrier((first, gains_next))
     grad_0, qk_0, value_0 = local_backward(first[0], first[1], gain_qk, gain_value)
     upstream_next = from_behind(grad_0, "section", -2)
     first, later = lax.optimization_barrier((first, inputs_next))

time: 255 us -> 256 us (level)
  starting transfers between devices: 49 us -> 43.9 us
  waiting for transfers between devices: 149 us -> 154 us
    ppermute x4, waiting for transfers between devices: 137 us -> 45.2 us  [from_behind(): return lax.ppermute(block, axis, route)]
    all_to_all x2, waiting for transfers between devices: 0.01 us -> 85 us  [to_heads(): lax.all_to_all(block, 'tp', split_axis=block.ndim - 1, concat_axis=block....]
    all_to_all x1, waiting for transfers between devices: 12.2 us -> 23.5 us  [shards(): lax.all_to_all(grad_1, 'tp', split_axis=0, concat_axis=1, tiled=True)]
    all_to_all x2, starting transfers between devices: 31.5 us -> 25.2 us  [to_heads(): lax.all_to_all(block, 'tp', split_axis=block.ndim - 1, concat_axis=block....]
    all_to_all x2 -> x3, local copies, waits for them, and re-layouts: 1.71 us -> 6.15 us  [to_heads(): lax.all_to_all(block, 'tp', split_axis=block.ndim - 1, concat_axis=block....]
    ppermute x4, starting transfers between devices: 8.6 us -> 12.4 us  [from_behind(): return lax.ppermute(block, axis, route)]
    all_to_all x1, starting transfers between devices: 8.95 us -> 6.24 us  [shards(): lax.all_to_all(grad_1, 'tp', split_axis=0, concat_axis=1, tiled=True)]
    another operation x2 -> x1, local copies, waits for them, and re-layouts: 6.32 us -> 4.48 us  [shards(): first = to_heads(jnp.stack([saved_inputs[0, 0], incoming[0]]))]
  transfers between devices with their start and end apart: 7 -> 7, of which waited for: 4 -> 6; matrix products, arithmetic and copies ran while one was open for 3% -> 4% of each run, Pallas kernels for 6% -> 6%
where the time goes in v4:
time: 256 us; the launch traced here: 254 us
  waiting for transfers between devices  154 us (60%)
  starting transfers between devices  43.9 us (17%)
  Pallas kernels  32.8 us (13%)
  local copies, waits for them, and re-layouts  21.7 us (8%)
    all_to_all x2, waiting for transfers between devices, to_heads(): lax.all_to_all(block, 'tp', split_axis=block.ndim - 1, concat_axis=block....  85 us
    ppermute x4, waiting for transfers between devices, from_behind(): return lax.ppermute(block, axis, route)  45.2 us
    pallas_call x2, Pallas kernels, local_backward(): pl.pallas_call(attention_kernel, grid=(heads, count), in_specs=[tile, til...  32.8 us
    all_to_all x2, starting transfers between devices, to_heads(): lax.all_to_all(block, 'tp', split_axis=block.ndim - 1, concat_axis=block....  25.2 us
    all_to_all x1, waiting for transfers between devices, shards(): lax.all_to_all(grad_1, 'tp', split_axis=0, concat_axis=1, tiled=True)  23.5 us
    ppermute x4, starting transfers between devices, from_behind(): return lax.ppermute(block, axis, route)  12.4 us
    all_to_all x1, starting transfers between devices, shards(): lax.all_to_all(grad_1, 'tp', split_axis=0, concat_axis=1, tiled=True)  6.24 us
    all_to_all x3, local copies, waits for them, and re-layouts, to_heads(): lax.all_to_all(block, 'tp', split_axis=block.ndim - 1, concat_axis=block....  6.15 us
  transfers between devices with their start and end apart: 7, of which 6 were waited for; matrix products, arithmetic and copies ran while one was open for 4% of the time, Pallas kernels for 6%

profile of v4, /device:TPU:57, one launch (start us, length us, event | category | flops | bytes accessed | tf_op | source)
XLA Modules:
  0.0 253.7 jit_solution(1074996283304467206)
XLA Ops:
  0.6 0.0 copy-start
  0.6 1.9 fusion
  2.5 0.1 copy-done
  2.6 0.2 pad_maximum_fusion
  2.8 4.5 %copy.25 = bf16[2,128,4608]{1,0,2:T(2,128)(2,1)} copy(bf16[2,128,4608]{2,1,0:T(8,128)(2,1)S(1)} %pad_maximum_fusion) | data formatting | bytes 4718592 | tf_op jit(solution)/shard_map/stack | solution.py:103
  7.3 16.1 %all-to-all-start = ((bf16[2,128,4608]{1,0,2:T(2,128)(2,1)}), bf16[2,128,4608]{1,0,2:T(2,128)(2,1)S(1)}, u32[]{:S(2)}, u32[]{:S(2)}) async-start(bf16[2,128,4608]{1,0,2:T(2,128)(2,1)} %copy.25), calls=%async_computation | async-start | bytes 4718592 | tf_op jit(solution)/shard_map/all_to_all | solution.py:93
  23.5 1.4 copy.32
  24.9 2.9 %collective-permute-start.1 = (bf16[128,4608]{0,1:T(8,128)(2,1)}, bf16[128,4608]{0,1:T(8,128)(2,1)}, u32[]{:S(2)}, u32[]{:S(2)}) collective-permute-start(bf16[128,4608]{0,1:T(8,128)(2,1)} %bitcast.22), channel_id=1, source_target_pairs={{12,0},{24,12},{36,24},{48,36},{60,48},{72,60},{84,72},{96,84},{10... | collective-permute-start | bytes 3538952 | tf_op jit(solution)/shard_map/ppermute | solution.py:14
  27.7 0.7 constant_dynamic-slice_fusion
  28.4 0.0 copy-start.1
  28.4 0.0 copy-start.2
  28.5 2.4 collective-permute-start
  30.9 63.1 %all-to-all-done = bf16[2,128,4608]{1,0,2:T(2,128)(2,1)S(1)} async-done(((bf16[2,128,4608]{1,0,2:T(2,128)(2,1)}), bf16[2,128,4608]{1,0,2:T(2,128)(2,1)S(1)}, u32[]{:S(2)}, u32[]{:S(2)}) %all-to-all-start) | async-done | bytes 2359328 | tf_op jit(solution)/shard_map/all_to_all | solution.py:93
  94.0 1.7 copy.26
  95.8 0.0 copy-done.1
  95.8 0.0 copy-done.2
  95.8 3.0 %copy.27 = bf16[2,12,128,384]{3,2,1,0:T(8,128)(2,1)S(1)} copy(bf16[2,12,128,384]{2,3,1,0:T(8,128)(2,1)} %bitcast.19) | data formatting | bytes 4718592 | tf_op jit(solution)/shard_map/all_to_all | solution.py:93
  98.8 6.4 %collective-permute-done = f32[2,384]{1,0:T(2,128)S(1)} collective-permute-done((f32[2,384]{1,0:T(2,128)S(1)}, f32[2,384]{1,0:T(2,128)S(1)}, u32[]{:S(2)}, u32[]{:S(2)}) %collective-permute-start) | collective-permute-done | bytes 3104 | tf_op jit(solution)/shard_map/ppermute | solution.py:14
  105.2 0.0 collective-permute-done.1
  105.2 9.1 %all-to-all-start.1 = ((bf16[128,12,384]{0,2,1:T(8,128)(2,1)}), bf16[128,12,384]{0,2,1:T(8,128)(2,1)S(1)}, u32[]{:S(2)}, u32[]{:S(2)}) async-start(bf16[128,12,384]{0,2,1:T(8,128)(2,1)} %bitcast.5), calls=%async_computation.1 | async-start | bytes 2359296 | tf_op jit(solution)/shard_map/all_to_all | solution.py:93
  114.3 1.6 slice_bitcast_fusion
  115.9 16.4 %shard_map.67 = (bf16[1536,384]{1,0:T(8,128)(2,1)}, f32[1,384]{1,0:T(1,128)}, f32[1,384]{1,0:T(1,128)}) custom-call(bf16[1536,384]{1,0:T(8,128)(2,1)} %get-tuple-element.31.x_ref, bf16[1536,384]{1,0:T(8,128)(2,1)} %get-tuple-element.30.u_ref, f32[1,384]{1,0:T(1,128)} %copy-done.2, f32[1,384]{1,0:T(1,128)} %copy-done.1), custom_call_target="tpu_custom_call" | custom-call | flops 1509949440 | bytes 3538944 | tf_op jit(solution)/shard_map/pallas_call | solution.py:72
  132.3 1.9 collective-permute-start.2
  134.2 0.6 fusion.1
  134.8 21.9 %all-to-all-done.1 = bf16[128,12,384]{0,2,1:T(8,128)(2,1)S(1)} async-done(((bf16[128,12,384]{0,2,1:T(8,128)(2,1)}), bf16[128,12,384]{0,2,1:T(8,128)(2,1)S(1)}, u32[]{:S(2)}, u32[]{:S(2)}) %all-to-all-start.1) | async-done | bytes 1179680 | tf_op jit(solution)/shard_map/all_to_all | solution.py:93
  156.7 1.4 copy.29
  158.1 25.1 %collective-permute-done.2.u_ref = bf16[1536,384]{1,0:T(8,128)(2,1)S(1)} collective-permute-done((bf16[1536,384]{1,0:T(8,128)(2,1)}, bf16[1536,384]{1,0:T(8,128)(2,1)S(1)}, u32[]{:S(2)}, u32[]{:S(2)}) %collective-permute-start.2) | collective-permute-done | bytes 1179680 | tf_op jit(solution)/shard_map/ppermute | solution.py:14
  183.2 0.0 copy-start.7
  183.2 1.0 copy-done.7
  184.2 16.4 %shard_map.68 = (bf16[1536,384]{1,0:T(8,128)(2,1)}, f32[1,384]{1,0:T(1,128)}, f32[1,384]{1,0:T(1,128)}) custom-call(bf16[1536,384]{1,0:T(8,128)(2,1)} %bitcast.23, bf16[1536,384]{1,0:T(8,128)(2,1)} %copy-done.7, f32[1,384]{1,0:T(1,128)} %get-tuple-element.37.gq_ref, f32[1,384]{1,0:T(1,128)} %get-tuple-element.36.gv_ref), custom_call_target="tpu_custom_call" | custom-call | flops 1509949440 | bytes 3538944 | tf_op jit(solution)/shard_map/pallas_call | solution.py:72
  200.6 2.4 copy.30
  202.9 0.0 copy-start.5
  203.0 0.0 copy-start.6
  203.0 0.0 copy-start.3
  203.0 0.0 copy-start.4
  203.0 6.2 %all-to-all-start.2 = ((bf16[12,128,384]{1,2,0:T(8,128)(2,1)}), bf16[12,128,384]{1,2,0:T(8,128)(2,1)S(1)}, u32[]{:S(2)}, u32[]{:S(2)}) async-start(bf16[12,128,384]{1,2,0:T(8,128)(2,1)} %copy.30), calls=%async_computation.2 | async-start | bytes 2359296 | tf_op jit(solution)/shard_map/all_to_all | solution.py:111
  209.2 0.0 copy-done.5
  209.2 0.0 copy-done.6
  209.2 5.2 %collective-permute-start.3 = (f32[2,384]{1,0:T(2,128)S(1)}, f32[2,384]{1,0:T(2,128)S(1)}, u32[]{:S(2)}, u32[]{:S(2)}) collective-permute-start(f32[2,384]{1,0:T(2,128)S(1)} %pad_maximum_fusion.2), channel_id=1, source_target_pairs={{756,0},{0,12},{12,24},{24,36},{36,48},{48,60},{60,72},{72,84},{84... | collective-permute-start | bytes 9224 | tf_op jit(solution)/shard_map/ppermute | solution.py:14
  214.5 13.8 %collective-permute-done.3 = f32[2,384]{1,0:T(2,128)S(1)} collective-permute-done((f32[2,384]{1,0:T(2,128)S(1)}, f32[2,384]{1,0:T(2,128)S(1)}, u32[]{:S(2)}, u32[]{:S(2)}) %collective-permute-start.3) | collective-permute-done | bytes 3104 | tf_op jit(solution)/shard_map/ppermute | solution.py:14
  228.2 0.0 copy-done.3
  228.2 0.0 copy-done.4
  228.2 0.6 slice_add_fusion
  228.8 23.5 %all-to-all-done.2 = bf16[12,128,384]{1,2,0:T(8,128)(2,1)S(1)} async-done(((bf16[12,128,384]{1,2,0:T(8,128)(2,1)}), bf16[12,128,384]{1,2,0:T(8,128)(2,1)S(1)}, u32[]{:S(2)}, u32[]{:S(2)}) %all-to-all-start.2) | async-done | bytes 1179680 | tf_op jit(solution)/shard_map/all_to_all | solution.py:111
  252.3 1.4 copy.31
  (2 shorter events, 0.0 us)
Async XLA Ops:
  0.6 2.0 copy-start
  7.3 86.7 %all-to-all-start = ((bf16[2,128,4608]{1,0,2:T(2,128)(2,1)}), bf16[2,128,4608]{1,0,2:T(2,128)(2,1)S(1)}, u32[]{:S(2)}, u32[]{:S(2)}) async-start(bf16[2,128,4608]{1,0,2:T(2,128)(2,1)} %copy.25), calls=%async_computation | async-start | bytes 4718592 | tf_op jit(solution)/shard_map/all_to_all | solution.py:93
  24.9 80.3 %collective-permute-start.1 = (bf16[128,4608]{0,1:T(8,128)(2,1)}, bf16[128,4608]{0,1:T(8,128)(2,1)}, u32[]{:S(2)}, u32[]{:S(2)}) collective-permute-start(bf16[128,4608]{0,1:T(8,128)(2,1)} %bitcast.22), channel_id=1, source_target_pairs={{12,0},{24,12},{36,24},{48,36},{60,48},{72,60},{84,72},{96,84},{10... | collective-permute-start | bytes 3538952 | tf_op jit(solution)/shard_map/ppermute | solution.py:14
  28.4 67.3 %copy-start.1 = (f32[1,384]{1,0:T(1,128)}, f32[1,384]{1,0:T(1,128)S(1)}, u32[]{:S(2)}) copy-start(f32[1,384]{1,0:T(1,128)S(1)} %get-tuple-element.38.gv_ref) | copy-start | bytes 4612
  28.4 67.3 %copy-start.2 = (f32[1,384]{1,0:T(1,128)}, f32[1,384]{1,0:T(1,128)S(1)}, u32[]{:S(2)}) copy-start(f32[1,384]{1,0:T(1,128)S(1)} %get-tuple-element.39.gq_ref) | copy-start | bytes 4612
  28.5 76.7 %collective-permute-start = (f32[2,384]{1,0:T(2,128)S(1)}, f32[2,384]{1,0:T(2,128)S(1)}, u32[]{:S(2)}, u32[]{:S(2)}) collective-permute-start(f32[2,384]{1,0:T(2,128)S(1)} %pad_maximum_fusion.1), channel_id=1, source_target_pairs={{12,0},{24,12},{36,24},{48,36},{60,48},{72,60},{84,72},{96,84},{10... | collective-permute-start | bytes 9224 | tf_op jit(solution)/shard_map/ppermute | solution.py:14
  105.2 51.5 %all-to-all-start.1 = ((bf16[128,12,384]{0,2,1:T(8,128)(2,1)}), bf16[128,12,384]{0,2,1:T(8,128)(2,1)S(1)}, u32[]{:S(2)}, u32[]{:S(2)}) async-start(bf16[128,12,384]{0,2,1:T(8,128)(2,1)} %bitcast.5), calls=%async_computation.1 | async-start | bytes 2359296 | tf_op jit(solution)/shard_map/all_to_all | solution.py:93
  132.3 50.8 %collective-permute-start.2 = (bf16[1536,384]{1,0:T(8,128)(2,1)}, bf16[1536,384]{1,0:T(8,128)(2,1)S(1)}, u32[]{:S(2)}, u32[]{:S(2)}) collective-permute-start(bf16[1536,384]{1,0:T(8,128)(2,1)} %get-tuple-element.14), channel_id=1, source_target_pairs={{24,0},{36,12},{48,24},{60,36},{72,48},{84,60},{96,72},{108,84},{1... | collective-permute-start | bytes 3538952 | tf_op jit(solution)/shard_map/ppermute | solution.py:14
  183.2 1.0 copy-start.7
  202.9 6.3 %copy-start.5 = (f32[1,384]{1,0:T(1,128)S(1)}, f32[1,384]{1,0:T(1,128)}, u32[]{:S(2)}) copy-start(f32[1,384]{1,0:T(1,128)} %get-tuple-element.18) | copy-start | bytes 4612
  203.0 6.3 %copy-start.6 = (f32[1,384]{1,0:T(1,128)S(1)}, f32[1,384]{1,0:T(1,128)}, u32[]{:S(2)}) copy-start(f32[1,384]{1,0:T(1,128)} %get-tuple-element.19) | copy-start | bytes 4612
  203.0 25.3 %copy-start.3 = (f32[1,384]{1,0:T(1,128)S(1)}, f32[1,384]{1,0:T(1,128)}, u32[]{:S(2)}) copy-start(f32[1,384]{1,0:T(1,128)} %get-tuple-element.17) | copy-start | bytes 4612
  203.0 25.3 %copy-start.4 = (f32[1,384]{1,0:T(1,128)S(1)}, f32[1,384]{1,0:T(1,128)}, u32[]{:S(2)}) copy-start(f32[1,384]{1,0:T(1,128)} %get-tuple-element.20) | copy-start | bytes 4612
  203.0 49.3 %all-to-all-start.2 = ((bf16[12,128,384]{1,2,0:T(8,128)(2,1)}), bf16[12,128,384]{1,2,0:T(8,128)(2,1)S(1)}, u32[]{:S(2)}, u32[]{:S(2)}) async-start(bf16[12,128,384]{1,2,0:T(8,128)(2,1)} %copy.30), calls=%async_computation.2 | async-start | bytes 2359296 | tf_op jit(solution)/shard_map/all_to_all | solution.py:111
  209.2 19.0 %collective-permute-start.3 = (f32[2,384]{1,0:T(2,128)S(1)}, f32[2,384]{1,0:T(2,128)S(1)}, u32[]{:S(2)}, u32[]{:S(2)}) collective-permute-start(f32[2,384]{1,0:T(2,128)S(1)} %pad_maximum_fusion.2), channel_id=1, source_target_pairs={{756,0},{0,12},{12,24},{24,36},{36,48},{48,60},{60,72},{72,84},{84... | collective-permute-start | bytes 9224 | tf_op jit(solution)/shard_map/ppermute | solution.py:14

commit v5 on v2

--- a/solution.py
+++ b/solution.py
@@ -21,12 +21,12 @@
 def attention_kernel(x_ref, u_ref, gq_ref, gv_ref, g_ref, qs_ref, vs_ref):
     n = pl.program_id(1)
     scale = HEAD_DIM ** (-0.5)
-    wide = x_ref[...].astype(jnp.float32)
+    wide = x_ref[...].reshape(SEQ_LEN, HEAD_DIM).astype(jnp.float32)
     gq = gq_ref[...]
     gv = gv_ref[...]
     keys = (wide * gq).astype(jnp.bfloat16)
     values = (wide * gv).astype(jnp.bfloat16)
-    up = u_ref[...]
+    up = u_ref[...].reshape(SEQ_LEN, HEAD_DIM)
     nt = (((1,), (1,)), ((), ()))
     tn = (((0,), (0,)), ((), ()))
     scores = lax.dot_general(keys, keys, nt, preferred_element_type=jnp.float32) * scale
@@ -44,7 +44,8 @@
     key_grad = lax.dot_general(score_low, keys, tn, preferred_element_type=jnp.float32) * scale
     value_grad = lax.dot_general(probs_low, up, tn, preferred_element_type=jnp.float32)
     qk_total = query_grad + key_grad
-    g_ref[...] = (up.astype(jnp.float32) + qk_total * gq + value_grad * gv).astype(jnp.bfloat16)
+    grad_in = (up.astype(jnp.float32) + qk_total * gq + value_grad * gv).astype(jnp.bfloat16)
+    g_ref[...] = grad_in.reshape(g_ref.shape)
     qk_part = jnp.sum(wide * qk_total, axis=0, keepdims=True)
     value_part = jnp.sum(wide * value_grad, axis=0, keepdims=True)
 
@@ -62,27 +63,33 @@
 INTERPRET = False
 
 
-def local_backward(inputs, upstream, gain_qk, gain_value):
-    rows, width = inputs.shape
+def tile_of(array, slot):
+    half = array.shape[-2]
+    if slot is None:
+        return pl.BlockSpec((2, half, HEAD_DIM), lambda h, n: (n, 0, h))
+    return pl.BlockSpec((2, None, half, HEAD_DIM), lambda h, n: (n, slot, 0, h))
+
+
+def local_backward(inputs, inputs_slot, upstream, upstream_slot, gain_qk, gain_value):
+    blocks, half, width = upstream.shape[0], upstream.shape[-2], upstream.shape[-1]
     heads = width // HEAD_DIM
-    count = rows // SEQ_LEN
-    tile = pl.BlockSpec((SEQ_LEN, HEAD_DIM), lambda h, n: (n, h))
+    count = blocks * half // SEQ_LEN
     gain = pl.BlockSpec((1, HEAD_DIM), lambda h, n: (0, h))
     flops = heads * count * 5 * 2 * SEQ_LEN * SEQ_LEN * HEAD_DIM
     grad_in, qk_part, value_part = pl.pallas_call(
         attention_kernel,
         grid=(heads, count),
-        in_specs=[tile, tile, gain, gain],
-        out_specs=[tile, gain, gain],
+        in_specs=[tile_of(inputs, inputs_slot), tile_of(upstream, upstream_slot), gain, gain],
+        out_specs=[tile_of(upstream, None), gain, gain],
         out_shape=[
-            jax.ShapeDtypeStruct((rows, width), jnp.bfloat16),
+            jax.ShapeDtypeStruct((blocks, half, width), jnp.bfloat16),
             jax.ShapeDtypeStruct((1, width), jnp.float32),
             jax.ShapeDtypeStruct((1, width), jnp.float32),
         ],
         cost_estimate=pl.CostEstimate(
             flops=flops,
             transcendentals=heads * count * SEQ_LEN * SEQ_LEN,
-            bytes_accessed=3 * rows * width * 2,
+            bytes_accessed=3 * blocks * half * width * 2,
         ),
         interpret=INTERPRET,
     )(inputs, upstream, gain_qk[None], gain_value[None])
@@ -90,7 +97,16 @@
 
 
 def to_heads(block):
-    return lax.all_to_all(block, "tp", split_axis=block.ndim - 1, concat_axis=block.ndim - 2, tiled=True)
+    parts = lax.axis_size("tp")
+    lead = block.shape[:-2]
+    split = block.reshape(lead + (block.shape[-2], parts, block.shape[-1] // parts))
+    order = (len(lead) + 1,) + tuple(range(len(lead))) + (len(lead), len(lead) + 2)
+    return lax.all_to_all(jnp.transpose(split, order), "tp", 0, 0, tiled=True)
+
+
+def to_tokens(block):
+    back = lax.all_to_all(block, "tp", 0, 0, tiled=True)
+    return jnp.transpose(back, (1, 0, 2)).reshape(block.shape[1], -1)
 
 
 def shards(saved_inputs, incoming, qk_gain, value_gain):
@@ -100,21 +116,17 @@
     gain_qk = lax.dynamic_slice_in_dim(qk_gain[0], offset, local_width)
     gain_value = lax.dynamic_slice_in_dim(value_gain[0], offset, local_width)
     first = to_heads(jnp.stack([saved_inputs[0, 0], incoming[0]]))
-    inputs_heads = [first[0]]
+    grad_in, qk_sum, value_sum = local_backward(first, 0, first, 1, gain_qk, gain_value)
     for t in range(1, tick_count):
         first, later = lax.optimization_barrier((first, saved_inputs[t, 0]))
-        inputs_heads.append(to_heads(later))
-    upstream = first[1]
-    qk_sum = jnp.zeros((local_width,), jnp.float32)
-    value_sum = jnp.zeros((local_width,), jnp.float32)
-    for tick_index in range(tick_count):
+        inputs_heads = to_heads(later)
+        upstream = pass_on(grad_in)
         grad_in, qk_part, value_part = local_backward(
-            inputs_heads[tick_index], upstream, gain_qk, gain_value
+            inputs_heads, None, upstream, None, gain_qk, gain_value
         )
         qk_sum = qk_sum + qk_part
         value_sum = value_sum + value_part
-        upstream = pass_on(grad_in)
-    passed = lax.all_to_all(upstream, "tp", split_axis=0, concat_axis=1, tiled=True)
+    passed = to_tokens(pass_on(grad_in))
     return (passed[None], qk_sum[None], value_sum[None])
 
 

time: 246 us -> 253 us (1.028)
  the two profiles are of different devices: /device:TPU:64 before, /device:TPU:57 now
where the time goes in v5:
time: 253 us; the launch traced here: 250 us
  waiting for transfers between devices  156 us (62%)
  starting transfers between devices  40.3 us (16%)
  Pallas kernels  32.8 us (13%)
  local copies, waits for them, and re-layouts  16 us (6%)
  other arithmetic  4.07 us (2%)
    all_to_all x2, waiting for transfers between devices, to_heads(): return lax.all_to_all(jnp.transpose(split, order), 'tp', 0, 0, tiled=True)  69.9 us
    ppermute x2, waiting for transfers between devices, from_behind(): return lax.ppermute(block, axis, route)  63.5 us
    pallas_call x2, Pallas kernels, local_backward(): pl.pallas_call(attention_kernel, grid=(heads, count), in_specs=[tile_of(i...  32.8 us
    all_to_all x2, starting transfers between devices, to_heads(): return lax.all_to_all(jnp.transpose(split, order), 'tp', 0, 0, tiled=True)  29.6 us
    all_to_all x1, waiting for transfers between devices, to_tokens(): back = lax.all_to_all(block, 'tp', 0, 0, tiled=True)  22.8 us
    unnamed x16, local copies, waits for them, and re-layouts  7.59 us
    ppermute x2, starting transfers between devices, from_behind(): return lax.ppermute(block, axis, route)  5.67 us
  transfers between devices with their start and end apart: 5, of which 4 were waited for; matrix products, arithmetic and copies ran while one was open for 1% of the time, Pallas kernels for 7%

profile of v5, /device:TPU:57, one launch (start us, length us, event | category | flops | bytes accessed | tf_op | source)
XLA Modules:
  0.0 250.2 jit_solution(17941450559158535501)
XLA Ops:
  0.6 1.7 copy.8
  2.3 0.7 copy.10
  3.1 2.8 %fusion = (bf16[1,1,128,4608]{3,2,1,0:T(8,128)(2,1)S(1)}, bf16[1,1,128,4608]{3,2,1,0:T(8,128)(2,1)}) fusion(bf16[2,1,128,4608]{3,2,1,0:T(8,128)(2,1)} %param.4), kind=kLoop, calls=%fused_computation.3 | loop fusion | bytes 4718592 | tf_op jit(solution)/shard_map/slice | solution.py:121
  5.9 1.7 copy.15
  7.6 1.4 copy.9
  9.0 2.9 %maximum_bitcast_fusion = bf16[12,2,128,384]{3,2,1,0:T(8,128)(2,1)} fusion(bf16[1,128,12,384]{3,1,0,2:T(8,128)(2,1)S(1)} %copy.10, bf16[1,128,12,384]{3,1,0,2:T(8,128)(2,1)} %copy.9), kind=kLoop, calls=%fused_computation | loop fusion | flops 1179648 | bytes 4718592 | tf_op jit(solution)/shard_map/transpose | solution.py:104
  11.9 16.2 %all-to-all-start = ((bf16[12,2,128,384]{3,2,1,0:T(8,128)(2,1)}), bf16[12,2,128,384]{3,2,1,0:T(8,128)(2,1)}, u32[]{:S(2)}, u32[]{:S(2)}) async-start(bf16[12,2,128,384]{3,2,1,0:T(8,128)(2,1)} %maximum_bitcast_fusion), calls=%async_computation | async-start | bytes 4718592 | tf_op jit(solution)/shard_map/all_to_all | solution.py:104
  28.1 0.7 copy.16
  28.8 69.9 %all-to-all-done.x_ref.u_ref = bf16[12,2,128,384]{3,2,1,0:T(8,128)(2,1)} async-done(((bf16[12,2,128,384]{3,2,1,0:T(8,128)(2,1)}), bf16[12,2,128,384]{3,2,1,0:T(8,128)(2,1)}, u32[]{:S(2)}, u32[]{:S(2)}) %all-to-all-start) | async-done | bytes 2359328 | tf_op jit(solution)/shard_map/all_to_all | solution.py:104
  98.7 1.4 copy.12
  100.1 13.5 %all-to-all-start.1 = ((bf16[12,128,384]{2,1,0:T(8,128)(2,1)}), bf16[12,128,384]{2,1,0:T(8,128)(2,1)S(1)}, u32[]{:S(2)}, u32[]{:S(2)}) async-start(bf16[12,128,384]{2,1,0:T(8,128)(2,1)} %bitcast.5), calls=%async_computation.1 | async-start | bytes 2359296 | tf_op jit(solution)/shard_map/all_to_all | solution.py:104
  113.7 1.3 constant_dynamic-slice_fusion
  114.9 16.4 %shard_map.67 = (bf16[12,128,384]{2,1,0:T(8,128)(2,1)}, f32[1,384]{1,0:T(1,128)}, f32[1,384]{1,0:T(1,128)}) custom-call(bf16[12,2,128,384]{3,2,1,0:T(8,128)(2,1)} %all-to-all-done.x_ref.u_ref, bf16[12,2,128,384]{3,2,1,0:T(8,128)(2,1)} %all-to-all-done.x_ref.u_ref, f32[1,384]{1,0:T(1,128)} %get-tuple-element.23.gq_ref, f32[1,384]{1,0:T(1,128)} %get-tuple-element.22.gv_ref), custom_call_target="tpu_custom_call" | custom-call | flops 1509949440 | bytes 3538944 | tf_op jit(solution)/shard_map/pallas_call | solution.py:79
  131.3 3.7 %collective-permute-start = (bf16[12,128,384]{2,1,0:T(8,128)(2,1)}, bf16[12,128,384]{2,1,0:T(8,128)(2,1)S(1)}, u32[]{:S(2)}, u32[]{:S(2)}) collective-permute-start(bf16[12,128,384]{2,1,0:T(8,128)(2,1)} %get-tuple-element.11), channel_id=1, source_target_pairs={{12,0},{24,12},{36,24},{48,36},{60,48},{72,60},{84,72},{96,84},{10... | collective-permute-start | bytes 3538952 | tf_op jit(solution)/shard_map/ppermute | solution.py:14
  135.1 28.4 %collective-permute-done.u_ref = bf16[12,128,384]{2,1,0:T(8,128)(2,1)S(1)} collective-permute-done((bf16[12,128,384]{2,1,0:T(8,128)(2,1)}, bf16[12,128,384]{2,1,0:T(8,128)(2,1)S(1)}, u32[]{:S(2)}, u32[]{:S(2)}) %collective-permute-start) | collective-permute-done | bytes 1179680 | tf_op jit(solution)/shard_map/ppermute | solution.py:14
  163.5 0.0 copy-start.5
  163.5 0.0 all-to-all-done.1.x_ref
  163.5 1.0 copy-done.5
  164.6 0.0 copy-start
  164.6 1.0 copy-done
  165.6 16.4 %shard_map.68 = (bf16[12,128,384]{2,1,0:T(8,128)(2,1)}, f32[1,384]{1,0:T(1,128)}, f32[1,384]{1,0:T(1,128)}) custom-call(bf16[12,128,384]{2,1,0:T(8,128)(2,1)} %copy-done, bf16[12,128,384]{2,1,0:T(8,128)(2,1)} %copy-done.5, f32[1,384]{1,0:T(1,128)} %get-tuple-element.23.gq_ref, f32[1,384]{1,0:T(1,128)} %get-tuple-element.22.gv_ref), custom_call_target="tpu_custom_call" | custom-call | flops 1509949440 | bytes 3538944 | tf_op jit(solution)/shard_map/pallas_call | solution.py:79
  182.0 0.0 copy-start.2
  182.0 0.0 copy-start.4
  182.0 0.0 copy-start.1
  182.0 0.0 copy-start.3
  182.0 1.9 collective-permute-start.1
  184.0 35.1 %collective-permute-done.1 = bf16[12,128,384]{2,1,0:T(8,128)(2,1)} collective-permute-done((bf16[12,128,384]{2,1,0:T(8,128)(2,1)}, bf16[12,128,384]{2,1,0:T(8,128)(2,1)}, u32[]{:S(2)}, u32[]{:S(2)}) %collective-permute-start.1) | collective-permute-done | bytes 1179680 | tf_op jit(solution)/shard_map/ppermute | solution.py:14
  219.0 5.0 %all-to-all-start.2 = ((bf16[12,128,384]{2,1,0:T(8,128)(2,1)}), bf16[12,128,384]{2,1,0:T(8,128)(2,1)S(1)}, u32[]{:S(2)}, u32[]{:S(2)}) async-start(bf16[12,128,384]{2,1,0:T(8,128)(2,1)} %collective-permute-done.1), calls=%async_computation.2 | async-start | bytes 2359296 | tf_op jit(solution)/shard_map/all_to_all | solution.py:108
  224.0 0.0 copy-done.2
  224.0 0.0 copy-done.4
  224.0 0.6 add.13
  224.6 0.0 copy-done.1
  224.6 0.0 copy-done.3
  224.6 0.6 add.14
  225.2 22.8 %all-to-all-done.2 = bf16[12,128,384]{2,1,0:T(8,128)(2,1)S(1)} async-done(((bf16[12,128,384]{2,1,0:T(8,128)(2,1)}), bf16[12,128,384]{2,1,0:T(8,128)(2,1)S(1)}, u32[]{:S(2)}, u32[]{:S(2)}) %all-to-all-start.2) | async-done | bytes 1179680 | tf_op jit(solution)/shard_map/all_to_all | solution.py:108
  248.0 0.8 copy.13
  248.8 1.4 copy.14
Async XLA Ops:
  11.9 86.8 %all-to-all-start = ((bf16[12,2,128,384]{3,2,1,0:T(8,128)(2,1)}), bf16[12,2,128,384]{3,2,1,0:T(8,128)(2,1)}, u32[]{:S(2)}, u32[]{:S(2)}) async-start(bf16[12,2,128,384]{3,2,1,0:T(8,128)(2,1)} %maximum_bitcast_fusion), calls=%async_computation | async-start | bytes 4718592 | tf_op jit(solution)/shard_map/all_to_all | solution.py:104
  100.1 63.4 %all-to-all-start.1 = ((bf16[12,128,384]{2,1,0:T(8,128)(2,1)}), bf16[12,128,384]{2,1,0:T(8,128)(2,1)S(1)}, u32[]{:S(2)}, u32[]{:S(2)}) async-start(bf16[12,128,384]{2,1,0:T(8,128)(2,1)} %bitcast.5), calls=%async_computation.1 | async-start | bytes 2359296 | tf_op jit(solution)/shard_map/all_to_all | solution.py:104
  131.3 32.2 %collective-permute-start = (bf16[12,128,384]{2,1,0:T(8,128)(2,1)}, bf16[12,128,384]{2,1,0:T(8,128)(2,1)S(1)}, u32[]{:S(2)}, u32[]{:S(2)}) collective-permute-start(bf16[12,128,384]{2,1,0:T(8,128)(2,1)} %get-tuple-element.11), channel_id=1, source_target_pairs={{12,0},{24,12},{36,24},{48,36},{60,48},{72,60},{84,72},{96,84},{10... | collective-permute-start | bytes 3538952 | tf_op jit(solution)/shard_map/ppermute | solution.py:14
  163.5 1.0 copy-start.5
  164.6 1.0 copy-start
  182.0 42.0 %copy-start.2 = (f32[1,384]{1,0:T(1,128)S(1)}, f32[1,384]{1,0:T(1,128)}, u32[]{:S(2)}) copy-start(f32[1,384]{1,0:T(1,128)} %get-tuple-element.13) | copy-start | bytes 4612
  182.0 42.0 %copy-start.4 = (f32[1,384]{1,0:T(1,128)S(1)}, f32[1,384]{1,0:T(1,128)}, u32[]{:S(2)}) copy-start(f32[1,384]{1,0:T(1,128)} %get-tuple-element.14) | copy-start | bytes 4612
  182.0 42.6 %copy-start.1 = (f32[1,384]{1,0:T(1,128)S(1)}, f32[1,384]{1,0:T(1,128)}, u32[]{:S(2)}) copy-start(f32[1,384]{1,0:T(1,128)} %get-tuple-element.15) | copy-start | bytes 4612
  182.0 42.6 %copy-start.3 = (f32[1,384]{1,0:T(1,128)S(1)}, f32[1,384]{1,0:T(1,128)}, u32[]{:S(2)}) copy-start(f32[1,384]{1,0:T(1,128)} %get-tuple-element.16) | copy-start | bytes 4612
  182.0 37.0 %collective-permute-start.1 = (bf16[12,128,384]{2,1,0:T(8,128)(2,1)}, bf16[12,128,384]{2,1,0:T(8,128)(2,1)}, u32[]{:S(2)}, u32[]{:S(2)}) collective-permute-start(bf16[12,128,384]{2,1,0:T(8,128)(2,1)} %get-tuple-element.12), channel_id=1, source_target_pairs={{12,0},{24,12},{36,24},{48,36},{60,48},{72,60},{84,72},{96,84},{10... | collective-permute-start | bytes 3538952 | tf_op jit(solution)/shard_map/ppermute | solution.py:14
  219.0 29.0 %all-to-all-start.2 = ((bf16[12,128,384]{2,1,0:T(8,128)(2,1)}), bf16[12,128,384]{2,1,0:T(8,128)(2,1)S(1)}, u32[]{:S(2)}, u32[]{:S(2)}) async-start(bf16[12,128,384]{2,1,0:T(8,128)(2,1)} %collective-permute-done.1), calls=%async_computation.2 | async-start | bytes 2359296 | tf_op jit(solution)/shard_map/all_to_all | solution.py:108

commit v6 on v5

--- a/solution.py
+++ b/solution.py
@@ -96,12 +96,40 @@
     return grad_in, qk_part[0], value_part[0]
 
 
+def split_kernel(a_ref, b_ref, c_ref, first_ref, later_ref):
+    first_ref[0, 0] = a_ref[...]
+    first_ref[0, 1] = b_ref[...]
+    later_ref[0] = c_ref[...]
+
+
+def split_blocks(saved_inputs, incoming):
+    parts = lax.axis_size("tp")
+    ticks, _, rows, width = saved_inputs.shape
+    cut = width // parts
+    stacked = saved_inputs.reshape(ticks, rows, width)
+    grad = incoming.reshape(rows, width)
+    return pl.pallas_call(
+        split_kernel,
+        grid=(parts,),
+        in_specs=[
+            pl.BlockSpec((None, rows, cut), lambda j: (0, 0, j)),
+            pl.BlockSpec((rows, cut), lambda j: (0, j)),
+            pl.BlockSpec((None, rows, cut), lambda j: (1, 0, j)),
+        ],
+        out_specs=[
+            pl.BlockSpec((1, 2, rows, cut), lambda j: (j, 0, 0, 0)),
+            pl.BlockSpec((1, rows, cut), lambda j: (j, 0, 0)),
+        ],
+        out_shape=[
+            jax.ShapeDtypeStruct((parts, 2, rows, cut), saved_inputs.dtype),
+            jax.ShapeDtypeStruct((parts, rows, cut), saved_inputs.dtype),
+        ],
+        interpret=INTERPRET,
+    )(stacked, grad, stacked)
+
+
 def to_heads(block):
-    parts = lax.axis_size("tp")
-    lead = block.shape[:-2]
-    split = block.reshape(lead + (block.shape[-2], parts, block.shape[-1] // parts))
-    order = (len(lead) + 1,) + tuple(range(len(lead))) + (len(lead), len(lead) + 2)
-    return lax.all_to_all(jnp.transpose(split, order), "tp", 0, 0, tiled=True)
+    return lax.all_to_all(block, "tp", 0, 0, tiled=True)
 
 
 def to_tokens(block):
@@ -115,10 +143,11 @@
     offset = lax.axis_index("tp") * local_width
     gain_qk = lax.dynamic_slice_in_dim(qk_gain[0], offset, local_width)
     gain_value = lax.dynamic_slice_in_dim(value_gain[0], offset, local_width)
-    first = to_heads(jnp.stack([saved_inputs[0, 0], incoming[0]]))
+    first, later = split_blocks(saved_inputs, incoming)
+    first = to_heads(first)
     grad_in, qk_sum, value_sum = local_backward(first, 0, first, 1, gain_qk, gain_value)
     for t in range(1, tick_count):
-        first, later = lax.optimization_barrier((first, saved_inputs[t, 0]))
+        first, later = lax.optimization_barrier((first, later))
         inputs_heads = to_heads(later)
         upstream = pass_on(grad_in)
         grad_in, qk_part, value_part = local_backward(

time: 253 us -> 233 us (0.921)
  the two profiles are of different devices: /device:TPU:57 before, /device:TPU:6 now
where the time goes in v6:
time: 233 us; the launch traced here: 230 us
  blocking collectives  83.5 us (36%)
  waiting for transfers between devices  63.4 us (27%)
  Pallas kernels  41.1 us (18%)
  starting transfers between devices  35 us (15%)
  local copies, waits for them, and re-layouts  5.5 us (2%)
    all_to_all x1, blocking collectives, to_heads(): return lax.all_to_all(block, 'tp', 0, 0, tiled=True)  83.5 us
    pallas_call x2, Pallas kernels, local_backward(): pl.pallas_call(attention_kernel, grid=(heads, count), in_specs=[tile_of(i...  32.8 us
    ppermute x2, waiting for transfers between devices, from_behind(): return lax.ppermute(block, axis, route)  31.7 us
    all_to_all x1, waiting for transfers between devices, to_tokens(): back = lax.all_to_all(block, 'tp', 0, 0, tiled=True)  31.7 us
    ppermute x2, starting transfers between devices, from_behind(): return lax.ppermute(block, axis, route)  16.4 us
    all_to_all x1, starting transfers between devices, to_heads(): return lax.all_to_all(block, 'tp', 0, 0, tiled=True)  12.5 us
    pallas_call x1, Pallas kernels, split_blocks(): pl.pallas_call(split_kernel, grid=(parts,), in_specs=[pl.BlockSpec((None,...  8.28 us
    all_to_all x1, starting transfers between devices, to_tokens(): back = lax.all_to_all(block, 'tp', 0, 0, tiled=True)  6.13 us
  transfers between devices with their start and end apart: 4, of which 3 were waited for; matrix products, arithmetic and copies ran while one was open for 1% of the time, Pallas kernels for 7%

profile of v6, /device:TPU:6, one launch (start us, length us, event | category | flops | bytes accessed | tf_op | source)
XLA Modules:
  0.0 230.4 jit_solution(17417169538732552734)
XLA Ops:
  0.6 8.3 %shard_map.67 = (bf16[12,2,128,384]{3,2,1,0:T(8,128)(2,1)}, bf16[12,128,384]{2,1,0:T(8,128)(2,1)}) custom-call(bf16[2,128,4608]{2,1,0:T(8,128)(2,1)} %bitcast.4, bf16[128,4608]{1,0:T(8,128)(2,1)} %bitcast.8, bf16[2,128,4608]{2,1,0:T(8,128)(2,1)} %bitcast.5), custom_call_target="tpu_custom_call" | custom-call | tf_op jit(solution)/shard_map/pallas_call | solution.py:111
  8.9 83.5 %all_to_all.15.x_ref.u_ref = bf16[12,2,128,384]{3,2,1,0:T(8,128)(2,1)} all-to-all(bf16[12,2,128,384]{3,2,1,0:T(8,128)(2,1)} %get-tuple-element.12), channel_id=1, replica_groups=mesh['section'=64,'tp'=12] {'tp'}, dimensions={0} | all-to-all | bytes 4718592 | tf_op jit(solution)/shard_map/all_to_all | solution.py:132
  92.5 12.5 %all-to-all-start.1 = ((bf16[12,128,384]{2,1,0:T(8,128)(2,1)}), bf16[12,128,384]{2,1,0:T(8,128)(2,1)S(1)}, u32[]{:S(2)}, u32[]{:S(2)}) async-start(bf16[12,128,384]{2,1,0:T(8,128)(2,1)} %get-tuple-element.14), calls=%async_computation.1 | async-start | bytes 2359296 | tf_op jit(solution)/shard_map/all_to_all | solution.py:132
  104.9 1.3 constant_dynamic-slice_fusion
  106.2 16.4 %shard_map.68 = (bf16[12,128,384]{2,1,0:T(8,128)(2,1)}, f32[1,384]{1,0:T(1,128)}, f32[1,384]{1,0:T(1,128)}) custom-call(bf16[12,2,128,384]{3,2,1,0:T(8,128)(2,1)} %all_to_all.15.x_ref.u_ref, bf16[12,2,128,384]{3,2,1,0:T(8,128)(2,1)} %all_to_all.15.x_ref.u_ref, f32[1,384]{1,0:T(1,128)} %get-tuple-element.25.gq_ref, f32[1,384]{1,0:T(1,128)} %get-tuple-element.24.gv_ref), custom_call_target="tpu_custom_call" | custom-call | flops 1509949440 | bytes 3538944 | tf_op jit(solution)/shard_map/pallas_call | solution.py:79
  122.6 8.7 %collective-permute-start = (bf16[12,128,384]{2,1,0:T(8,128)(2,1)}, bf16[12,128,384]{2,1,0:T(8,128)(2,1)S(1)}, u32[]{:S(2)}, u32[]{:S(2)}) collective-permute-start(bf16[12,128,384]{2,1,0:T(8,128)(2,1)} %get-tuple-element.15), channel_id=1, source_target_pairs={{12,0},{24,12},{36,24},{48,36},{60,48},{72,60},{84,72},{96,84},{10... | collective-permute-start | bytes 3538952 | tf_op jit(solution)/shard_map/ppermute | solution.py:14
  131.3 16.1 %collective-permute-done.u_ref = bf16[12,128,384]{2,1,0:T(8,128)(2,1)S(1)} collective-permute-done((bf16[12,128,384]{2,1,0:T(8,128)(2,1)}, bf16[12,128,384]{2,1,0:T(8,128)(2,1)S(1)}, u32[]{:S(2)}, u32[]{:S(2)}) %collective-permute-start) | collective-permute-done | bytes 1179680 | tf_op jit(solution)/shard_map/ppermute | solution.py:14
  147.4 0.0 copy-start.5
  147.4 0.0 all-to-all-done.1.x_ref
  147.4 1.0 copy-done.5
  148.4 0.0 copy-start
  148.4 1.0 copy-done
  149.4 16.4 %shard_map.69 = (bf16[12,128,384]{2,1,0:T(8,128)(2,1)}, f32[1,384]{1,0:T(1,128)}, f32[1,384]{1,0:T(1,128)}) custom-call(bf16[12,128,384]{2,1,0:T(8,128)(2,1)} %copy-done, bf16[12,128,384]{2,1,0:T(8,128)(2,1)} %copy-done.5, f32[1,384]{1,0:T(1,128)} %get-tuple-element.25.gq_ref, f32[1,384]{1,0:T(1,128)} %get-tuple-element.24.gv_ref), custom_call_target="tpu_custom_call" | custom-call | flops 1509949440 | bytes 3538944 | tf_op jit(solution)/shard_map/pallas_call | solution.py:79
  165.8 0.0 copy-start.2
  165.8 0.0 copy-start.4
  165.8 0.0 copy-start.1
  165.9 0.0 copy-start.3
  165.9 7.7 %collective-permute-start.1 = (bf16[12,128,384]{2,1,0:T(8,128)(2,1)}, bf16[12,128,384]{2,1,0:T(8,128)(2,1)}, u32[]{:S(2)}, u32[]{:S(2)}) collective-permute-start(bf16[12,128,384]{2,1,0:T(8,128)(2,1)} %get-tuple-element.16), channel_id=1, source_target_pairs={{12,0},{24,12},{36,24},{48,36},{60,48},{72,60},{84,72},{96,84},{10... | collective-permute-start | bytes 3538952 | tf_op jit(solution)/shard_map/ppermute | solution.py:14
  173.6 15.6 %collective-permute-done.1 = bf16[12,128,384]{2,1,0:T(8,128)(2,1)} collective-permute-done((bf16[12,128,384]{2,1,0:T(8,128)(2,1)}, bf16[12,128,384]{2,1,0:T(8,128)(2,1)}, u32[]{:S(2)}, u32[]{:S(2)}) %collective-permute-start.1) | collective-permute-done | bytes 1179680 | tf_op jit(solution)/shard_map/ppermute | solution.py:14
  189.2 6.1 %all-to-all-start.2 = ((bf16[12,128,384]{2,1,0:T(8,128)(2,1)}), bf16[12,128,384]{2,1,0:T(8,128)(2,1)S(1)}, u32[]{:S(2)}, u32[]{:S(2)}) async-start(bf16[12,128,384]{2,1,0:T(8,128)(2,1)} %collective-permute-done.1), calls=%async_computation.2 | async-start | bytes 2359296 | tf_op jit(solution)/shard_map/all_to_all | solution.py:136
  195.4 0.0 copy-done.2
  195.4 0.0 copy-done.4
  195.4 0.6 add.13
  195.9 0.0 copy-done.1
  195.9 0.0 copy-done.3
  195.9 0.6 add.14
  196.5 31.7 %all-to-all-done.2 = bf16[12,128,384]{2,1,0:T(8,128)(2,1)S(1)} async-done(((bf16[12,128,384]{2,1,0:T(8,128)(2,1)}), bf16[12,128,384]{2,1,0:T(8,128)(2,1)S(1)}, u32[]{:S(2)}, u32[]{:S(2)}) %all-to-all-start.2) | async-done | bytes 1179680 | tf_op jit(solution)/shard_map/all_to_all | solution.py:136
  228.2 0.8 copy.7
  229.0 1.4 copy.8
Async XLA Ops:
  92.5 54.9 %all-to-all-start.1 = ((bf16[12,128,384]{2,1,0:T(8,128)(2,1)}), bf16[12,128,384]{2,1,0:T(8,128)(2,1)S(1)}, u32[]{:S(2)}, u32[]{:S(2)}) async-start(bf16[12,128,384]{2,1,0:T(8,128)(2,1)} %get-tuple-element.14), calls=%async_computation.1 | async-start | bytes 2359296 | tf_op jit(solution)/shard_map/all_to_all | solution.py:132
  122.6 24.8 %collective-permute-start = (bf16[12,128,384]{2,1,0:T(8,128)(2,1)}, bf16[12,128,384]{2,1,0:T(8,128)(2,1)S(1)}, u32[]{:S(2)}, u32[]{:S(2)}) collective-permute-start(bf16[12,128,384]{2,1,0:T(8,128)(2,1)} %get-tuple-element.15), channel_id=1, source_target_pairs={{12,0},{24,12},{36,24},{48,36},{60,48},{72,60},{84,72},{96,84},{10... | collective-permute-start | bytes 3538952 | tf_op jit(solution)/shard_map/ppermute | solution.py:14
  147.4 1.0 copy-start.5
  148.4 1.0 copy-start
  165.8 29.5 %copy-start.2 = (f32[1,384]{1,0:T(1,128)S(1)}, f32[1,384]{1,0:T(1,128)}, u32[]{:S(2)}) copy-start(f32[1,384]{1,0:T(1,128)} %get-tuple-element.17) | copy-start | bytes 4612
  165.8 29.5 %copy-start.4 = (f32[1,384]{1,0:T(1,128)S(1)}, f32[1,384]{1,0:T(1,128)}, u32[]{:S(2)}) copy-start(f32[1,384]{1,0:T(1,128)} %get-tuple-element.18) | copy-start | bytes 4612
  165.8 30.1 %copy-start.1 = (f32[1,384]{1,0:T(1,128)S(1)}, f32[1,384]{1,0:T(1,128)}, u32[]{:S(2)}) copy-start(f32[1,384]{1,0:T(1,128)} %get-tuple-element.19) | copy-start | bytes 4612
  165.9 30.1 %copy-start.3 = (f32[1,384]{1,0:T(1,128)S(1)}, f32[1,384]{1,0:T(1,128)}, u32[]{:S(2)}) copy-start(f32[1,384]{1,0:T(1,128)} %get-tuple-element.20) | copy-start | bytes 4612
  165.9 23.4 %collective-permute-start.1 = (bf16[12,128,384]{2,1,0:T(8,128)(2,1)}, bf16[12,128,384]{2,1,0:T(8,128)(2,1)}, u32[]{:S(2)}, u32[]{:S(2)}) collective-permute-start(bf16[12,128,384]{2,1,0:T(8,128)(2,1)} %get-tuple-element.16), channel_id=1, source_target_pairs={{12,0},{24,12},{36,24},{48,36},{60,48},{72,60},{84,72},{96,84},{10... | collective-permute-start | bytes 3538952 | tf_op jit(solution)/shard_map/ppermute | solution.py:14
  189.2 39.0 %all-to-all-start.2 = ((bf16[12,128,384]{2,1,0:T(8,128)(2,1)}), bf16[12,128,384]{2,1,0:T(8,128)(2,1)S(1)}, u32[]{:S(2)}, u32[]{:S(2)}) async-start(bf16[12,128,384]{2,1,0:T(8,128)(2,1)} %collective-permute-done.1), calls=%async_computation.2 | async-start | bytes 2359296 | tf_op jit(solution)/shard_map/all_to_all | solution.py:136

commit v7 on v6

--- a/solution.py
+++ b/solution.py
@@ -3,6 +3,7 @@
 from jax import lax
 from jax.sharding import PartitionSpec as P
 from jax.experimental import pallas as pl
+from jax.experimental.pallas import tpu as pltpu
 
 HEAD_DIM = 128
 SEQ_LEN = 256
@@ -18,15 +19,10 @@
     return from_behind(grad_in, "section", -1)
 
 
-def attention_kernel(x_ref, u_ref, gq_ref, gv_ref, g_ref, qs_ref, vs_ref):
-    n = pl.program_id(1)
+def attend_head(wide, up, gq, gv):
     scale = HEAD_DIM ** (-0.5)
-    wide = x_ref[...].reshape(SEQ_LEN, HEAD_DIM).astype(jnp.float32)
-    gq = gq_ref[...]
-    gv = gv_ref[...]
     keys = (wide * gq).astype(jnp.bfloat16)
     values = (wide * gv).astype(jnp.bfloat16)
-    up = u_ref[...].reshape(SEQ_LEN, HEAD_DIM)
     nt = (((1,), (1,)), ((), ()))
     tn = (((0,), (0,)), ((), ()))
     scores = lax.dot_general(keys, keys, nt, preferred_element_type=jnp.float32) * scale
@@ -45,40 +41,51 @@
     value_grad = lax.dot_general(probs_low, up, tn, preferred_element_type=jnp.float32)
     qk_total = query_grad + key_grad
     grad_in = (up.astype(jnp.float32) + qk_total * gq + value_grad * gv).astype(jnp.bfloat16)
-    g_ref[...] = grad_in.reshape(g_ref.shape)
     qk_part = jnp.sum(wide * qk_total, axis=0, keepdims=True)
     value_part = jnp.sum(wide * value_grad, axis=0, keepdims=True)
+    return grad_in, qk_part, value_part
 
-    @pl.when(n == 0)
-    def _():
-        qs_ref[...] = qk_part
-        vs_ref[...] = value_part
 
-    @pl.when(n > 0)
-    def _():
-        qs_ref[...] += qk_part
-        vs_ref[...] += value_part
+def attention_kernel(x_ref, u_ref, gq_ref, gv_ref, g_ref, qs_ref, vs_ref):
+    n = pl.program_id(0)
+    heads = g_ref.shape[-1] // HEAD_DIM
+    for h in range(heads):
+        cols = slice(h * HEAD_DIM, (h + 1) * HEAD_DIM)
+        wide = x_ref[:, :, cols].reshape(SEQ_LEN, HEAD_DIM).astype(jnp.float32)
+        up = u_ref[:, :, cols].reshape(SEQ_LEN, HEAD_DIM)
+        grad_in, qk_part, value_part = attend_head(wide, up, gq_ref[:, cols], gv_ref[:, cols])
+        g_ref[:, :, cols] = grad_in.reshape(g_ref.shape[0], g_ref.shape[1], HEAD_DIM)
+
+        @pl.when(n == 0)
+        def _():
+            qs_ref[:, cols] = qk_part
+            vs_ref[:, cols] = value_part
+
+        @pl.when(n > 0)
+        def _():
+            qs_ref[:, cols] += qk_part
+            vs_ref[:, cols] += value_part
 
 
 INTERPRET = False
 
 
 def tile_of(array, slot):
-    half = array.shape[-2]
+    half, width = array.shape[-2], array.shape[-1]
     if slot is None:
-        return pl.BlockSpec((2, half, HEAD_DIM), lambda h, n: (n, 0, h))
-    return pl.BlockSpec((2, None, half, HEAD_DIM), lambda h, n: (n, slot, 0, h))
+        return pl.BlockSpec((2, half, width), lambda n: (n, 0, 0))
+    return pl.BlockSpec((2, None, half, width), lambda n: (n, slot, 0, 0))
 
 
 def local_backward(inputs, inputs_slot, upstream, upstream_slot, gain_qk, gain_value):
     blocks, half, width = upstream.shape[0], upstream.shape[-2], upstream.shape[-1]
     heads = width // HEAD_DIM
     count = blocks * half // SEQ_LEN
-    gain = pl.BlockSpec((1, HEAD_DIM), lambda h, n: (0, h))
+    gain = pl.BlockSpec((1, width), lambda n: (0, 0))
     flops = heads * count * 5 * 2 * SEQ_LEN * SEQ_LEN * HEAD_DIM
     grad_in, qk_part, value_part = pl.pallas_call(
         attention_kernel,
-        grid=(heads, count),
+        grid=(count,),
         in_specs=[tile_of(inputs, inputs_slot), tile_of(upstream, upstream_slot), gain, gain],
         out_specs=[tile_of(upstream, None), gain, gain],
         out_shape=[
@@ -96,36 +103,37 @@
     return grad_in, qk_part[0], value_part[0]
 
 
-def split_kernel(a_ref, b_ref, c_ref, first_ref, later_ref):
-    first_ref[0, 0] = a_ref[...]
-    first_ref[0, 1] = b_ref[...]
-    later_ref[0] = c_ref[...]
-
-
 def split_blocks(saved_inputs, incoming):
     parts = lax.axis_size("tp")
     ticks, _, rows, width = saved_inputs.shape
     cut = width // parts
     stacked = saved_inputs.reshape(ticks, rows, width)
     grad = incoming.reshape(rows, width)
+
+    def split_kernel(x_hbm, g_hbm, first_hbm, later_hbm, sems):
+        copies = []
+        for j in range(parts):
+            cols = pl.ds(j * cut, cut)
+            copies.append(pltpu.make_async_copy(x_hbm.at[0, :, cols], first_hbm.at[j, 0], sems.at[0, j]))
+            copies.append(pltpu.make_async_copy(g_hbm.at[:, cols], first_hbm.at[j, 1], sems.at[1, j]))
+            copies.append(pltpu.make_async_copy(x_hbm.at[1, :, cols], later_hbm.at[j], sems.at[2, j]))
+        for c in copies:
+            c.start()
+        for c in copies:
+            c.wait()
+
+    anywhere = pl.BlockSpec(memory_space=pl.ANY)
     return pl.pallas_call(
         split_kernel,
-        grid=(parts,),
-        in_specs=[
-            pl.BlockSpec((None, rows, cut), lambda j: (0, 0, j)),
-            pl.BlockSpec((rows, cut), lambda j: (0, j)),
-            pl.BlockSpec((None, rows, cut), lambda j: (1, 0, j)),
-        ],
-        out_specs=[
-            pl.BlockSpec((1, 2, rows, cut), lambda j: (j, 0, 0, 0)),
-            pl.BlockSpec((1, rows, cut), lambda j: (j, 0, 0)),
-        ],
+        in_specs=[anywhere, anywhere],
+        out_specs=[anywhere, anywhere],
         out_shape=[
             jax.ShapeDtypeStruct((parts, 2, rows, cut), saved_inputs.dtype),
             jax.ShapeDtypeStruct((parts, rows, cut), saved_inputs.dtype),
         ],
+        scratch_shapes=[pltpu.SemaphoreType.DMA((3, parts))],
         interpret=INTERPRET,
-    )(stacked, grad, stacked)
+    )(stacked, grad)
 
 
 def to_heads(block):

time: 233 us -> 331 us (1.42)
  the two profiles are of different devices: /device:TPU:6 before, /device:TPU:64 now
where the time goes in v7:
time: 331 us; the launch traced here: 330 us
  Pallas kernels  139 us (42%)
  blocking collectives  77.3 us (23%)
  waiting for transfers between devices  74.4 us (22%)
  starting transfers between devices  32.2 us (10%)
  local copies, waits for them, and re-layouts  5.5 us (2%)
    pallas_call x1, Pallas kernels, split_blocks(): pl.pallas_call(split_kernel, in_specs=[anywhere, anywhere], out_specs=[an...  109 us
    all_to_all x1, blocking collectives, to_heads(): return lax.all_to_all(block, 'tp', 0, 0, tiled=True)  77.3 us
    ppermute x2, waiting for transfers between devices, from_behind(): return lax.ppermute(block, axis, route)  45.7 us
    pallas_call x2, Pallas kernels, local_backward(): pl.pallas_call(attention_kernel, grid=(count,), in_specs=[tile_of(inputs,...  30.5 us
    all_to_all x1, waiting for transfers between devices, to_tokens(): back = lax.all_to_all(block, 'tp', 0, 0, tiled=True)  28.6 us
    ppermute x2, starting transfers between devices, from_behind(): return lax.ppermute(block, axis, route)  15.4 us
    all_to_all x1, starting transfers between devices, to_tokens(): back = lax.all_to_all(block, 'tp', 0, 0, tiled=True)  11.1 us
  transfers between devices with their start and end apart: 4, of which 3 were waited for; matrix products, arithmetic and copies ran while one was open for 1% of the time, Pallas kernels for 5%

profile of v7, /device:TPU:64, one launch (start us, length us, event | category | flops | bytes accessed | tf_op | source)
XLA Modules:
  0.0 330.3 jit_solution(16256145507816674420)
XLA Ops:
  0.6 108.6 %shard_map.67 = (bf16[12,2,128,384]{3,2,1,0:T(8,128)(2,1)}, bf16[12,128,384]{2,1,0:T(8,128)(2,1)}) custom-call(bf16[2,128,4608]{2,1,0:T(8,128)(2,1)} %bitcast.6, bf16[128,4608]{1,0:T(8,128)(2,1)} %bitcast.7), custom_call_target="tpu_custom_call" | custom-call | tf_op jit(solution)/shard_map/pallas_call | solution.py:126
  109.3 77.3 %all_to_all.15.x_ref.u_ref = bf16[12,2,128,384]{3,2,1,0:T(8,128)(2,1)} all-to-all(bf16[12,2,128,384]{3,2,1,0:T(8,128)(2,1)} %get-tuple-element.12), channel_id=1, replica_groups=mesh['section'=64,'tp'=12] {'tp'}, dimensions={0} | all-to-all | bytes 4718592 | tf_op jit(solution)/shard_map/all_to_all | solution.py:140
  186.5 5.7 %all-to-all-start.1 = ((bf16[12,128,384]{2,1,0:T(8,128)(2,1)}), bf16[12,128,384]{2,1,0:T(8,128)(2,1)S(1)}, u32[]{:S(2)}, u32[]{:S(2)}) async-start(bf16[12,128,384]{2,1,0:T(8,128)(2,1)} %get-tuple-element.14), calls=%async_computation.1 | async-start | bytes 2359296 | tf_op jit(solution)/shard_map/all_to_all | solution.py:140
  192.2 1.3 constant_dynamic-slice_fusion
  193.5 15.3 %shard_map.68 = (bf16[12,128,384]{2,1,0:T(8,128)(2,1)}, f32[1,384]{1,0:T(1,128)}, f32[1,384]{1,0:T(1,128)}) custom-call(bf16[12,2,128,384]{3,2,1,0:T(8,128)(2,1)} %all_to_all.15.x_ref.u_ref, bf16[12,2,128,384]{3,2,1,0:T(8,128)(2,1)} %all_to_all.15.x_ref.u_ref, f32[1,384]{1,0:T(1,128)} %get-tuple-element.25.gq_ref, f32[1,384]{1,0:T(1,128)} %get-tuple-element.24.gv_ref), custom_call_target="tpu_custom_call" | custom-call | flops 1509949440 | bytes 3538944 | tf_op jit(solution)/shard_map/pallas_call | solution.py:86
  208.8 9.6 %collective-permute-start = (bf16[12,128,384]{2,1,0:T(8,128)(2,1)}, bf16[12,128,384]{2,1,0:T(8,128)(2,1)S(1)}, u32[]{:S(2)}, u32[]{:S(2)}) collective-permute-start(bf16[12,128,384]{2,1,0:T(8,128)(2,1)} %get-tuple-element.15), channel_id=1, source_target_pairs={{12,0},{24,12},{36,24},{48,36},{60,48},{72,60},{84,72},{96,84},{10... | collective-permute-start | bytes 3538952 | tf_op jit(solution)/shard_map/ppermute | solution.py:15
  218.3 26.5 %collective-permute-done.u_ref = bf16[12,128,384]{2,1,0:T(8,128)(2,1)S(1)} collective-permute-done((bf16[12,128,384]{2,1,0:T(8,128)(2,1)}, bf16[12,128,384]{2,1,0:T(8,128)(2,1)S(1)}, u32[]{:S(2)}, u32[]{:S(2)}) %collective-permute-start) | collective-permute-done | bytes 1179680 | tf_op jit(solution)/shard_map/ppermute | solution.py:15
  244.8 0.0 copy-start.5
  244.8 0.0 all-to-all-done.1.x_ref
  244.9 1.0 copy-done.5
  245.9 0.0 copy-start
  245.9 1.0 copy-done
  246.9 15.3 %shard_map.69 = (bf16[12,128,384]{2,1,0:T(8,128)(2,1)}, f32[1,384]{1,0:T(1,128)}, f32[1,384]{1,0:T(1,128)}) custom-call(bf16[12,128,384]{2,1,0:T(8,128)(2,1)} %copy-done, bf16[12,128,384]{2,1,0:T(8,128)(2,1)} %copy-done.5, f32[1,384]{1,0:T(1,128)} %get-tuple-element.25.gq_ref, f32[1,384]{1,0:T(1,128)} %get-tuple-element.24.gv_ref), custom_call_target="tpu_custom_call" | custom-call | flops 1509949440 | bytes 3538944 | tf_op jit(solution)/shard_map/pallas_call | solution.py:86
  262.2 0.0 copy-start.2
  262.2 0.0 copy-start.4
  262.2 0.0 copy-start.1
  262.2 0.0 copy-start.3
  262.2 5.8 %collective-permute-start.1 = (bf16[12,128,384]{2,1,0:T(8,128)(2,1)}, bf16[12,128,384]{2,1,0:T(8,128)(2,1)}, u32[]{:S(2)}, u32[]{:S(2)}) collective-permute-start(bf16[12,128,384]{2,1,0:T(8,128)(2,1)} %get-tuple-element.16), channel_id=1, source_target_pairs={{12,0},{24,12},{36,24},{48,36},{60,48},{72,60},{84,72},{96,84},{10... | collective-permute-start | bytes 3538952 | tf_op jit(solution)/shard_map/ppermute | solution.py:15
  268.0 19.2 %collective-permute-done.1 = bf16[12,128,384]{2,1,0:T(8,128)(2,1)} collective-permute-done((bf16[12,128,384]{2,1,0:T(8,128)(2,1)}, bf16[12,128,384]{2,1,0:T(8,128)(2,1)}, u32[]{:S(2)}, u32[]{:S(2)}) %collective-permute-start.1) | collective-permute-done | bytes 1179680 | tf_op jit(solution)/shard_map/ppermute | solution.py:15
  287.2 11.1 %all-to-all-start.2 = ((bf16[12,128,384]{2,1,0:T(8,128)(2,1)}), bf16[12,128,384]{2,1,0:T(8,128)(2,1)S(1)}, u32[]{:S(2)}, u32[]{:S(2)}) async-start(bf16[12,128,384]{2,1,0:T(8,128)(2,1)} %collective-permute-done.1), calls=%async_computation.2 | async-start | bytes 2359296 | tf_op jit(solution)/shard_map/all_to_all | solution.py:144
  298.4 0.0 copy-done.2
  298.4 0.0 copy-done.4
  298.4 0.6 add.13
  299.0 0.0 copy-done.1
  299.0 0.0 copy-done.3
  299.0 0.6 add.14
  299.5 28.6 %all-to-all-done.2 = bf16[12,128,384]{2,1,0:T(8,128)(2,1)S(1)} async-done(((bf16[12,128,384]{2,1,0:T(8,128)(2,1)}), bf16[12,128,384]{2,1,0:T(8,128)(2,1)S(1)}, u32[]{:S(2)}, u32[]{:S(2)}) %all-to-all-start.2) | async-done | bytes 1179680 | tf_op jit(solution)/shard_map/all_to_all | solution.py:144
  328.1 0.8 copy.7
  328.9 1.4 copy.8
Async XLA Ops:
  186.5 58.3 %all-to-all-start.1 = ((bf16[12,128,384]{2,1,0:T(8,128)(2,1)}), bf16[12,128,384]{2,1,0:T(8,128)(2,1)S(1)}, u32[]{:S(2)}, u32[]{:S(2)}) async-start(bf16[12,128,384]{2,1,0:T(8,128)(2,1)} %get-tuple-element.14), calls=%async_computation.1 | async-start | bytes 2359296 | tf_op jit(solution)/shard_map/all_to_all | solution.py:140
  208.8 36.1 %collective-permute-start = (bf16[12,128,384]{2,1,0:T(8,128)(2,1)}, bf16[12,128,384]{2,1,0:T(8,128)(2,1)S(1)}, u32[]{:S(2)}, u32[]{:S(2)}) collective-permute-start(bf16[12,128,384]{2,1,0:T(8,128)(2,1)} %get-tuple-element.15), channel_id=1, source_target_pairs={{12,0},{24,12},{36,24},{48,36},{60,48},{72,60},{84,72},{96,84},{10... | collective-permute-start | bytes 3538952 | tf_op jit(solution)/shard_map/ppermute | solution.py:15
  244.8 1.0 copy-start.5
  245.9 1.0 copy-start
  262.2 36.2 %copy-start.2 = (f32[1,384]{1,0:T(1,128)S(1)}, f32[1,384]{1,0:T(1,128)}, u32[]{:S(2)}) copy-start(f32[1,384]{1,0:T(1,128)} %get-tuple-element.17) | copy-start | bytes 4612
  262.2 36.2 %copy-start.4 = (f32[1,384]{1,0:T(1,128)S(1)}, f32[1,384]{1,0:T(1,128)}, u32[]{:S(2)}) copy-start(f32[1,384]{1,0:T(1,128)} %get-tuple-element.18) | copy-start | bytes 4612
  262.2 36.8 %copy-start.1 = (f32[1,384]{1,0:T(1,128)S(1)}, f32[1,384]{1,0:T(1,128)}, u32[]{:S(2)}) copy-start(f32[1,384]{1,0:T(1,128)} %get-tuple-element.19) | copy-start | bytes 4612
  262.2 36.8 %copy-start.3 = (f32[1,384]{1,0:T(1,128)S(1)}, f32[1,384]{1,0:T(1,128)}, u32[]{:S(2)}) copy-start(f32[1,384]{1,0:T(1,128)} %get-tuple-element.20) | copy-start | bytes 4612
  262.2 25.1 %collective-permute-start.1 = (bf16[12,128,384]{2,1,0:T(8,128)(2,1)}, bf16[12,128,384]{2,1,0:T(8,128)(2,1)}, u32[]{:S(2)}, u32[]{:S(2)}) collective-permute-start(bf16[12,128,384]{2,1,0:T(8,128)(2,1)} %get-tuple-element.16), channel_id=1, source_target_pairs={{12,0},{24,12},{36,24},{48,36},{60,48},{72,60},{84,72},{96,84},{10... | collective-permute-start | bytes 3538952 | tf_op jit(solution)/shard_map/ppermute | solution.py:15
  287.2 40.9 %all-to-all-start.2 = ((bf16[12,128,384]{2,1,0:T(8,128)(2,1)}), bf16[12,128,384]{2,1,0:T(8,128)(2,1)S(1)}, u32[]{:S(2)}, u32[]{:S(2)}) async-start(bf16[12,128,384]{2,1,0:T(8,128)(2,1)} %collective-permute-done.1), calls=%async_computation.2 | async-start | bytes 2359296 | tf_op jit(solution)/shard_map/all_to_all | solution.py:144

commit v8 on v7

--- a/solution.py
+++ b/solution.py
@@ -3,7 +3,6 @@
 from jax import lax
 from jax.sharding import PartitionSpec as P
 from jax.experimental import pallas as pl
-from jax.experimental.pallas import tpu as pltpu
 
 HEAD_DIM = 128
 SEQ_LEN = 256
@@ -107,33 +106,35 @@
     parts = lax.axis_size("tp")
     ticks, _, rows, width = saved_inputs.shape
     cut = width // parts
+    group = 4 if parts % 4 == 0 else 1
     stacked = saved_inputs.reshape(ticks, rows, width)
     grad = incoming.reshape(rows, width)
 
-    def split_kernel(x_hbm, g_hbm, first_hbm, later_hbm, sems):
-        copies = []
-        for j in range(parts):
-            cols = pl.ds(j * cut, cut)
-            copies.append(pltpu.make_async_copy(x_hbm.at[0, :, cols], first_hbm.at[j, 0], sems.at[0, j]))
-            copies.append(pltpu.make_async_copy(g_hbm.at[:, cols], first_hbm.at[j, 1], sems.at[1, j]))
-            copies.append(pltpu.make_async_copy(x_hbm.at[1, :, cols], later_hbm.at[j], sems.at[2, j]))
-        for c in copies:
-            c.start()
-        for c in copies:
-            c.wait()
+    def split_kernel(a_ref, b_ref, c_ref, first_ref, later_ref):
+        for j in range(group):
+            cols = slice(j * cut, (j + 1) * cut)
+            first_ref[j, 0] = a_ref[:, cols]
+            first_ref[j, 1] = b_ref[:, cols]
+            later_ref[j] = c_ref[:, cols]
 
-    anywhere = pl.BlockSpec(memory_space=pl.ANY)
     return pl.pallas_call(
         split_kernel,
-        in_specs=[anywhere, anywhere],
-        out_specs=[anywhere, anywhere],
+        grid=(parts // group,),
+        in_specs=[
+            pl.BlockSpec((None, rows, group * cut), lambda j: (0, 0, j)),
+            pl.BlockSpec((rows, group * cut), lambda j: (0, j)),
+            pl.BlockSpec((None, rows, group * cut), lambda j: (1, 0, j)),
+        ],
+        out_specs=[
+            pl.BlockSpec((group, 2, rows, cut), lambda j: (j, 0, 0, 0)),
+            pl.BlockSpec((group, rows, cut), lambda j: (j, 0, 0)),
+        ],
         out_shape=[
             jax.ShapeDtypeStruct((parts, 2, rows, cut), saved_inputs.dtype),
             jax.ShapeDtypeStruct((parts, rows, cut), saved_inputs.dtype),
         ],
-        scratch_shapes=[pltpu.SemaphoreType.DMA((3, parts))],
         interpret=INTERPRET,
-    )(stacked, grad)
+    )(stacked, grad, stacked)
 
 
 def to_heads(block):

time: 331 us -> 227 us (0.69)
  Pallas kernels: 139 us -> 35.2 us
    pallas_call x1, Pallas kernels: 109 us -> 4.62 us  [split_blocks(): pl.pallas_call(split_kernel, grid=(parts // group,), in_specs=[pl.BlockSp...]
  transfers between devices with their start and end apart: 4 -> 4, of which waited for: 3 -> 3; matrix products, arithmetic and copies ran while one was open for 1% -> 1% of each run, Pallas kernels for 5% -> 7%
where the time goes in v8:
time: 227 us; the launch traced here: 226 us
  blocking collectives  77.3 us (34%)
  waiting for transfers between devices  74.4 us (33%)
  Pallas kernels  35.2 us (16%)
  starting transfers between devices  32.2 us (14%)
  local copies, waits for them, and re-layouts  5.5 us (2%)
    all_to_all x1, blocking collectives, to_heads(): return lax.all_to_all(block, 'tp', 0, 0, tiled=True)  77.3 us
    ppermute x2, waiting for transfers between devices, from_behind(): return lax.ppermute(block, axis, route)  45.7 us
    pallas_call x2, Pallas kernels, local_backward(): pl.pallas_call(attention_kernel, grid=(count,), in_specs=[tile_of(inputs,...  30.5 us
    all_to_all x1, waiting for transfers between devices, to_tokens(): back = lax.all_to_all(block, 'tp', 0, 0, tiled=True)  28.6 us
    ppermute x2, starting transfers between devices, from_behind(): return lax.ppermute(block, axis, route)  15.4 us
    all_to_all x1, starting transfers between devices, to_tokens(): back = lax.all_to_all(block, 'tp', 0, 0, tiled=True)  11.1 us
    all_to_all x1, starting transfers between devices, to_heads(): return lax.all_to_all(block, 'tp', 0, 0, tiled=True)  5.69 us
    pallas_call x1, Pallas kernels, split_blocks(): pl.pallas_call(split_kernel, grid=(parts // group,), in_specs=[pl.BlockSp...  4.62 us
  transfers between devices with their start and end apart: 4, of which 3 were waited for; matrix products, arithmetic and copies ran while one was open for 1% of the time, Pallas kernels for 7%

profile of v8, /device:TPU:64, one launch (start us, length us, event | category | flops | bytes accessed | tf_op | source)
XLA Modules:
  0.0 226.3 jit_solution(943311322073600623)
XLA Ops:
  0.6 4.6 %shard_map.67 = (bf16[12,2,128,384]{3,2,1,0:T(8,128)(2,1)}, bf16[12,128,384]{2,1,0:T(8,128)(2,1)}) custom-call(bf16[2,128,4608]{2,1,0:T(8,128)(2,1)} %bitcast.4, bf16[128,4608]{1,0:T(8,128)(2,1)} %bitcast.8, bf16[2,128,4608]{2,1,0:T(8,128)(2,1)} %bitcast.5), custom_call_target="tpu_custom_call" | custom-call | tf_op jit(solution)/shard_map/pallas_call | solution.py:120
  5.3 77.3 %all_to_all.15.x_ref.u_ref = bf16[12,2,128,384]{3,2,1,0:T(8,128)(2,1)} all-to-all(bf16[12,2,128,384]{3,2,1,0:T(8,128)(2,1)} %get-tuple-element.12), channel_id=1, replica_groups=mesh['section'=64,'tp'=12] {'tp'}, dimensions={0} | all-to-all | bytes 4718592 | tf_op jit(solution)/shard_map/all_to_all | solution.py:141
  82.5 5.7 %all-to-all-start.1 = ((bf16[12,128,384]{2,1,0:T(8,128)(2,1)}), bf16[12,128,384]{2,1,0:T(8,128)(2,1)S(1)}, u32[]{:S(2)}, u32[]{:S(2)}) async-start(bf16[12,128,384]{2,1,0:T(8,128)(2,1)} %get-tuple-element.14), calls=%async_computation.1 | async-start | bytes 2359296 | tf_op jit(solution)/shard_map/all_to_all | solution.py:141
  88.2 1.3 constant_dynamic-slice_fusion
  89.5 15.3 %shard_map.68 = (bf16[12,128,384]{2,1,0:T(8,128)(2,1)}, f32[1,384]{1,0:T(1,128)}, f32[1,384]{1,0:T(1,128)}) custom-call(bf16[12,2,128,384]{3,2,1,0:T(8,128)(2,1)} %all_to_all.15.x_ref.u_ref, bf16[12,2,128,384]{3,2,1,0:T(8,128)(2,1)} %all_to_all.15.x_ref.u_ref, f32[1,384]{1,0:T(1,128)} %get-tuple-element.25.gq_ref, f32[1,384]{1,0:T(1,128)} %get-tuple-element.24.gv_ref), custom_call_target="tpu_custom_call" | custom-call | flops 1509949440 | bytes 3538944 | tf_op jit(solution)/shard_map/pallas_call | solution.py:85
  104.8 9.6 %collective-permute-start = (bf16[12,128,384]{2,1,0:T(8,128)(2,1)}, bf16[12,128,384]{2,1,0:T(8,128)(2,1)S(1)}, u32[]{:S(2)}, u32[]{:S(2)}) collective-permute-start(bf16[12,128,384]{2,1,0:T(8,128)(2,1)} %get-tuple-element.15), channel_id=1, source_target_pairs={{12,0},{24,12},{36,24},{48,36},{60,48},{72,60},{84,72},{96,84},{10... | collective-permute-start | bytes 3538952 | tf_op jit(solution)/shard_map/ppermute | solution.py:14
  114.3 26.5 %collective-permute-done.u_ref = bf16[12,128,384]{2,1,0:T(8,128)(2,1)S(1)} collective-permute-done((bf16[12,128,384]{2,1,0:T(8,128)(2,1)}, bf16[12,128,384]{2,1,0:T(8,128)(2,1)S(1)}, u32[]{:S(2)}, u32[]{:S(2)}) %collective-permute-start) | collective-permute-done | bytes 1179680 | tf_op jit(solution)/shard_map/ppermute | solution.py:14
  140.8 0.0 copy-start.5
  140.8 0.0 all-to-all-done.1.x_ref
  140.8 1.0 copy-done.5
  141.9 0.0 copy-start
  141.9 1.0 copy-done
  142.9 15.3 %shard_map.69 = (bf16[12,128,384]{2,1,0:T(8,128)(2,1)}, f32[1,384]{1,0:T(1,128)}, f32[1,384]{1,0:T(1,128)}) custom-call(bf16[12,128,384]{2,1,0:T(8,128)(2,1)} %copy-done, bf16[12,128,384]{2,1,0:T(8,128)(2,1)} %copy-done.5, f32[1,384]{1,0:T(1,128)} %get-tuple-element.25.gq_ref, f32[1,384]{1,0:T(1,128)} %get-tuple-element.24.gv_ref), custom_call_target="tpu_custom_call" | custom-call | flops 1509949440 | bytes 3538944 | tf_op jit(solution)/shard_map/pallas_call | solution.py:85
  158.1 0.0 copy-start.2
  158.1 0.0 copy-start.4
  158.1 0.0 copy-start.1
  158.1 0.0 copy-start.3
  158.2 5.8 %collective-permute-start.1 = (bf16[12,128,384]{2,1,0:T(8,128)(2,1)}, bf16[12,128,384]{2,1,0:T(8,128)(2,1)}, u32[]{:S(2)}, u32[]{:S(2)}) collective-permute-start(bf16[12,128,384]{2,1,0:T(8,128)(2,1)} %get-tuple-element.16), channel_id=1, source_target_pairs={{12,0},{24,12},{36,24},{48,36},{60,48},{72,60},{84,72},{96,84},{10... | collective-permute-start | bytes 3538952 | tf_op jit(solution)/shard_map/ppermute | solution.py:14
  164.0 19.2 %collective-permute-done.1 = bf16[12,128,384]{2,1,0:T(8,128)(2,1)} collective-permute-done((bf16[12,128,384]{2,1,0:T(8,128)(2,1)}, bf16[12,128,384]{2,1,0:T(8,128)(2,1)}, u32[]{:S(2)}, u32[]{:S(2)}) %collective-permute-start.1) | collective-permute-done | bytes 1179680 | tf_op jit(solution)/shard_map/ppermute | solution.py:14
  183.2 11.1 %all-to-all-start.2 = ((bf16[12,128,384]{2,1,0:T(8,128)(2,1)}), bf16[12,128,384]{2,1,0:T(8,128)(2,1)S(1)}, u32[]{:S(2)}, u32[]{:S(2)}) async-start(bf16[12,128,384]{2,1,0:T(8,128)(2,1)} %collective-permute-done.1), calls=%async_computation.2 | async-start | bytes 2359296 | tf_op jit(solution)/shard_map/all_to_all | solution.py:145
  194.3 0.0 copy-done.2
  194.4 0.0 copy-done.4
  194.4 0.6 add.13
  194.9 0.0 copy-done.1
  194.9 0.0 copy-done.3
  194.9 0.6 add.14
  195.5 28.6 %all-to-all-done.2 = bf16[12,128,384]{2,1,0:T(8,128)(2,1)S(1)} async-done(((bf16[12,128,384]{2,1,0:T(8,128)(2,1)}), bf16[12,128,384]{2,1,0:T(8,128)(2,1)S(1)}, u32[]{:S(2)}, u32[]{:S(2)}) %all-to-all-start.2) | async-done | bytes 1179680 | tf_op jit(solution)/shard_map/all_to_all | solution.py:145
  224.1 0.8 copy.7
  224.9 1.4 copy.8
Async XLA Ops:
  82.5 58.3 %all-to-all-start.1 = ((bf16[12,128,384]{2,1,0:T(8,128)(2,1)}), bf16[12,128,384]{2,1,0:T(8,128)(2,1)S(1)}, u32[]{:S(2)}, u32[]{:S(2)}) async-start(bf16[12,128,384]{2,1,0:T(8,128)(2,1)} %get-tuple-element.14), calls=%async_computation.1 | async-start | bytes 2359296 | tf_op jit(solution)/shard_map/all_to_all | solution.py:141
  104.8 36.1 %collective-permute-start = (bf16[12,128,384]{2,1,0:T(8,128)(2,1)}, bf16[12,128,384]{2,1,0:T(8,128)(2,1)S(1)}, u32[]{:S(2)}, u32[]{:S(2)}) collective-permute-start(bf16[12,128,384]{2,1,0:T(8,128)(2,1)} %get-tuple-element.15), channel_id=1, source_target_pairs={{12,0},{24,12},{36,24},{48,36},{60,48},{72,60},{84,72},{96,84},{10... | collective-permute-start | bytes 3538952 | tf_op jit(solution)/shard_map/ppermute | solution.py:14
  140.8 1.0 copy-start.5
  141.9 1.0 copy-start
  158.1 36.2 %copy-start.2 = (f32[1,384]{1,0:T(1,128)S(1)}, f32[1,384]{1,0:T(1,128)}, u32[]{:S(2)}) copy-start(f32[1,384]{1,0:T(1,128)} %get-tuple-element.17) | copy-start | bytes 4612
  158.1 36.2 %copy-start.4 = (f32[1,384]{1,0:T(1,128)S(1)}, f32[1,384]{1,0:T(1,128)}, u32[]{:S(2)}) copy-start(f32[1,384]{1,0:T(1,128)} %get-tuple-element.18) | copy-start | bytes 4612
  158.1 36.8 %copy-start.1 = (f32[1,384]{1,0:T(1,128)S(1)}, f32[1,384]{1,0:T(1,128)}, u32[]{:S(2)}) copy-start(f32[1,384]{1,0:T(1,128)} %get-tuple-element.19) | copy-start | bytes 4612
  158.1 36.8 %copy-start.3 = (f32[1,384]{1,0:T(1,128)S(1)}, f32[1,384]{1,0:T(1,128)}, u32[]{:S(2)}) copy-start(f32[1,384]{1,0:T(1,128)} %get-tuple-element.20) | copy-start | bytes 4612
  158.2 25.1 %collective-permute-start.1 = (bf16[12,128,384]{2,1,0:T(8,128)(2,1)}, bf16[12,128,384]{2,1,0:T(8,128)(2,1)}, u32[]{:S(2)}, u32[]{:S(2)}) collective-permute-start(bf16[12,128,384]{2,1,0:T(8,128)(2,1)} %get-tuple-element.16), channel_id=1, source_target_pairs={{12,0},{24,12},{36,24},{48,36},{60,48},{72,60},{84,72},{96,84},{10... | collective-permute-start | bytes 3538952 | tf_op jit(solution)/shard_map/ppermute | solution.py:14
  183.2 40.9 %all-to-all-start.2 = ((bf16[12,128,384]{2,1,0:T(8,128)(2,1)}), bf16[12,128,384]{2,1,0:T(8,128)(2,1)S(1)}, u32[]{:S(2)}, u32[]{:S(2)}) async-start(bf16[12,128,384]{2,1,0:T(8,128)(2,1)} %collective-permute-done.1), calls=%async_computation.2 | async-start | bytes 2359296 | tf_op jit(solution)/shard_map/all_to_all | solution.py:145

commit v9 on v8

--- a/solution.py
+++ b/solution.py
@@ -18,14 +18,10 @@
     return from_behind(grad_in, "section", -1)
 
 
-def attend_head(wide, up, gq, gv):
-    scale = HEAD_DIM ** (-0.5)
-    keys = (wide * gq).astype(jnp.bfloat16)
-    values = (wide * gv).astype(jnp.bfloat16)
+def half_softmax_grads(queries, keys, values, up, offset, scale):
     nt = (((1,), (1,)), ((), ()))
-    tn = (((0,), (0,)), ((), ()))
-    scores = lax.dot_general(keys, keys, nt, preferred_element_type=jnp.float32) * scale
-    rows = lax.broadcasted_iota(jnp.int32, scores.shape, 0)
+    scores = lax.dot_general(queries, keys, nt, preferred_element_type=jnp.float32) * scale
+    rows = lax.broadcasted_iota(jnp.int32, scores.shape, 0) + offset
     cols = lax.broadcasted_iota(jnp.int32, scores.shape, 1)
     scores = jnp.where(cols <= rows, scores, -jnp.inf)
     row_max = jnp.max(scores, axis=1, keepdims=True)
@@ -33,13 +29,34 @@
     probs = weights / jnp.sum(weights, axis=1, keepdims=True)
     prob_grad = lax.dot_general(up, values, nt, preferred_element_type=jnp.float32)
     score_grad = probs * (prob_grad - jnp.sum(probs * prob_grad, axis=1, keepdims=True))
-    score_low = score_grad.astype(jnp.bfloat16)
-    probs_low = probs.astype(jnp.bfloat16)
-    query_grad = jnp.dot(score_low, keys, preferred_element_type=jnp.float32) * scale
-    key_grad = lax.dot_general(score_low, keys, tn, preferred_element_type=jnp.float32) * scale
-    value_grad = lax.dot_general(probs_low, up, tn, preferred_element_type=jnp.float32)
-    qk_total = query_grad + key_grad
-    grad_in = (up.astype(jnp.float32) + qk_total * gq + value_grad * gv).astype(jnp.bfloat16)
+    return probs.astype(jnp.bfloat16), score_grad.astype(jnp.bfloat16)
+
+
+def attend_head(wide, up, gq, gv):
+    scale = HEAD_DIM ** (-0.5)
+    half = SEQ_LEN // 2
+    keys = (wide * gq).astype(jnp.bfloat16)
+    values = (wide * gv).astype(jnp.bfloat16)
+    tn = (((0,), (0,)), ((), ()))
+    k_a, k_b = keys[:half], keys[half:]
+    u_a, u_b = up[:half], up[half:]
+    p_a, s_a = half_softmax_grads(k_a, k_a, values[:half], u_a, 0, scale)
+    p_b, s_b = half_softmax_grads(k_b, keys, values, u_b, half, scale)
+    f32 = jnp.float32
+    query_a = jnp.dot(s_a, k_a, preferred_element_type=f32) * scale
+    query_b = jnp.dot(s_b, keys, preferred_element_type=f32) * scale
+    key_a = (
+        lax.dot_general(s_a, k_a, tn, preferred_element_type=f32)
+        + lax.dot_general(s_b[:, :half], k_b, tn, preferred_element_type=f32)
+    ) * scale
+    key_b = lax.dot_general(s_b[:, half:], k_b, tn, preferred_element_type=f32) * scale
+    value_a = lax.dot_general(p_a, u_a, tn, preferred_element_type=f32) + lax.dot_general(
+        p_b[:, :half], u_b, tn, preferred_element_type=f32
+    )
+    value_b = lax.dot_general(p_b[:, half:], u_b, tn, preferred_element_type=f32)
+    qk_total = jnp.concatenate([query_a + key_a, query_b + key_b], axis=0)
+    value_grad = jnp.concatenate([value_a, value_b], axis=0)
+    grad_in = (up.astype(f32) + qk_total * gq + value_grad * gv).astype(jnp.bfloat16)
     qk_part = jnp.sum(wide * qk_total, axis=0, keepdims=True)
     value_part = jnp.sum(wide * value_grad, axis=0, keepdims=True)
     return grad_in, qk_part, value_part
@@ -153,6 +170,7 @@
     gain_qk = lax.dynamic_slice_in_dim(qk_gain[0], offset, local_width)
     gain_value = lax.dynamic_slice_in_dim(value_gain[0], offset, local_width)
     first, later = split_blocks(saved_inputs, incoming)
+    first, gain_qk, gain_value = lax.optimization_barrier((first, gain_qk, gain_value))
     first = to_heads(first)
     grad_in, qk_sum, value_sum = local_backward(first, 0, first, 1, gain_qk, gain_value)
     for t in range(1, tick_count):

time: 227 us -> 228 us (level)
  no operation moved by 1% of the time
where the time goes in v9:
time: 228 us
  blocking collectives  77.3 us (34%)
  waiting for transfers between devices  74.5 us (33%)
  Pallas kernels  36 us (16%)
  starting transfers between devices  32.1 us (14%)
  local copies, waits for them, and re-layouts  6.06 us (3%)
    all_to_all x1, blocking collectives, to_heads(): return lax.all_to_all(block, 'tp', 0, 0, tiled=True)  77.3 us
    ppermute x2, waiting for transfers between devices, from_behind(): return lax.ppermute(block, axis, route)  45.2 us
    pallas_call x2, Pallas kernels, local_backward(): pl.pallas_call(attention_kernel, grid=(count,), in_specs=[tile_of(inputs,...  31.4 us
    all_to_all x1, waiting for transfers between devices, to_tokens(): back = lax.all_to_all(block, 'tp', 0, 0, tiled=True)  29.3 us
    ppermute x2, starting transfers between devices, from_behind(): return lax.ppermute(block, axis, route)  15.4 us
    all_to_all x1, starting transfers between devices, to_tokens(): back = lax.all_to_all(block, 'tp', 0, 0, tiled=True)  11 us
    all_to_all x1, starting transfers between devices, to_heads(): return lax.all_to_all(block, 'tp', 0, 0, tiled=True)  5.69 us
    pallas_call x1, Pallas kernels, split_blocks(): pl.pallas_call(split_kernel, grid=(parts // group,), in_specs=[pl.BlockSp...  4.62 us
  transfers between devices with their start and end apart: 4, of which 3 were waited for; matrix products, arithmetic and copies ran while one was open for 1% of the time, Pallas kernels for 7%

profile of v9, /device:TPU:64, one launch (start us, length us, event | category | flops | bytes accessed | tf_op | source)
XLA Modules:
  0.0 227.8 jit_solution(6142759863596503959)
XLA Ops:
  0.6 4.6 %shard_map.67 = (bf16[12,2,128,384]{3,2,1,0:T(8,128)(2,1)}, bf16[12,128,384]{2,1,0:T(8,128)(2,1)}) custom-call(bf16[2,128,4608]{2,1,0:T(8,128)(2,1)} %bitcast.4, bf16[128,4608]{1,0:T(8,128)(2,1)} %bitcast.8, bf16[2,128,4608]{2,1,0:T(8,128)(2,1)} %bitcast.5), custom_call_target="tpu_custom_call" | custom-call | tf_op jit(solution)/shard_map/pallas_call | solution.py:137
  5.3 0.7 dynamic-slice_reduce_fusion
  6.0 77.3 %all_to_all.15.x_ref.u_ref = bf16[12,2,128,384]{3,2,1,0:T(8,128)(2,1)} all-to-all(bf16[12,2,128,384]{3,2,1,0:T(8,128)(2,1)} %get-tuple-element.16), channel_id=1, replica_groups=mesh['section'=64,'tp'=12] {'tp'}, dimensions={0} | all-to-all | bytes 4718592 | tf_op jit(solution)/shard_map/all_to_all | solution.py:158
  83.3 5.7 %all-to-all-start.1 = ((bf16[12,128,384]{2,1,0:T(8,128)(2,1)}), bf16[12,128,384]{2,1,0:T(8,128)(2,1)S(1)}, u32[]{:S(2)}, u32[]{:S(2)}) async-start(bf16[12,128,384]{2,1,0:T(8,128)(2,1)} %get-tuple-element.18), calls=%async_computation.1 | async-start | bytes 2359296 | tf_op jit(solution)/shard_map/all_to_all | solution.py:158
  88.9 0.6 broadcast_in_dim.4.gq_ref
  89.5 0.6 broadcast_in_dim.5.gv_ref
  90.1 15.7 %shard_map.68 = (bf16[12,128,384]{2,1,0:T(8,128)(2,1)}, f32[1,384]{1,0:T(1,128)}, f32[1,384]{1,0:T(1,128)}) custom-call(bf16[12,2,128,384]{3,2,1,0:T(8,128)(2,1)} %all_to_all.15.x_ref.u_ref, bf16[12,2,128,384]{3,2,1,0:T(8,128)(2,1)} %all_to_all.15.x_ref.u_ref, f32[1,384]{1,0:T(1,128)} %broadcast_in_dim.4.gq_ref, f32[1,384]{1,0:T(1,128)} %broadcast_in_dim.5.gv_ref), custom_call_target="tpu_custom_call" | custom-call | flops 1509949440 | bytes 3538944 | tf_op jit(solution)/shard_map/pallas_call | solution.py:102
  105.8 9.5 %collective-permute-start = (bf16[12,128,384]{2,1,0:T(8,128)(2,1)}, bf16[12,128,384]{2,1,0:T(8,128)(2,1)S(1)}, u32[]{:S(2)}, u32[]{:S(2)}) collective-permute-start(bf16[12,128,384]{2,1,0:T(8,128)(2,1)} %get-tuple-element.21), channel_id=1, source_target_pairs={{12,0},{24,12},{36,24},{48,36},{60,48},{72,60},{84,72},{96,84},{10... | collective-permute-start | bytes 3538952 | tf_op jit(solution)/shard_map/ppermute | solution.py:14
  115.3 26.2 %collective-permute-done.u_ref = bf16[12,128,384]{2,1,0:T(8,128)(2,1)S(1)} collective-permute-done((bf16[12,128,384]{2,1,0:T(8,128)(2,1)}, bf16[12,128,384]{2,1,0:T(8,128)(2,1)S(1)}, u32[]{:S(2)}, u32[]{:S(2)}) %collective-permute-start) | collective-permute-done | bytes 1179680 | tf_op jit(solution)/shard_map/ppermute | solution.py:14
  141.6 0.0 copy-start.5
  141.6 0.0 all-to-all-done.1.x_ref
  141.6 1.0 copy-done.5
  142.6 0.0 copy-start
  142.6 1.0 copy-done
  143.6 15.7 %shard_map.69 = (bf16[12,128,384]{2,1,0:T(8,128)(2,1)}, f32[1,384]{1,0:T(1,128)}, f32[1,384]{1,0:T(1,128)}) custom-call(bf16[12,128,384]{2,1,0:T(8,128)(2,1)} %copy-done, bf16[12,128,384]{2,1,0:T(8,128)(2,1)} %copy-done.5, f32[1,384]{1,0:T(1,128)} %broadcast_in_dim.4.gq_ref, f32[1,384]{1,0:T(1,128)} %broadcast_in_dim.5.gv_ref), custom_call_target="tpu_custom_call" | custom-call | flops 1509949440 | bytes 3538944 | tf_op jit(solution)/shard_map/pallas_call | solution.py:102
  159.3 0.0 copy-start.2
  159.3 0.0 copy-start.4
  159.3 0.0 copy-start.1
  159.3 0.0 copy-start.3
  159.3 5.8 %collective-permute-start.1 = (bf16[12,128,384]{2,1,0:T(8,128)(2,1)}, bf16[12,128,384]{2,1,0:T(8,128)(2,1)}, u32[]{:S(2)}, u32[]{:S(2)}) collective-permute-start(bf16[12,128,384]{2,1,0:T(8,128)(2,1)} %get-tuple-element.22), channel_id=1, source_target_pairs={{12,0},{24,12},{36,24},{48,36},{60,48},{72,60},{84,72},{96,84},{10... | collective-permute-start | bytes 3538952 | tf_op jit(solution)/shard_map/ppermute | solution.py:14
  165.1 19.0 %collective-permute-done.1 = bf16[12,128,384]{2,1,0:T(8,128)(2,1)} collective-permute-done((bf16[12,128,384]{2,1,0:T(8,128)(2,1)}, bf16[12,128,384]{2,1,0:T(8,128)(2,1)}, u32[]{:S(2)}, u32[]{:S(2)}) %collective-permute-start.1) | collective-permute-done | bytes 1179680 | tf_op jit(solution)/shard_map/ppermute | solution.py:14
  184.1 11.0 %all-to-all-start.2 = ((bf16[12,128,384]{2,1,0:T(8,128)(2,1)}), bf16[12,128,384]{2,1,0:T(8,128)(2,1)S(1)}, u32[]{:S(2)}, u32[]{:S(2)}) async-start(bf16[12,128,384]{2,1,0:T(8,128)(2,1)} %collective-permute-done.1), calls=%async_computation.2 | async-start | bytes 2359296 | tf_op jit(solution)/shard_map/all_to_all | solution.py:162
  195.1 0.0 copy-done.2
  195.1 0.0 copy-done.4
  195.1 0.6 add.14
  195.7 0.0 copy-done.1
  195.7 0.0 copy-done.3
  195.7 0.6 add.13
  196.3 29.3 %all-to-all-done.2 = bf16[12,128,384]{2,1,0:T(8,128)(2,1)S(1)} async-done(((bf16[12,128,384]{2,1,0:T(8,128)(2,1)}), bf16[12,128,384]{2,1,0:T(8,128)(2,1)S(1)}, u32[]{:S(2)}, u32[]{:S(2)}) %all-to-all-start.2) | async-done | bytes 1179680 | tf_op jit(solution)/shard_map/all_to_all | solution.py:162
  225.6 0.8 copy.7
  226.4 1.4 copy.8
Async XLA Ops:
  83.3 58.3 %all-to-all-start.1 = ((bf16[12,128,384]{2,1,0:T(8,128)(2,1)}), bf16[12,128,384]{2,1,0:T(8,128)(2,1)S(1)}, u32[]{:S(2)}, u32[]{:S(2)}) async-start(bf16[12,128,384]{2,1,0:T(8,128)(2,1)} %get-tuple-element.18), calls=%async_computation.1 | async-start | bytes 2359296 | tf_op jit(solution)/shard_map/all_to_all | solution.py:158
  105.8 35.8 %collective-permute-start = (bf16[12,128,384]{2,1,0:T(8,128)(2,1)}, bf16[12,128,384]{2,1,0:T(8,128)(2,1)S(1)}, u32[]{:S(2)}, u32[]{:S(2)}) collective-permute-start(bf16[12,128,384]{2,1,0:T(8,128)(2,1)} %get-tuple-element.21), channel_id=1, source_target_pairs={{12,0},{24,12},{36,24},{48,36},{60,48},{72,60},{84,72},{96,84},{10... | collective-permute-start | bytes 3538952 | tf_op jit(solution)/shard_map/ppermute | solution.py:14
  141.6 1.0 copy-start.5
  142.6 1.0 copy-start
  159.3 35.9 %copy-start.2 = (f32[1,384]{1,0:T(1,128)S(1)}, f32[1,384]{1,0:T(1,128)}, u32[]{:S(2)}) copy-start(f32[1,384]{1,0:T(1,128)} %get-tuple-element.25) | copy-start | bytes 4612
  159.3 35.9 %copy-start.4 = (f32[1,384]{1,0:T(1,128)S(1)}, f32[1,384]{1,0:T(1,128)}, u32[]{:S(2)}) copy-start(f32[1,384]{1,0:T(1,128)} %get-tuple-element.26) | copy-start | bytes 4612
  159.3 36.4 %copy-start.1 = (f32[1,384]{1,0:T(1,128)S(1)}, f32[1,384]{1,0:T(1,128)}, u32[]{:S(2)}) copy-start(f32[1,384]{1,0:T(1,128)} %get-tuple-element.23) | copy-start | bytes 4612
  159.3 36.4 %copy-start.3 = (f32[1,384]{1,0:T(1,128)S(1)}, f32[1,384]{1,0:T(1,128)}, u32[]{:S(2)}) copy-start(f32[1,384]{1,0:T(1,128)} %get-tuple-element.24) | copy-start | bytes 4612
  159.3 24.8 %collective-permute-start.1 = (bf16[12,128,384]{2,1,0:T(8,128)(2,1)}, bf16[12,128,384]{2,1,0:T(8,128)(2,1)}, u32[]{:S(2)}, u32[]{:S(2)}) collective-permute-start(bf16[12,128,384]{2,1,0:T(8,128)(2,1)} %get-tuple-element.22), channel_id=1, source_target_pairs={{12,0},{24,12},{36,24},{48,36},{60,48},{72,60},{84,72},{96,84},{10... | collective-permute-start | bytes 3538952 | tf_op jit(solution)/shard_map/ppermute | solution.py:14
  184.1 41.5 %all-to-all-start.2 = ((bf16[12,128,384]{2,1,0:T(8,128)(2,1)}), bf16[12,128,384]{2,1,0:T(8,128)(2,1)S(1)}, u32[]{:S(2)}, u32[]{:S(2)}) async-start(bf16[12,128,384]{2,1,0:T(8,128)(2,1)} %collective-permute-done.1), calls=%async_computation.2 | async-start | bytes 2359296 | tf_op jit(solution)/shard_map/all_to_all | solution.py:162

commit v10 on v8

--- a/solution.py
+++ b/solution.py
@@ -164,7 +164,10 @@
         )
         qk_sum = qk_sum + qk_part
         value_sum = value_sum + value_part
-    passed = to_tokens(pass_on(grad_in))
+    half = grad_in.shape[1] // 2
+    early = to_tokens(pass_on(grad_in[:, :half]))
+    late = pass_on(to_tokens(grad_in[:, half:]))
+    passed = jnp.concatenate([early, late], axis=0)
     return (passed[None], qk_sum[None], value_sum[None])
 
 

time: 227 us -> 223 us (0.982)
  the two profiles are of different devices: /device:TPU:64 before, /device:TPU:57 now
where the time goes in v10:
time: 223 us; the launch traced here: 221 us
  blocking collectives  81.5 us (37%)
  waiting for transfers between devices  57.6 us (26%)
  starting transfers between devices  38.3 us (17%)
  Pallas kernels  35.2 us (16%)
  local copies, waits for them, and re-layouts  5.66 us (3%)
    all_to_all x1, blocking collectives, to_heads(): return lax.all_to_all(block, 'tp', 0, 0, tiled=True)  81.5 us
    ppermute x3, waiting for transfers between devices, from_behind(): return lax.ppermute(block, axis, route)  44.9 us
    pallas_call x2, Pallas kernels, local_backward(): pl.pallas_call(attention_kernel, grid=(count,), in_specs=[tile_of(inputs,...  30.5 us
    all_to_all x2, starting transfers between devices, to_tokens(): back = lax.all_to_all(block, 'tp', 0, 0, tiled=True)  17.8 us
    ppermute x3, starting transfers between devices, from_behind(): return lax.ppermute(block, axis, route)  13.4 us
    all_to_all x2, waiting for transfers between devices, to_tokens(): back = lax.all_to_all(block, 'tp', 0, 0, tiled=True)  12.7 us
    all_to_all x1, starting transfers between devices, to_heads(): return lax.all_to_all(block, 'tp', 0, 0, tiled=True)  7.05 us
    pallas_call x1, Pallas kernels, split_blocks(): pl.pallas_call(split_kernel, grid=(parts // group,), in_specs=[pl.BlockSp...  4.62 us
  transfers between devices with their start and end apart: 6, of which 3 were waited for; matrix products, arithmetic and copies ran while one was open for 1% of the time, Pallas kernels for 7%

profile of v10, /device:TPU:57, one launch (start us, length us, event | category | flops | bytes accessed | tf_op | source)
XLA Modules:
  0.0 221.3 jit_solution(3871931435972018002)
XLA Ops:
  0.6 4.6 %shard_map.67 = (bf16[12,2,128,384]{3,2,1,0:T(8,128)(2,1)}, bf16[12,128,384]{2,1,0:T(8,128)(2,1)}) custom-call(bf16[2,128,4608]{2,1,0:T(8,128)(2,1)} %bitcast.10, bf16[128,4608]{1,0:T(8,128)(2,1)} %bitcast.15, bf16[2,128,4608]{2,1,0:T(8,128)(2,1)} %bitcast.11), custom_call_target="tpu_custom_call" | custom-call | tf_op jit(solution)/shard_map/pallas_call | solution.py:120
  5.3 81.5 %all_to_all.20.x_ref.u_ref = bf16[12,2,128,384]{3,2,1,0:T(8,128)(2,1)} all-to-all(bf16[12,2,128,384]{3,2,1,0:T(8,128)(2,1)} %get-tuple-element.12), channel_id=1, replica_groups=mesh['section'=64,'tp'=12] {'tp'}, dimensions={0} | all-to-all | bytes 4718592 | tf_op jit(solution)/shard_map/all_to_all | solution.py:141
  86.8 7.1 %all-to-all-start.1 = ((bf16[12,128,384]{2,1,0:T(8,128)(2,1)}), bf16[12,128,384]{2,1,0:T(8,128)(2,1)S(1)}, u32[]{:S(2)}, u32[]{:S(2)}) async-start(bf16[12,128,384]{2,1,0:T(8,128)(2,1)} %get-tuple-element.14), calls=%async_computation.1 | async-start | bytes 2359296 | tf_op jit(solution)/shard_map/all_to_all | solution.py:141
  93.9 1.3 constant_dynamic-slice_fusion
  95.1 15.3 %shard_map.68 = (bf16[12,128,384]{2,1,0:T(8,128)(2,1)}, f32[1,384]{1,0:T(1,128)}, f32[1,384]{1,0:T(1,128)}) custom-call(bf16[12,2,128,384]{3,2,1,0:T(8,128)(2,1)} %all_to_all.20.x_ref.u_ref, bf16[12,2,128,384]{3,2,1,0:T(8,128)(2,1)} %all_to_all.20.x_ref.u_ref, f32[1,384]{1,0:T(1,128)} %get-tuple-element.24.gq_ref, f32[1,384]{1,0:T(1,128)} %get-tuple-element.23.gv_ref), custom_call_target="tpu_custom_call" | custom-call | flops 1509949440 | bytes 3538944 | tf_op jit(solution)/shard_map/pallas_call | solution.py:85
  110.4 9.6 %collective-permute-start = (bf16[12,128,384]{2,1,0:T(8,128)(2,1)}, bf16[12,128,384]{2,1,0:T(8,128)(2,1)S(1)}, u32[]{:S(2)}, u32[]{:S(2)}) collective-permute-start(bf16[12,128,384]{2,1,0:T(8,128)(2,1)} %get-tuple-element.15), channel_id=1, source_target_pairs={{12,0},{24,12},{36,24},{48,36},{60,48},{72,60},{84,72},{96,84},{10... | collective-permute-start | bytes 3538952 | tf_op jit(solution)/shard_map/ppermute | solution.py:14
  120.0 22.7 %collective-permute-done.u_ref = bf16[12,128,384]{2,1,0:T(8,128)(2,1)S(1)} collective-permute-done((bf16[12,128,384]{2,1,0:T(8,128)(2,1)}, bf16[12,128,384]{2,1,0:T(8,128)(2,1)S(1)}, u32[]{:S(2)}, u32[]{:S(2)}) %collective-permute-start) | collective-permute-done | bytes 1179680 | tf_op jit(solution)/shard_map/ppermute | solution.py:14
  142.7 0.0 copy-start.5
  142.7 0.0 all-to-all-done.1.x_ref
  142.7 1.0 copy-done.5
  143.8 0.0 copy-start
  143.8 1.0 copy-done
  144.8 15.3 %shard_map.69 = (bf16[12,128,384]{2,1,0:T(8,128)(2,1)}, f32[1,384]{1,0:T(1,128)}, f32[1,384]{1,0:T(1,128)}) custom-call(bf16[12,128,384]{2,1,0:T(8,128)(2,1)} %copy-done, bf16[12,128,384]{2,1,0:T(8,128)(2,1)} %copy-done.5, f32[1,384]{1,0:T(1,128)} %get-tuple-element.24.gq_ref, f32[1,384]{1,0:T(1,128)} %get-tuple-element.23.gv_ref), custom_call_target="tpu_custom_call" | custom-call | flops 1509949440 | bytes 3538944 | tf_op jit(solution)/shard_map/pallas_call | solution.py:85
  160.1 2.2 fusion
  162.2 6.7 %all-to-all-start.3 = ((bf16[12,64,384]{2,1,0:T(8,128)(2,1)}), bf16[12,64,384]{2,1,0:T(8,128)(2,1)S(1)}, u32[]{:S(2)}, u32[]{:S(2)}) async-start(bf16[12,64,384]{2,1,0:T(8,128)(2,1)} %get-tuple-element.22), calls=%async_computation.3 | async-start | bytes 1179648 | tf_op jit(solution)/shard_map/all_to_all | solution.py:145
  169.0 0.0 copy-start.2
  169.0 0.0 copy-start.4
  169.0 0.0 copy-start.1
  169.0 0.0 copy-start.3
  169.0 1.9 collective-permute-start.1
  170.9 22.2 %collective-permute-done.1 = bf16[12,64,384]{2,1,0:T(8,128)(2,1)} collective-permute-done((bf16[12,64,384]{2,1,0:T(8,128)(2,1)S(1)}, bf16[12,64,384]{2,1,0:T(8,128)(2,1)}, u32[]{:S(2)}, u32[]{:S(2)}) %collective-permute-start.1) | collective-permute-done | bytes 589856 | tf_op jit(solution)/shard_map/ppermute | solution.py:14
  193.1 0.0 all-to-all-done.3
  193.1 11.1 %all-to-all-start.2 = ((bf16[12,64,384]{2,1,0:T(8,128)(2,1)}), bf16[12,64,384]{2,1,0:T(8,128)(2,1)S(1)}, u32[]{:S(2)}, u32[]{:S(2)}) async-start(bf16[12,64,384]{2,1,0:T(8,128)(2,1)} %collective-permute-done.1), calls=%async_computation.2 | async-start | bytes 1179648 | tf_op jit(solution)/shard_map/all_to_all | solution.py:145
  204.2 0.1 copy.10
  204.3 1.9 collective-permute-start.2
  206.2 0.0 copy-done.2
  206.2 0.0 copy-done.4
  206.2 0.6 add.13
  206.8 0.0 copy-done.1
  206.8 0.0 copy-done.3
  206.8 0.6 add.14
  207.4 12.7 %all-to-all-done.2 = bf16[12,64,384]{2,1,0:T(8,128)(2,1)S(1)} async-done(((bf16[12,64,384]{2,1,0:T(8,128)(2,1)}), bf16[12,64,384]{2,1,0:T(8,128)(2,1)S(1)}, u32[]{:S(2)}, u32[]{:S(2)}) %all-to-all-start.2) | async-done | bytes 589856 | tf_op jit(solution)/shard_map/all_to_all | solution.py:145
  220.1 0.1 copy.9
  220.2 0.0 collective-permute-done.2
  220.2 1.1 maximum_bitcast_fusion
Async XLA Ops:
  86.8 55.9 %all-to-all-start.1 = ((bf16[12,128,384]{2,1,0:T(8,128)(2,1)}), bf16[12,128,384]{2,1,0:T(8,128)(2,1)S(1)}, u32[]{:S(2)}, u32[]{:S(2)}) async-start(bf16[12,128,384]{2,1,0:T(8,128)(2,1)} %get-tuple-element.14), calls=%async_computation.1 | async-start | bytes 2359296 | tf_op jit(solution)/shard_map/all_to_all | solution.py:141
  110.4 32.3 %collective-permute-start = (bf16[12,128,384]{2,1,0:T(8,128)(2,1)}, bf16[12,128,384]{2,1,0:T(8,128)(2,1)S(1)}, u32[]{:S(2)}, u32[]{:S(2)}) collective-permute-start(bf16[12,128,384]{2,1,0:T(8,128)(2,1)} %get-tuple-element.15), channel_id=1, source_target_pairs={{12,0},{24,12},{36,24},{48,36},{60,48},{72,60},{84,72},{96,84},{10... | collective-permute-start | bytes 3538952 | tf_op jit(solution)/shard_map/ppermute | solution.py:14
  142.7 1.1 copy-start.5
  143.8 1.0 copy-start
  162.2 30.9 %all-to-all-start.3 = ((bf16[12,64,384]{2,1,0:T(8,128)(2,1)}), bf16[12,64,384]{2,1,0:T(8,128)(2,1)S(1)}, u32[]{:S(2)}, u32[]{:S(2)}) async-start(bf16[12,64,384]{2,1,0:T(8,128)(2,1)} %get-tuple-element.22), calls=%async_computation.3 | async-start | bytes 1179648 | tf_op jit(solution)/shard_map/all_to_all | solution.py:145
  169.0 37.3 %copy-start.2 = (f32[1,384]{1,0:T(1,128)S(1)}, f32[1,384]{1,0:T(1,128)}, u32[]{:S(2)}) copy-start(f32[1,384]{1,0:T(1,128)} %get-tuple-element.17) | copy-start | bytes 4612
  169.0 37.3 %copy-start.4 = (f32[1,384]{1,0:T(1,128)S(1)}, f32[1,384]{1,0:T(1,128)}, u32[]{:S(2)}) copy-start(f32[1,384]{1,0:T(1,128)} %get-tuple-element.18) | copy-start | bytes 4612
  169.0 37.8 %copy-start.1 = (f32[1,384]{1,0:T(1,128)S(1)}, f32[1,384]{1,0:T(1,128)}, u32[]{:S(2)}) copy-start(f32[1,384]{1,0:T(1,128)} %get-tuple-element.19) | copy-start | bytes 4612
  169.0 37.8 %copy-start.3 = (f32[1,384]{1,0:T(1,128)S(1)}, f32[1,384]{1,0:T(1,128)}, u32[]{:S(2)}) copy-start(f32[1,384]{1,0:T(1,128)} %get-tuple-element.20) | copy-start | bytes 4612
  169.0 24.1 %collective-permute-start.1 = (bf16[12,64,384]{2,1,0:T(8,128)(2,1)S(1)}, bf16[12,64,384]{2,1,0:T(8,128)(2,1)}, u32[]{:S(2)}, u32[]{:S(2)}) collective-permute-start(bf16[12,64,384]{2,1,0:T(8,128)(2,1)S(1)} %get-tuple-element.21), channel_id=1, source_target_pairs={{12,0},{24,12},{36,24},{48,36},{60,48},{72,60},{84,72},{96,84},{10... | collective-permute-start | bytes 1769480 | tf_op jit(solution)/shard_map/ppermute | solution.py:14
  193.1 27.0 %all-to-all-start.2 = ((bf16[12,64,384]{2,1,0:T(8,128)(2,1)}), bf16[12,64,384]{2,1,0:T(8,128)(2,1)S(1)}, u32[]{:S(2)}, u32[]{:S(2)}) async-start(bf16[12,64,384]{2,1,0:T(8,128)(2,1)} %collective-permute-done.1), calls=%async_computation.2 | async-start | bytes 1179648 | tf_op jit(solution)/shard_map/all_to_all | solution.py:145
  204.3 15.9 %collective-permute-start.2 = (bf16[64,4608]{1,0:T(8,128)(2,1)S(1)}, bf16[64,4608]{1,0:T(8,128)(2,1)S(1)}, u32[]{:S(2)}, u32[]{:S(2)}) collective-permute-start(bf16[64,4608]{1,0:T(8,128)(2,1)S(1)} %bitcast.16), channel_id=1, source_target_pairs={{12,0},{24,12},{36,24},{48,36},{60,48},{72,60},{84,72},{96,84},{10... | collective-permute-start | bytes 1769480 | tf_op jit(solution)/shard_map/ppermute | solution.py:14

commit v11 on v8

--- a/solution.py
+++ b/solution.py
@@ -53,7 +53,12 @@
         wide = x_ref[:, :, cols].reshape(SEQ_LEN, HEAD_DIM).astype(jnp.float32)
         up = u_ref[:, :, cols].reshape(SEQ_LEN, HEAD_DIM)
         grad_in, qk_part, value_part = attend_head(wide, up, gq_ref[:, cols], gv_ref[:, cols])
-        g_ref[:, :, cols] = grad_in.reshape(g_ref.shape[0], g_ref.shape[1], HEAD_DIM)
+        if len(g_ref.shape) == 4:
+            parts = grad_in.reshape(g_ref.shape[1], g_ref.shape[0], g_ref.shape[2], HEAD_DIM)
+            for r in range(g_ref.shape[0]):
+                g_ref[r, :, :, cols] = parts[:, r]
+        else:
+            g_ref[:, :, cols] = grad_in.reshape(g_ref.shape[0], g_ref.shape[1], HEAD_DIM)
 
         @pl.when(n == 0)
         def _():
@@ -76,19 +81,25 @@
     return pl.BlockSpec((2, None, half, width), lambda n: (n, slot, 0, 0))
 
 
-def local_backward(inputs, inputs_slot, upstream, upstream_slot, gain_qk, gain_value):
+def local_backward(inputs, inputs_slot, upstream, upstream_slot, gain_qk, gain_value, halves=False):
     blocks, half, width = upstream.shape[0], upstream.shape[-2], upstream.shape[-1]
     heads = width // HEAD_DIM
     count = blocks * half // SEQ_LEN
     gain = pl.BlockSpec((1, width), lambda n: (0, 0))
     flops = heads * count * 5 * 2 * SEQ_LEN * SEQ_LEN * HEAD_DIM
+    if halves:
+        grad_shape = (2, blocks, half // 2, width)
+        grad_spec = pl.BlockSpec((2, 2, half // 2, width), lambda n: (0, n, 0, 0))
+    else:
+        grad_shape = (blocks, half, width)
+        grad_spec = tile_of(upstream, None)
     grad_in, qk_part, value_part = pl.pallas_call(
         attention_kernel,
         grid=(count,),
         in_specs=[tile_of(inputs, inputs_slot), tile_of(upstream, upstream_slot), gain, gain],
-        out_specs=[tile_of(upstream, None), gain, gain],
+        out_specs=[grad_spec, gain, gain],
         out_shape=[
-            jax.ShapeDtypeStruct((blocks, half, width), jnp.bfloat16),
+            jax.ShapeDtypeStruct(grad_shape, jnp.bfloat16),
             jax.ShapeDtypeStruct((1, width), jnp.float32),
             jax.ShapeDtypeStruct((1, width), jnp.float32),
         ],
@@ -153,6 +164,7 @@
     gain_qk = lax.dynamic_slice_in_dim(qk_gain[0], offset, local_width)
     gain_value = lax.dynamic_slice_in_dim(value_gain[0], offset, local_width)
     first, later = split_blocks(saved_inputs, incoming)
+    first, gain_qk, gain_value = lax.optimization_barrier((first, gain_qk, gain_value))
     first = to_heads(first)
     grad_in, qk_sum, value_sum = local_backward(first, 0, first, 1, gain_qk, gain_value)
     for t in range(1, tick_count):
@@ -160,11 +172,13 @@
         inputs_heads = to_heads(later)
         upstream = pass_on(grad_in)
         grad_in, qk_part, value_part = local_backward(
-            inputs_heads, None, upstream, None, gain_qk, gain_value
+            inputs_heads, None, upstream, None, gain_qk, gain_value, halves=t == tick_count - 1
         )
         qk_sum = qk_sum + qk_part
         value_sum = value_sum + value_part
-    passed = to_tokens(pass_on(grad_in))
+    early = to_tokens(pass_on(grad_in[0]))
+    late = pass_on(to_tokens(grad_in[1]))
+    passed = jnp.concatenate([early, late], axis=0)
     return (passed[None], qk_sum[None], value_sum[None])
 
 

time: 227 us -> 222 us (0.978)
  the two profiles are of different devices: /device:TPU:64 before, /device:TPU:57 now
where the time goes in v11:
time: 222 us; the launch traced here: 218 us
  blocking collectives  81.5 us (37%)
  waiting for transfers between devices  57.5 us (26%)
  Pallas kernels  35.1 us (16%)
  starting transfers between devices  35.1 us (16%)
  local copies, waits for them, and re-layouts  6.21 us (3%)
  other arithmetic  2.22 us (1%)
    all_to_all x1, blocking collectives, to_heads(): return lax.all_to_all(block, 'tp', 0, 0, tiled=True)  81.5 us
    ppermute x3, waiting for transfers between devices, from_behind(): return lax.ppermute(block, axis, route)  47.3 us
    pallas_call x2, Pallas kernels, local_backward(): pl.pallas_call(attention_kernel, grid=(count,), in_specs=[tile_of(inputs,...  30.5 us
    all_to_all x2, starting transfers between devices, to_tokens(): back = lax.all_to_all(block, 'tp', 0, 0, tiled=True)  14.6 us
    ppermute x3, starting transfers between devices, from_behind(): return lax.ppermute(block, axis, route)  13.4 us
    all_to_all x2, waiting for transfers between devices, to_tokens(): back = lax.all_to_all(block, 'tp', 0, 0, tiled=True)  10.2 us
    all_to_all x1, starting transfers between devices, to_heads(): return lax.all_to_all(block, 'tp', 0, 0, tiled=True)  7.05 us
    pallas_call x1, Pallas kernels, split_blocks(): pl.pallas_call(split_kernel, grid=(parts // group,), in_specs=[pl.BlockSp...  4.62 us
  transfers between devices with their start and end apart: 6, of which 4 were waited for; matrix products, arithmetic and copies ran while one was open for 1% of the time, Pallas kernels for 7%

profile of v11, /device:TPU:57, one launch (start us, length us, event | category | flops | bytes accessed | tf_op | source)
XLA Modules:
  0.0 218.5 jit_solution(14319621349653745905)
XLA Ops:
  0.6 4.6 %shard_map.67 = (bf16[12,2,128,384]{3,2,1,0:T(8,128)(2,1)}, bf16[12,128,384]{2,1,0:T(8,128)(2,1)}) custom-call(bf16[2,128,4608]{2,1,0:T(8,128)(2,1)} %bitcast.14, bf16[128,4608]{1,0:T(8,128)(2,1)} %bitcast.19, bf16[2,128,4608]{2,1,0:T(8,128)(2,1)} %bitcast.15), custom_call_target="tpu_custom_call" | custom-call | tf_op jit(solution)/shard_map/pallas_call | solution.py:131
  5.3 0.7 dynamic-slice_reduce_fusion
  6.0 81.5 %all_to_all.20.x_ref.u_ref = bf16[12,2,128,384]{3,2,1,0:T(8,128)(2,1)} all-to-all(bf16[12,2,128,384]{3,2,1,0:T(8,128)(2,1)} %get-tuple-element.16), channel_id=1, replica_groups=mesh['section'=64,'tp'=12] {'tp'}, dimensions={0} | all-to-all | bytes 4718592 | tf_op jit(solution)/shard_map/all_to_all | solution.py:152
  87.5 7.1 %all-to-all-start.1 = ((bf16[12,128,384]{2,1,0:T(8,128)(2,1)}), bf16[12,128,384]{2,1,0:T(8,128)(2,1)S(1)}, u32[]{:S(2)}, u32[]{:S(2)}) async-start(bf16[12,128,384]{2,1,0:T(8,128)(2,1)} %get-tuple-element.18), calls=%async_computation.1 | async-start | bytes 2359296 | tf_op jit(solution)/shard_map/all_to_all | solution.py:152
  94.6 0.6 broadcast_in_dim.6.gq_ref
  95.2 0.6 broadcast_in_dim.14.gv_ref
  95.7 15.3 %shard_map.68 = (bf16[12,128,384]{2,1,0:T(8,128)(2,1)}, f32[1,384]{1,0:T(1,128)}, f32[1,384]{1,0:T(1,128)}) custom-call(bf16[12,2,128,384]{3,2,1,0:T(8,128)(2,1)} %all_to_all.20.x_ref.u_ref, bf16[12,2,128,384]{3,2,1,0:T(8,128)(2,1)} %all_to_all.20.x_ref.u_ref, f32[1,384]{1,0:T(1,128)} %broadcast_in_dim.6.gq_ref, f32[1,384]{1,0:T(1,128)} %broadcast_in_dim.14.gv_ref), custom_call_target="tpu_custom_call" | custom-call | flops 1509949440 | bytes 3538944 | tf_op jit(solution)/shard_map/pallas_call | solution.py:96
  111.0 9.6 %collective-permute-start = (bf16[12,128,384]{2,1,0:T(8,128)(2,1)}, bf16[12,128,384]{2,1,0:T(8,128)(2,1)S(1)}, u32[]{:S(2)}, u32[]{:S(2)}) collective-permute-start(bf16[12,128,384]{2,1,0:T(8,128)(2,1)} %get-tuple-element.21), channel_id=1, source_target_pairs={{12,0},{24,12},{36,24},{48,36},{60,48},{72,60},{84,72},{96,84},{10... | collective-permute-start | bytes 3538952 | tf_op jit(solution)/shard_map/ppermute | solution.py:14
  120.6 22.9 %collective-permute-done.u_ref = bf16[12,128,384]{2,1,0:T(8,128)(2,1)S(1)} collective-permute-done((bf16[12,128,384]{2,1,0:T(8,128)(2,1)}, bf16[12,128,384]{2,1,0:T(8,128)(2,1)S(1)}, u32[]{:S(2)}, u32[]{:S(2)}) %collective-permute-start) | collective-permute-done | bytes 1179680 | tf_op jit(solution)/shard_map/ppermute | solution.py:14
  143.5 0.0 copy-start.5
  143.5 0.0 all-to-all-done.1.x_ref
  143.5 1.0 copy-done.5
  144.5 0.0 copy-start
  144.5 1.0 copy-done
  145.5 15.3 %shard_map.69 = (bf16[2,12,64,384]{3,2,1,0:T(8,128)(2,1)}, f32[1,384]{1,0:T(1,128)}, f32[1,384]{1,0:T(1,128)}) custom-call(bf16[12,128,384]{2,1,0:T(8,128)(2,1)} %copy-done, bf16[12,128,384]{2,1,0:T(8,128)(2,1)} %copy-done.5, f32[1,384]{1,0:T(1,128)} %broadcast_in_dim.6.gq_ref, f32[1,384]{1,0:T(1,128)} %broadcast_in_dim.14.gv_ref), custom_call_target="tpu_custom_call" | custom-call | flops 1509949440 | bytes 3538944 | tf_op jit(solution)/shard_map/pallas_call | solution.py:96
  160.8 2.2 slice_bitcast_fusion.1
  163.0 6.7 %all-to-all-start.3 = ((bf16[12,64,384]{2,1,0:T(8,128)(2,1)}), bf16[12,64,384]{2,1,0:T(8,128)(2,1)S(1)}, u32[]{:S(2)}, u32[]{:S(2)}) async-start(bf16[12,64,384]{2,1,0:T(8,128)(2,1)} %get-tuple-element.28), calls=%async_computation.3 | async-start | bytes 1179648 | tf_op jit(solution)/shard_map/all_to_all | solution.py:156
  169.7 0.0 copy-start.2
  169.7 0.0 copy-start.4
  169.7 0.0 copy-start.1
  169.7 0.0 copy-start.3
  169.7 1.9 collective-permute-start.1
  171.7 21.9 %collective-permute-done.1 = bf16[12,64,384]{2,1,0:T(8,128)(2,1)} collective-permute-done((bf16[12,64,384]{2,1,0:T(8,128)(2,1)S(1)}, bf16[12,64,384]{2,1,0:T(8,128)(2,1)}, u32[]{:S(2)}, u32[]{:S(2)}) %collective-permute-start.1) | collective-permute-done | bytes 589856 | tf_op jit(solution)/shard_map/ppermute | solution.py:14
  193.5 0.0 all-to-all-done.3
  193.5 7.9 %all-to-all-start.2 = ((bf16[12,64,384]{2,1,0:T(8,128)(2,1)}), bf16[12,64,384]{2,1,0:T(8,128)(2,1)S(1)}, u32[]{:S(2)}, u32[]{:S(2)}) async-start(bf16[12,64,384]{2,1,0:T(8,128)(2,1)} %collective-permute-done.1), calls=%async_computation.2 | async-start | bytes 1179648 | tf_op jit(solution)/shard_map/all_to_all | solution.py:156
  201.4 0.1 copy.10
  201.5 1.9 collective-permute-start.2
  203.4 0.0 copy-done.2
  203.5 0.0 copy-done.4
  203.5 0.6 add.14
  204.0 0.0 copy-done.1
  204.0 0.0 copy-done.3
  204.0 0.6 add.13
  204.6 10.2 %all-to-all-done.2 = bf16[12,64,384]{2,1,0:T(8,128)(2,1)S(1)} async-done(((bf16[12,64,384]{2,1,0:T(8,128)(2,1)}), bf16[12,64,384]{2,1,0:T(8,128)(2,1)S(1)}, u32[]{:S(2)}, u32[]{:S(2)}) %all-to-all-start.2) | async-done | bytes 589856 | tf_op jit(solution)/shard_map/all_to_all | solution.py:156
  214.8 0.1 copy.9
  214.9 2.5 %collective-permute-done.2 = bf16[64,4608]{1,0:T(8,128)(2,1)S(1)} collective-permute-done((bf16[64,4608]{1,0:T(8,128)(2,1)S(1)}, bf16[64,4608]{1,0:T(8,128)(2,1)S(1)}, u32[]{:S(2)}, u32[]{:S(2)}) %collective-permute-start.2) | collective-permute-done | bytes 589856 | tf_op jit(solution)/shard_map/ppermute | solution.py:14
  217.4 1.1 maximum_bitcast_fusion
Async XLA Ops:
  87.5 55.9 %all-to-all-start.1 = ((bf16[12,128,384]{2,1,0:T(8,128)(2,1)}), bf16[12,128,384]{2,1,0:T(8,128)(2,1)S(1)}, u32[]{:S(2)}, u32[]{:S(2)}) async-start(bf16[12,128,384]{2,1,0:T(8,128)(2,1)} %get-tuple-element.18), calls=%async_computation.1 | async-start | bytes 2359296 | tf_op jit(solution)/shard_map/all_to_all | solution.py:152
  111.0 32.5 %collective-permute-start = (bf16[12,128,384]{2,1,0:T(8,128)(2,1)}, bf16[12,128,384]{2,1,0:T(8,128)(2,1)S(1)}, u32[]{:S(2)}, u32[]{:S(2)}) collective-permute-start(bf16[12,128,384]{2,1,0:T(8,128)(2,1)} %get-tuple-element.21), channel_id=1, source_target_pairs={{12,0},{24,12},{36,24},{48,36},{60,48},{72,60},{84,72},{96,84},{10... | collective-permute-start | bytes 3538952 | tf_op jit(solution)/shard_map/ppermute | solution.py:14
  143.5 1.0 copy-start.5
  144.5 1.0 copy-start
  163.0 30.6 %all-to-all-start.3 = ((bf16[12,64,384]{2,1,0:T(8,128)(2,1)}), bf16[12,64,384]{2,1,0:T(8,128)(2,1)S(1)}, u32[]{:S(2)}, u32[]{:S(2)}) async-start(bf16[12,64,384]{2,1,0:T(8,128)(2,1)} %get-tuple-element.28), calls=%async_computation.3 | async-start | bytes 1179648 | tf_op jit(solution)/shard_map/all_to_all | solution.py:156
  169.7 33.7 %copy-start.2 = (f32[1,384]{1,0:T(1,128)S(1)}, f32[1,384]{1,0:T(1,128)}, u32[]{:S(2)}) copy-start(f32[1,384]{1,0:T(1,128)} %get-tuple-element.25) | copy-start | bytes 4612
  169.7 33.7 %copy-start.4 = (f32[1,384]{1,0:T(1,128)S(1)}, f32[1,384]{1,0:T(1,128)}, u32[]{:S(2)}) copy-start(f32[1,384]{1,0:T(1,128)} %get-tuple-element.26) | copy-start | bytes 4612
  169.7 34.3 %copy-start.1 = (f32[1,384]{1,0:T(1,128)S(1)}, f32[1,384]{1,0:T(1,128)}, u32[]{:S(2)}) copy-start(f32[1,384]{1,0:T(1,128)} %get-tuple-element.23) | copy-start | bytes 4612
  169.7 34.3 %copy-start.3 = (f32[1,384]{1,0:T(1,128)S(1)}, f32[1,384]{1,0:T(1,128)}, u32[]{:S(2)}) copy-start(f32[1,384]{1,0:T(1,128)} %get-tuple-element.24) | copy-start | bytes 4612
  169.7 23.8 %collective-permute-start.1 = (bf16[12,64,384]{2,1,0:T(8,128)(2,1)S(1)}, bf16[12,64,384]{2,1,0:T(8,128)(2,1)}, u32[]{:S(2)}, u32[]{:S(2)}) collective-permute-start(bf16[12,64,384]{2,1,0:T(8,128)(2,1)S(1)} %get-tuple-element.27), channel_id=1, source_target_pairs={{12,0},{24,12},{36,24},{48,36},{60,48},{72,60},{84,72},{96,84},{10... | collective-permute-start | bytes 1769480 | tf_op jit(solution)/shard_map/ppermute | solution.py:14
  193.5 21.3 %all-to-all-start.2 = ((bf16[12,64,384]{2,1,0:T(8,128)(2,1)}), bf16[12,64,384]{2,1,0:T(8,128)(2,1)S(1)}, u32[]{:S(2)}, u32[]{:S(2)}) async-start(bf16[12,64,384]{2,1,0:T(8,128)(2,1)} %collective-permute-done.1), calls=%async_computation.2 | async-start | bytes 1179648 | tf_op jit(solution)/shard_map/all_to_all | solution.py:156
  201.5 15.8 %collective-permute-start.2 = (bf16[64,4608]{1,0:T(8,128)(2,1)S(1)}, bf16[64,4608]{1,0:T(8,128)(2,1)S(1)}, u32[]{:S(2)}, u32[]{:S(2)}) collective-permute-start(bf16[64,4608]{1,0:T(8,128)(2,1)S(1)} %bitcast.20), channel_id=1, source_target_pairs={{12,0},{24,12},{36,24},{48,36},{60,48},{72,60},{84,72},{96,84},{10... | collective-permute-start | bytes 1769480 | tf_op jit(solution)/shard_map/ppermute | solution.py:14

commit v12 on v11

--- a/solution.py
+++ b/solution.py
@@ -1,3 +1,5 @@
+import functools
+
 import jax
 import jax.numpy as jnp
 from jax import lax
@@ -45,13 +47,20 @@
     return grad_in, qk_part, value_part
 
 
-def attention_kernel(x_ref, u_ref, gq_ref, gv_ref, g_ref, qs_ref, vs_ref):
+def attention_kernel(x_ref, u_ref, *refs, split=0):
     n = pl.program_id(0)
+    if split:
+        ub_ref, gq_ref, gv_ref, g_ref, qs_ref, vs_ref = refs
+    else:
+        gq_ref, gv_ref, g_ref, qs_ref, vs_ref = refs
     heads = g_ref.shape[-1] // HEAD_DIM
     for h in range(heads):
         cols = slice(h * HEAD_DIM, (h + 1) * HEAD_DIM)
         wide = x_ref[:, :, cols].reshape(SEQ_LEN, HEAD_DIM).astype(jnp.float32)
-        up = u_ref[:, :, cols].reshape(SEQ_LEN, HEAD_DIM)
+        up = u_ref[:, :, cols]
+        if split:
+            up = jnp.where(n < split, up, ub_ref[:, :, cols])
+        up = up.reshape(SEQ_LEN, HEAD_DIM)
         grad_in, qk_part, value_part = attend_head(wide, up, gq_ref[:, cols], gv_ref[:, cols])
         if len(g_ref.shape) == 4:
             parts = grad_in.reshape(g_ref.shape[1], g_ref.shape[0], g_ref.shape[2], HEAD_DIM)
@@ -74,19 +83,33 @@
 INTERPRET = False
 
 
-def tile_of(array, slot):
+def tile_of(array, slot, base=0):
     half, width = array.shape[-2], array.shape[-1]
     if slot is None:
-        return pl.BlockSpec((2, half, width), lambda n: (n, 0, 0))
-    return pl.BlockSpec((2, None, half, width), lambda n: (n, slot, 0, 0))
-
-
-def local_backward(inputs, inputs_slot, upstream, upstream_slot, gain_qk, gain_value, halves=False):
-    blocks, half, width = upstream.shape[0], upstream.shape[-2], upstream.shape[-1]
+        return pl.BlockSpec((2, half, width), lambda n: (n + base, 0, 0))
+    return pl.BlockSpec((2, None, half, width), lambda n: (n + base, slot, 0, 0))
+
+
+def local_backward(inputs, inputs_slot, upstream, upstream_slot, gain_qk, gain_value, halves=False,
+                   base=0, count=None, upstream_b=None):
+    half, width = upstream.shape[-2], upstream.shape[-1]
     heads = width // HEAD_DIM
-    count = blocks * half // SEQ_LEN
+    if count is None:
+        count = inputs.shape[0] * half // SEQ_LEN
+    blocks = count * SEQ_LEN // half
     gain = pl.BlockSpec((1, width), lambda n: (0, 0))
     flops = heads * count * 5 * 2 * SEQ_LEN * SEQ_LEN * HEAD_DIM
+    if upstream_b is None:
+        up_specs = [tile_of(inputs, inputs_slot, base), tile_of(upstream, upstream_slot, base)]
+        up_args = (inputs, upstream)
+    else:
+        last = upstream.shape[0] // 2 - 1
+        up_specs = [
+            tile_of(inputs, inputs_slot),
+            pl.BlockSpec((2, half, width), lambda n: (jnp.minimum(n, last), 0, 0)),
+            pl.BlockSpec((2, half, width), lambda n: (jnp.maximum(n - last - 1, 0), 0, 0)),
+        ]
+        up_args = (inputs, upstream, upstream_b)
     if halves:
         grad_shape = (2, blocks, half // 2, width)
         grad_spec = pl.BlockSpec((2, 2, half // 2, width), lambda n: (0, n, 0, 0))
@@ -94,9 +117,9 @@
         grad_shape = (blocks, half, width)
         grad_spec = tile_of(upstream, None)
     grad_in, qk_part, value_part = pl.pallas_call(
-        attention_kernel,
+        functools.partial(attention_kernel, split=0 if upstream_b is None else upstream.shape[0] // 2),
         grid=(count,),
-        in_specs=[tile_of(inputs, inputs_slot), tile_of(upstream, upstream_slot), gain, gain],
+        in_specs=up_specs + [gain, gain],
         out_specs=[grad_spec, gain, gain],
         out_shape=[
             jax.ShapeDtypeStruct(grad_shape, jnp.bfloat16),
@@ -109,7 +132,7 @@
             bytes_accessed=3 * blocks * half * width * 2,
         ),
         interpret=INTERPRET,
-    )(inputs, upstream, gain_qk[None], gain_value[None])
+    )(*up_args, gain_qk[None], gain_value[None])
     return grad_in, qk_part[0], value_part[0]
 
 
@@ -166,13 +189,21 @@
     first, later = split_blocks(saved_inputs, incoming)
     first, gain_qk, gain_value = lax.optimization_barrier((first, gain_qk, gain_value))
     first = to_heads(first)
-    grad_in, qk_sum, value_sum = local_backward(first, 0, first, 1, gain_qk, gain_value)
+    count = first.shape[0] * first.shape[-2] // SEQ_LEN
+    part = count // 2
+    grad_a, qk_a, value_a = local_backward(first, 0, first, 1, gain_qk, gain_value, base=0, count=part)
+    upstream_a = pass_on(grad_a)
+    grad_b, qk_b, value_b = local_backward(
+        first, 0, first, 1, gain_qk, gain_value, base=part, count=count - part
+    )
+    upstream_b = pass_on(grad_b)
+    qk_sum = qk_a + qk_b
+    value_sum = value_a + value_b
     for t in range(1, tick_count):
         first, later = lax.optimization_barrier((first, later))
         inputs_heads = to_heads(later)
-        upstream = pass_on(grad_in)
         grad_in, qk_part, value_part = local_backward(
-            inputs_heads, None, upstream, None, gain_qk, gain_value, halves=t == tick_count - 1
+            inputs_heads, None, upstream_a, None, gain_qk, gain_value, halves=True, upstream_b=upstream_b
         )
         qk_sum = qk_sum + qk_part
         value_sum = value_sum + value_part

time: 222 us -> 222 us (level)
  waiting for transfers between devices: 57.5 us -> 51.8 us
  starting transfers between devices: 35.1 us -> 39.3 us
    ppermute x3 -> x4, waiting for transfers between devices: 47.3 us -> 41.6 us  [from_behind(): return lax.ppermute(block, axis, route)]
    all_to_all x2, starting transfers between devices: 14.6 us -> 16.9 us  [to_tokens(): back = lax.all_to_all(block, 'tp', 0, 0, tiled=True)]
    ppermute x3 -> x4, starting transfers between devices: 13.4 us -> 15.3 us  [from_behind(): return lax.ppermute(block, axis, route)]
    pallas_call x2 -> x3, Pallas kernels: 30.5 us -> 32.4 us  [local_backward(): pl.pallas_call(functools.partial(attention_kernel, split=0 if upstream_b...]
  transfers between devices with their start and end apart: 6 -> 7, of which waited for: 4 -> 5; matrix products, arithmetic and copies ran while one was open for 1% -> 1% of each run, Pallas kernels for 7% -> 8%
where the time goes in v12:
time: 222 us; the launch traced here: 219 us
  blocking collectives  81.5 us (37%)
  waiting for transfers between devices  51.8 us (23%)
  starting transfers between devices  39.3 us (18%)
  Pallas kernels  37 us (17%)
  local copies, waits for them, and re-layouts  6 us (3%)
  other arithmetic  2.22 us (1%)
    all_to_all x1, blocking collectives, to_heads(): return lax.all_to_all(block, 'tp', 0, 0, tiled=True)  81.5 us
    ppermute x4, waiting for transfers between devices, from_behind(): return lax.ppermute(block, axis, route)  41.6 us
    pallas_call x3, Pallas kernels, local_backward(): pl.pallas_call(functools.partial(attention_kernel, split=0 if upstream_b...  32.4 us
    all_to_all x2, starting transfers between devices, to_tokens(): back = lax.all_to_all(block, 'tp', 0, 0, tiled=True)  16.9 us
    ppermute x4, starting transfers between devices, from_behind(): return lax.ppermute(block, axis, route)  15.3 us
    all_to_all x2, waiting for transfers between devices, to_tokens(): back = lax.all_to_all(block, 'tp', 0, 0, tiled=True)  10.2 us
    all_to_all x1, starting transfers between devices, to_heads(): return lax.all_to_all(block, 'tp', 0, 0, tiled=True)  7.05 us
    pallas_call x1, Pallas kernels, split_blocks(): pl.pallas_call(split_kernel, grid=(parts // group,), in_specs=[pl.BlockSp...  4.62 us
  transfers between devices with their start and end apart: 7, of which 5 were waited for; matrix products, arithmetic and copies ran while one was open for 1% of the time, Pallas kernels for 8%

profile of v12, /device:TPU:57, one launch (start us, length us, event | category | flops | bytes accessed | tf_op | source)
XLA Modules:
  0.0 218.7 jit_solution(15002966973244117353)
XLA Ops:
  0.6 4.6 %shard_map.67 = (bf16[12,2,128,384]{3,2,1,0:T(8,128)(2,1)}, bf16[12,128,384]{2,1,0:T(8,128)(2,1)}) custom-call(bf16[2,128,4608]{2,1,0:T(8,128)(2,1)} %bitcast.14, bf16[128,4608]{1,0:T(8,128)(2,1)} %bitcast.19, bf16[2,128,4608]{2,1,0:T(8,128)(2,1)} %bitcast.15), custom_call_target="tpu_custom_call" | custom-call | tf_op jit(solution)/shard_map/pallas_call | solution.py:154
  5.3 0.7 dynamic-slice_reduce_fusion
  6.0 81.5 %all_to_all.20.x_ref.u_ref = bf16[12,2,128,384]{3,2,1,0:T(8,128)(2,1)} all-to-all(bf16[12,2,128,384]{3,2,1,0:T(8,128)(2,1)} %get-tuple-element.19), channel_id=1, replica_groups=mesh['section'=64,'tp'=12] {'tp'}, dimensions={0} | all-to-all | bytes 4718592 | tf_op jit(solution)/shard_map/all_to_all | solution.py:175
  87.5 7.1 %all-to-all-start.1 = ((bf16[12,128,384]{2,1,0:T(8,128)(2,1)}), bf16[12,128,384]{2,1,0:T(8,128)(2,1)S(1)}, u32[]{:S(2)}, u32[]{:S(2)}) async-start(bf16[12,128,384]{2,1,0:T(8,128)(2,1)} %get-tuple-element.21), calls=%async_computation.1 | async-start | bytes 2359296 | tf_op jit(solution)/shard_map/all_to_all | solution.py:175
  94.6 0.6 broadcast_in_dim.6.refs_0_.refs_1_
  95.2 0.6 broadcast_in_dim.7.refs_1_.refs_2_
  95.7 8.5 %shard_map.69 = (bf16[6,128,384]{2,1,0:T(8,128)(2,1)}, f32[1,384]{1,0:T(1,128)}, f32[1,384]{1,0:T(1,128)}) custom-call(bf16[12,2,128,384]{3,2,1,0:T(8,128)(2,1)} %all_to_all.20.x_ref.u_ref, bf16[12,2,128,384]{3,2,1,0:T(8,128)(2,1)} %all_to_all.20.x_ref.u_ref, f32[1,384]{1,0:T(1,128)} %broadcast_in_dim.6.refs_0_.refs_1_, f32[1,384]{1,0:T(1,128)} %broadcast_in_dim.7.refs_1_.refs_2_), custom_call_target="tpu_custom_call" | custom-call | flops 754974720 | bytes 1769472 | tf_op jit(solution)/shard_map/pallas_call | solution.py:119
  104.2 9.6 %collective-permute-start.1 = (bf16[6,128,384]{2,1,0:T(8,128)(2,1)}, bf16[6,128,384]{2,1,0:T(8,128)(2,1)S(1)}, u32[]{:S(2)}, u32[]{:S(2)}) collective-permute-start(bf16[6,128,384]{2,1,0:T(8,128)(2,1)} %get-tuple-element.25), channel_id=1, source_target_pairs={{12,0},{24,12},{36,24},{48,36},{60,48},{72,60},{84,72},{96,84},{10... | collective-permute-start | bytes 1769480 | tf_op jit(solution)/shard_map/ppermute | solution.py:16
  113.8 8.5 %shard_map.68 = (bf16[6,128,384]{2,1,0:T(8,128)(2,1)}, f32[1,384]{1,0:T(1,128)}, f32[1,384]{1,0:T(1,128)}) custom-call(bf16[12,2,128,384]{3,2,1,0:T(8,128)(2,1)} %all_to_all.20.x_ref.u_ref, bf16[12,2,128,384]{3,2,1,0:T(8,128)(2,1)} %all_to_all.20.x_ref.u_ref, f32[1,384]{1,0:T(1,128)} %broadcast_in_dim.6.refs_0_.refs_1_, f32[1,384]{1,0:T(1,128)} %broadcast_in_dim.7.refs_1_.refs_2_), custom_call_target="tpu_custom_call" | custom-call | flops 754974720 | bytes 1769472 | tf_op jit(solution)/shard_map/pallas_call | solution.py:119
  122.3 1.9 collective-permute-start
  124.2 13.0 %collective-permute-done.1.refs_0_ = bf16[6,128,384]{2,1,0:T(8,128)(2,1)S(1)} collective-permute-done((bf16[6,128,384]{2,1,0:T(8,128)(2,1)}, bf16[6,128,384]{2,1,0:T(8,128)(2,1)S(1)}, u32[]{:S(2)}, u32[]{:S(2)}) %collective-permute-start.1) | collective-permute-done | bytes 589856 | tf_op jit(solution)/shard_map/ppermute | solution.py:16
  137.2 0.0 copy-start.7
  137.2 6.3 %collective-permute-done.u_ref = bf16[6,128,384]{2,1,0:T(8,128)(2,1)S(1)} collective-permute-done((bf16[6,128,384]{2,1,0:T(8,128)(2,1)}, bf16[6,128,384]{2,1,0:T(8,128)(2,1)S(1)}, u32[]{:S(2)}, u32[]{:S(2)}) %collective-permute-start) | collective-permute-done | bytes 589856 | tf_op jit(solution)/shard_map/ppermute | solution.py:16
  143.5 0.0 copy-start.8
  143.5 0.0 all-to-all-done.1.x_ref
  143.5 0.0 copy-done.7
  143.5 0.8 copy-done.8
  144.3 0.0 copy-start
  144.3 1.0 copy-done
  145.3 15.4 %shard_map.70 = (bf16[2,12,64,384]{3,2,1,0:T(8,128)(2,1)}, f32[1,384]{1,0:T(1,128)}, f32[1,384]{1,0:T(1,128)}) custom-call(bf16[12,128,384]{2,1,0:T(8,128)(2,1)} %copy-done, bf16[6,128,384]{2,1,0:T(8,128)(2,1)} %copy-done.8, bf16[6,128,384]{2,1,0:T(8,128)(2,1)} %copy-done.7, f32[1,384]{1,0:T(1,128)} %broadcast_in_dim.6.refs_0_.refs_1_, ...), custom_call_target="tpu_custom_call" | custom-call | flops 1509949440 | bytes 3538944 | tf_op jit(solution)/shard_map/pallas_call | solution.py:119
  160.8 2.2 slice_bitcast_fusion.1
  162.9 6.7 %all-to-all-start.3 = ((bf16[12,64,384]{2,1,0:T(8,128)(2,1)}), bf16[12,64,384]{2,1,0:T(8,128)(2,1)S(1)}, u32[]{:S(2)}, u32[]{:S(2)}) async-start(bf16[12,64,384]{2,1,0:T(8,128)(2,1)} %get-tuple-element.34), calls=%async_computation.3 | async-start | bytes 1179648 | tf_op jit(solution)/shard_map/all_to_all | solution.py:179
  169.7 0.0 copy-start.2
  169.7 0.0 copy-start.4
  169.7 0.0 copy-start.6
  169.7 0.0 copy-start.1
  169.7 0.0 copy-start.3
  169.7 0.0 copy-start.5
  169.7 1.9 collective-permute-start.2
  171.7 19.3 %collective-permute-done.2 = bf16[12,64,384]{2,1,0:T(8,128)(2,1)} collective-permute-done((bf16[12,64,384]{2,1,0:T(8,128)(2,1)S(1)}, bf16[12,64,384]{2,1,0:T(8,128)(2,1)}, u32[]{:S(2)}, u32[]{:S(2)}) %collective-permute-start.2) | collective-permute-done | bytes 589856 | tf_op jit(solution)/shard_map/ppermute | solution.py:16
  190.9 0.0 all-to-all-done.3
  190.9 10.2 %all-to-all-start.2 = ((bf16[12,64,384]{2,1,0:T(8,128)(2,1)}), bf16[12,64,384]{2,1,0:T(8,128)(2,1)S(1)}, u32[]{:S(2)}, u32[]{:S(2)}) async-start(bf16[12,64,384]{2,1,0:T(8,128)(2,1)} %collective-permute-done.2), calls=%async_computation.2 | async-start | bytes 1179648 | tf_op jit(solution)/shard_map/all_to_all | solution.py:179
  201.1 0.1 copy.10
  201.2 1.9 collective-permute-start.3
  203.1 0.0 copy-done.2
  203.1 0.0 copy-done.4
  203.2 0.0 copy-done.6
  203.2 0.6 add_add_fusion
  203.7 0.0 copy-done.1
  203.7 0.0 copy-done.3
  203.7 0.0 copy-done.5
  203.7 0.6 add_add_fusion.1
  204.3 10.2 %all-to-all-done.2 = bf16[12,64,384]{2,1,0:T(8,128)(2,1)S(1)} async-done(((bf16[12,64,384]{2,1,0:T(8,128)(2,1)}), bf16[12,64,384]{2,1,0:T(8,128)(2,1)S(1)}, u32[]{:S(2)}, u32[]{:S(2)}) %all-to-all-start.2) | async-done | bytes 589856 | tf_op jit(solution)/shard_map/all_to_all | solution.py:179
  214.5 0.1 copy.9
  214.5 3.1 %collective-permute-done.3 = bf16[64,4608]{1,0:T(8,128)(2,1)S(1)} collective-permute-done((bf16[64,4608]{1,0:T(8,128)(2,1)S(1)}, bf16[64,4608]{1,0:T(8,128)(2,1)S(1)}, u32[]{:S(2)}, u32[]{:S(2)}) %collective-permute-start.3) | collective-permute-done | bytes 589856 | tf_op jit(solution)/shard_map/ppermute | solution.py:16
  217.6 1.1 maximum_bitcast_fusion
Async XLA Ops:
  87.5 55.9 %all-to-all-start.1 = ((bf16[12,128,384]{2,1,0:T(8,128)(2,1)}), bf16[12,128,384]{2,1,0:T(8,128)(2,1)S(1)}, u32[]{:S(2)}, u32[]{:S(2)}) async-start(bf16[12,128,384]{2,1,0:T(8,128)(2,1)} %get-tuple-element.21), calls=%async_computation.1 | async-start | bytes 2359296 | tf_op jit(solution)/shard_map/all_to_all | solution.py:175
  104.2 33.0 %collective-permute-start.1 = (bf16[6,128,384]{2,1,0:T(8,128)(2,1)}, bf16[6,128,384]{2,1,0:T(8,128)(2,1)S(1)}, u32[]{:S(2)}, u32[]{:S(2)}) collective-permute-start(bf16[6,128,384]{2,1,0:T(8,128)(2,1)} %get-tuple-element.25), channel_id=1, source_target_pairs={{12,0},{24,12},{36,24},{48,36},{60,48},{72,60},{84,72},{96,84},{10... | collective-permute-start | bytes 1769480 | tf_op jit(solution)/shard_map/ppermute | solution.py:16
  122.3 21.2 %collective-permute-start = (bf16[6,128,384]{2,1,0:T(8,128)(2,1)}, bf16[6,128,384]{2,1,0:T(8,128)(2,1)S(1)}, u32[]{:S(2)}, u32[]{:S(2)}) collective-permute-start(bf16[6,128,384]{2,1,0:T(8,128)(2,1)} %get-tuple-element.24), channel_id=1, source_target_pairs={{12,0},{24,12},{36,24},{48,36},{60,48},{72,60},{84,72},{96,84},{10... | collective-permute-start | bytes 1769480 | tf_op jit(solution)/shard_map/ppermute | solution.py:16
  137.2 6.3 %copy-start.7 = (bf16[6,128,384]{2,1,0:T(8,128)(2,1)}, bf16[6,128,384]{2,1,0:T(8,128)(2,1)S(1)}, u32[]{:S(2)}) copy-start(bf16[6,128,384]{2,1,0:T(8,128)(2,1)S(1)} %collective-permute-done.1.refs_0_) | copy-start | bytes 1769476
  143.5 0.8 copy-start.8
  144.3 1.0 copy-start
  162.9 28.0 %all-to-all-start.3 = ((bf16[12,64,384]{2,1,0:T(8,128)(2,1)}), bf16[12,64,384]{2,1,0:T(8,128)(2,1)S(1)}, u32[]{:S(2)}, u32[]{:S(2)}) async-start(bf16[12,64,384]{2,1,0:T(8,128)(2,1)} %get-tuple-element.34), calls=%async_computation.3 | async-start | bytes 1179648 | tf_op jit(solution)/shard_map/all_to_all | solution.py:179
  169.7 33.5 %copy-start.2 = (f32[1,384]{1,0:T(1,128)S(1)}, f32[1,384]{1,0:T(1,128)}, u32[]{:S(2)}) copy-start(f32[1,384]{1,0:T(1,128)} %get-tuple-element.31) | copy-start | bytes 4612
  169.7 33.5 %copy-start.4 = (f32[1,384]{1,0:T(1,128)S(1)}, f32[1,384]{1,0:T(1,128)}, u32[]{:S(2)}) copy-start(f32[1,384]{1,0:T(1,128)} %get-tuple-element.30) | copy-start | bytes 4612
  169.7 33.5 %copy-start.6 = (f32[1,384]{1,0:T(1,128)S(1)}, f32[1,384]{1,0:T(1,128)}, u32[]{:S(2)}) copy-start(f32[1,384]{1,0:T(1,128)} %get-tuple-element.32) | copy-start | bytes 4612
  169.7 34.0 %copy-start.1 = (f32[1,384]{1,0:T(1,128)S(1)}, f32[1,384]{1,0:T(1,128)}, u32[]{:S(2)}) copy-start(f32[1,384]{1,0:T(1,128)} %get-tuple-element.28) | copy-start | bytes 4612
  169.7 34.0 %copy-start.3 = (f32[1,384]{1,0:T(1,128)S(1)}, f32[1,384]{1,0:T(1,128)}, u32[]{:S(2)}) copy-start(f32[1,384]{1,0:T(1,128)} %get-tuple-element.27) | copy-start | bytes 4612
  169.7 34.0 %copy-start.5 = (f32[1,384]{1,0:T(1,128)S(1)}, f32[1,384]{1,0:T(1,128)}, u32[]{:S(2)}) copy-start(f32[1,384]{1,0:T(1,128)} %get-tuple-element.29) | copy-start | bytes 4612
  169.7 21.2 %collective-permute-start.2 = (bf16[12,64,384]{2,1,0:T(8,128)(2,1)S(1)}, bf16[12,64,384]{2,1,0:T(8,128)(2,1)}, u32[]{:S(2)}, u32[]{:S(2)}) collective-permute-start(bf16[12,64,384]{2,1,0:T(8,128)(2,1)S(1)} %get-tuple-element.33), channel_id=1, source_target_pairs={{12,0},{24,12},{36,24},{48,36},{60,48},{72,60},{84,72},{96,84},{10... | collective-permute-start | bytes 1769480 | tf_op jit(solution)/shard_map/ppermute | solution.py:16
  190.9 23.5 %all-to-all-start.2 = ((bf16[12,64,384]{2,1,0:T(8,128)(2,1)}), bf16[12,64,384]{2,1,0:T(8,128)(2,1)S(1)}, u32[]{:S(2)}, u32[]{:S(2)}) async-start(bf16[12,64,384]{2,1,0:T(8,128)(2,1)} %collective-permute-done.2), calls=%async_computation.2 | async-start | bytes 1179648 | tf_op jit(solution)/shard_map/all_to_all | solution.py:179
  201.2 16.4 %collective-permute-start.3 = (bf16[64,4608]{1,0:T(8,128)(2,1)S(1)}, bf16[64,4608]{1,0:T(8,128)(2,1)S(1)}, u32[]{:S(2)}, u32[]{:S(2)}) collective-permute-start(bf16[64,4608]{1,0:T(8,128)(2,1)S(1)} %bitcast.20), channel_id=1, source_target_pairs={{12,0},{24,12},{36,24},{48,36},{60,48},{72,60},{84,72},{96,84},{10... | collective-permute-start | bytes 1769480 | tf_op jit(solution)/shard_map/ppermute | solution.py:16
